TPU v7x, 256 devices: a whole 4x4x8 slice. The times are simulated.
256 devices in a mesh: coil: 8 (over z_hi, core), slab: 32 (over x, y, z_lo).
Axes of the slice: x: 4, y: 4, z: 8 (z_hi: 4, z_lo: 2; z = z_hi * 2 + z_lo), core: 2. Of those that a mesh axis runs over, the one named last changes fastest.
Arguments:
- image_field: float32 [2, 128, 192, 384], P(None, 'slab', 'coil'), may hold values from -6 to 6
- coil_maps: bfloat16 [2, 8, 128, 192, 384], P(None, 'coil', 'slab'), may hold values from -2 to 2
- kspace_data: bfloat16 [2, 8, 128, 192, 384], P(None, 'coil', None, 'slab'), may hold values from -6 to 6
- sampling_mask: int32 [128, 192], P(None, 'slab'), may hold values 0 or 1
- consistency_weight: float32 [1], replicated, may hold values from 0.5 to 2
- conv_first: bfloat16 [3, 3, 32, 3, 2], replicated, may hold values from -0.875 to 0.875
- conv_middle: bfloat16 [3, 3, 32, 3, 32], replicated, may hold values from -0.21875 to 0.21875
- conv_last: bfloat16 [3, 3, 2, 3, 32], replicated, may hold values from -0.21875 to 0.21875
Outputs:
- refined_image: float32 [2, 128, 192, 384], P(None, 'slab', 'coil')
All inputs are finite; a program needn't handle non-finite values. No bound on the sum of `sampling_mask` on one device may be relied on, other than what follows from the above.
Results may differ from a plain program's by a relative error of at most 0.02.
Values may be sent and summed in bfloat16 or wider, within the bound.
No kernel may reach another device: no remote copies, remote signals or barrier semaphores. Data moves between devices by JAX's collectives and lax.ppermute only.
A program may use at most 128 MiB of HBM per device.

v0:
```python
import math

import jax
import jax.numpy as jnp
from jax import lax
from jax.sharding import PartitionSpec as P


def padded_2(block, sides, width):
    for axis, dim in sides:
        count = lax.axis_size(axis)
        forward = [(i, i + 1) for i in range(count - 1)]
        backward = [(target, source) for source, target in forward]
        low = lax.ppermute(
            lax.slice_in_dim(block, block.shape[dim] - width, None, axis=dim), axis, forward
        )
        high = lax.ppermute(lax.slice_in_dim(block, 0, width, axis=dim), axis, backward)
        block = jnp.concatenate([low, block, high], axis=dim)
    return block


def fourier_tables(length):
    points = jnp.arange(length, dtype=jnp.int32)
    product = points[:, None] * points[None, :] % length
    angles = product.astype(jnp.float32) * (2.0 * math.pi / length)
    scaling = 1.0 / math.sqrt(length)
    return jnp.stack([jnp.cos(angles) * scaling, jnp.sin(angles) * scaling]).astype(jnp.bfloat16)


def fourier_section(values, along, inverse):
    length = values.shape[along]
    tables = fourier_tables(length)
    cosine = tables[0]
    sine = -tables[1] if inverse else tables[1]
    matrix = jnp.stack([jnp.stack([cosine, sine], axis=1), jnp.stack([-sine, cosine], axis=1)])
    result = lax.dot_general(
        matrix, values, (((2, 3), (0, along)), ((), ())), preferred_element_type=jnp.float32
    )
    result = jnp.moveaxis(result, 1, along)
    return result.astype(jnp.bfloat16)


def convolve(activations, weight):
    kernel = weight.transpose(2, 4, 0, 1, 3)
    return lax.conv_general_dilated(
        activations[None],
        kernel,
        (1, 1, 1),
        ((0, 0), (0, 0), (1, 1)),
        dimension_numbers=("NCDHW", "OIDHW", "NCDHW"),
        preferred_element_type=jnp.float32,
    )[0]


def inside_mask(depth_first, depth_count, row_first, row_count, depth_limit, row_limit):
    depth_places = depth_first + jnp.arange(depth_count, dtype=jnp.int32)
    row_places = row_first + jnp.arange(row_count, dtype=jnp.int32)
    depth_inside = (depth_places >= 0) & (depth_places < depth_limit)
    row_inside = (row_places >= 0) & (row_places < row_limit)
    return (depth_inside[:, None] & row_inside[None, :]).astype(jnp.float32)[None, :, :, None]


def per_device(
    image_field,
    coil_maps,
    kspace_data,
    sampling_mask,
    consistency_weight,
    conv_first,
    conv_middle,
    conv_last,
):
    slab_rows = image_field.shape[1]
    coil_rows = image_field.shape[2]
    phases = coil_maps.shape[3]
    partitions = kspace_data.shape[2]
    pixels = image_field.astype(jnp.bfloat16)
    sensitivity = coil_maps.astype(jnp.float32)
    values = lax.all_gather(pixels, "coil", axis=2, tiled=True).astype(jnp.float32)[:, None]
    expanded = jnp.stack(
        [
            sensitivity[0] * values[0] - sensitivity[1] * values[1],
            sensitivity[0] * values[1] + sensitivity[1] * values[0],
        ]
    ).astype(jnp.bfloat16)
    spectrum = fourier_section(expanded, 4, False)
    spectrum = fourier_section(spectrum, 3, False)
    spectrum = lax.all_to_all(spectrum, "slab", split_axis=3, concat_axis=2, tiled=True)
    spectrum = fourier_section(spectrum, 2, False)
    weights_mask = sampling_mask.astype(jnp.float32)[None, None, :, :, None]
    residual = (
        weights_mask * (spectrum.astype(jnp.float32) - kspace_data.astype(jnp.float32))
    ).astype(jnp.bfloat16)
    residual = fourier_section(residual, 2, True)
    residual = lax.all_to_all(residual, "slab", split_axis=2, concat_axis=3, tiled=True)
    residual = fourier_section(residual, 3, True)
    restored = fourier_section(residual, 4, True).astype(jnp.float32)
    sensitivity = coil_maps.astype(jnp.float32)
    partial_value = jnp.stack(
        [
            jnp.sum(sensitivity[0] * restored[0] + sensitivity[1] * restored[1], axis=0),
            jnp.sum(sensitivity[0] * restored[1] - sensitivity[1] * restored[0], axis=0),
        ]
    )
    step_size = consistency_weight[0]
    coil_first = lax.axis_index("coil") * coil_rows
    slab_first = lax.axis_index("slab") * slab_rows
    weights = (conv_first, conv_middle, conv_last)
    scattered = lax.psum_scatter(
        (-step_size * partial_value).astype(jnp.bfloat16), "coil", scatter_dimension=2, tiled=True
    )
    updated = image_field + scattered.astype(jnp.float32)
    activations = padded_2(updated.astype(jnp.bfloat16), (("coil", 2),), 3)
    for layer_index, weight in enumerate(weights):
        extended = padded_2(activations, (("slab", 1),), 1)
        output = convolve(extended, weight)
        if layer_index < 2:
            margin = 2 - layer_index
            inside = inside_mask(
                slab_first,
                output.shape[1],
                coil_first - margin,
                output.shape[2],
                partitions,
                phases,
            )
            activations = (jax.nn.relu(output) * inside).astype(jnp.bfloat16)
    return updated + output


def solution(mesh):
    placed = (
        P(None, "slab", "coil", None),
        P(None, "coil", "slab", None, None),
        P(None, "coil", None, "slab", None),
        P(None, "slab"),
        P(),
        P(),
        P(),
        P(),
    )
    return jax.shard_map(
        per_device,
        mesh=mesh,
        in_specs=placed,
        out_specs=P(None, "slab", "coil", None),
        check_vma=False,
    )
```

profile of v0, /device:TPU:121, one launch (start us, length us, event | category | flops | bytes accessed | tf_op | source)
XLA Modules:
  0.0 1173.3 jit_solution(3126058988162864414)
XLA Ops:
  6.5 1.7 copy.213
  8.2 1.4 convert_element_type.202
  10.5 0.8 fusion.88
  11.3 2.3 fusion.87
  13.6 2.6 fusion.70
  16.2 0.9 fusion.75
  17.1 1.3 fusion.60
  18.3 21.2 %all-gather.2.cloned.1.call-done = bf16[2,4,192,384]{3,2,0,1:T(8,128)(2,1)} async-done(((bf16[2,4,24,384]{3,2,0,1:T(8,128)(2,1)}), bf16[2,4,192,384]{3,2,0,1:T(8,128)(2,1)}) %all-gather.2.cloned.1.call-update) | async-done | bytes 1179664 | tf_op jit(solution)/shard_map/all_gather | solution.py:79
  39.5 1.4 convert_element_type.208
  42.2 1.1 fusion.34
  43.3 0.8 fusion.30
  44.1 1.9 copy.147
  46.1 8.2 all-to-all-start
  54.9 15.4 %all-to-all-done = bf16[2,1,4,192,384]{4,2,0,1,3:T(4,128)(2,1)} async-done(((bf16[2,1,4,192,384]{4,2,0,1,3:T(4,128)(2,1)}), bf16[2,1,4,192,384]{4,2,0,1,3:T(4,128)(2,1)}, u32[]{:S(2)}, u32[]{:S(2)}) %all-to-all-start) | async-done | bytes 1179680 | tf_op jit(solution)/shard_map/all_to_all | solution.py:88
  70.3 1.7 copy.148
  72.0 1.6 copy.149
  73.5 3.2 reshape.521
  76.7 2.1 fusion.36
  79.3 2.2 copy.152
  81.6 19.0 %all-to-all-start.1 = ((bf16[2,1,128,6,384]{4,0,3,1,2:T(2,128)(2,1)}), bf16[2,1,128,6,384]{4,0,3,1,2:T(2,128)(2,1)}, u32[]{:S(2)}, u32[]{:S(2)}) async-start(bf16[2,1,128,6,384]{4,0,3,1,2:T(2,128)(2,1)} %copy.152), calls=%async_computation.1 | async-start | bytes 2359296 | tf_op jit(solution)/shard_map/all_to_all | solution.py:95
  101.3 15.0 %all-to-all-done.1 = bf16[2,1,128,6,384]{4,0,3,1,2:T(2,128)(2,1)} async-done(((bf16[2,1,128,6,384]{4,0,3,1,2:T(2,128)(2,1)}), bf16[2,1,128,6,384]{4,0,3,1,2:T(2,128)(2,1)}, u32[]{:S(2)}, u32[]{:S(2)}) %all-to-all-start.1) | async-done | bytes 1179680 | tf_op jit(solution)/shard_map/all_to_all | solution.py:95
  116.3 1.8 copy.153
  119.1 1.1 convert_bitcast_fusion
  120.8 1.2 copy.214
  122.0 1.7 reshape.533
  123.8 39.6 %reduce-scatter.4.cloned.1.call-done = bf16[24,3072]{1,0:T(8,128)(2,1)} async-done(((bf16[192,3072]{1,0:T(8,128)(2,1)}), bf16[24,3072]{1,0:T(8,128)(2,1)}) %reduce-scatter.4.cloned.1.call-update) | async-done | bytes 147472
  163.4 1.0 reshape.534
  164.5 3.7 collective-permute-start
  168.2 1.9 collective-permute-start.1
  170.1 5.3 collective-permute-done.1
  175.5 2.6 collective-permute-start.2
  178.1 2.6 collective-permute-start.3
  180.8 5.1 collective-permute-done.3
  187.0 6.6 copy.163
  193.6 1.2 slice.148
  194.8 6.4 fusion.135
  201.2 37.1 %select_maximum_fusion = f32[4,28,8,49,32]{4,2,3,1,0:T(8,128)} fusion(pred[8,49]{0,1:T(8,128)(4,1)S(1)} %copy-done.15, bf16[3,3,32,3,2]{2,4,3,1,0:T(2,128)(2,1)S(1)} %copy-done.13, bf16[2,6,30,8,51]{3,0,4,2,1:T(2,128)(2,1)S(1)} %fusion.135), kind=kOutput, calls=%fused_computation.4 | convolution fusion | flops 154542080 | bytes 5917320 | tf_op jit(solution)/shard_map/conv_general_dilated | solution.py:45
  238.3 20.3 %copy.164 = f32[4,28,8,49,32]{3,2,4,1,0:T(8,128)} copy(f32[4,28,8,49,32]{4,2,3,1,0:T(8,128)} %select_maximum_fusion) | data formatting | bytes 11239424 | tf_op jit(solution)/shard_map/jit(relu)/max | solution.py:127
  258.6 13.2 %reshape.482 = f32[4,28,1,392,32]{3,4,1,0,2:T(8,128)} reshape(f32[4,28,8,49,32]{3,2,4,1,0:T(8,128)} %copy.164) | data formatting | bytes 11239424 | tf_op jit(solution)/shard_map/jit(relu)/max | solution.py:127
  271.8 3.0 fusion.18
  274.8 1.3 fusion.119
  276.0 1.9 collective-permute-start.4
  278.0 3.6 collective-permute-start.5
  281.6 14.1 %collective-permute-done.4 = bf16[32,1,28,384]{3,0,2,1:T(8,128)(2,1)} collective-permute-done((bf16[32,1,28,384]{3,0,2,1:T(8,128)(2,1)}, bf16[32,1,28,384]{3,0,2,1:T(8,128)(2,1)}, u32[]{:S(2)}, u32[]{:S(2)}) %collective-permute-start.4) | collective-permute-done | bytes 688160 | tf_op jit(solution)/shard_map/ppermute | solution.py:14
  295.7 12.2 %collective-permute-done.5 = bf16[32,1,28,384]{3,0,2,1:T(8,128)(2,1)} collective-permute-done((bf16[32,1,28,384]{3,0,2,1:T(8,128)(2,1)}, bf16[32,1,28,384]{3,0,2,1:T(8,128)(2,1)}, u32[]{:S(2)}, u32[]{:S(2)}) %collective-permute-start.5) | collective-permute-done | bytes 688160 | tf_op jit(solution)/shard_map/ppermute | solution.py:17
  307.9 1.7 maximum_bitcast_fusion
  309.6 5.2 pad.2
  314.8 16.9 %reshape.485 = bf16[32,6,28,1,8,49]{5,4,0,2,1,3:T(8,128)(2,1)} reshape(bf16[32,6,28,1,392]{4,0,2,1,3:T(8,128)(2,1)} %pad.2) | data formatting | bytes 8429568 | tf_op jit(solution)/shard_map/conv_general_dilated | solution.py:45
  331.8 22.9 %copy.166 = bf16[32,6,28,1,8,49]{0,4,5,2,1,3:T(8,128)(2,1)} copy(bf16[32,6,28,1,8,49]{5,4,0,2,1,3:T(8,128)(2,1)} %reshape.485) | data formatting | bytes 8429568 | tf_op jit(solution)/shard_map/conv_general_dilated | solution.py:45
  354.7 1.3 slice.152
  356.0 42.4 %select_maximum_fusion.1 = f32[4,26,8,49,32]{4,2,3,1,0:T(8,128)} fusion(pred[8,49]{0,1:T(8,128)(4,1)S(1)} %copy-done.15, bf16[3,3,32,3,32]{4,2,3,1,0:T(8,128)(2,1)S(1)} %copy-done, bf16[32,6,28,1,7,2]{0,4,5,2,1,3:T(8,128)(2,1)S(1)} %slice.152, bf16[32,6,28,1,8,49]{0,4,5,2,1,3:T(8,128)(2,1)} %copy.166), kind=kOutput, calls=%fused_computation.5 | convolution fusion | flops 2270076928 | bytes 9639304 | tf_op jit(solution)/shard_map/conv_general_dilated | solution.py:45
  398.4 18.5 %copy.167 = f32[4,26,8,49,32]{3,2,4,1,0:T(8,128)} copy(f32[4,26,8,49,32]{4,2,3,1,0:T(8,128)} %select_maximum_fusion.1) | data formatting | bytes 10436608 | tf_op jit(solution)/shard_map/jit(relu)/max | solution.py:127
  416.9 12.0 %reshape.489 = f32[4,26,1,392,32]{3,4,1,0,2:T(8,128)} reshape(f32[4,26,8,49,32]{3,2,4,1,0:T(8,128)} %copy.167) | data formatting | bytes 10436608 | tf_op jit(solution)/shard_map/jit(relu)/max | solution.py:127
  428.9 2.8 fusion.20
  431.9 1.9 collective-permute-start.6
  433.8 3.8 collective-permute-start.7
  437.6 12.4 %collective-permute-done.6 = bf16[32,1,26,384]{3,0,2,1:T(8,128)(2,1)S(1)} collective-permute-done((bf16[32,1,26,384]{3,0,2,1:T(8,128)(2,1)S(1)}, bf16[32,1,26,384]{3,0,2,1:T(8,128)(2,1)S(1)}, u32[]{:S(2)}, u32[]{:S(2)}) %collective-permute-start.6) | collective-permute-done | bytes 639008 | tf_op jit(solution)/shard_map/ppermute | solution.py:14
  449.9 14.8 %collective-permute-done.7 = bf16[32,1,26,384]{3,0,2,1:T(8,128)(2,1)S(1)} collective-permute-done((bf16[32,1,26,384]{3,0,2,1:T(8,128)(2,1)S(1)}, bf16[32,1,26,384]{3,0,2,1:T(8,128)(2,1)S(1)}, u32[]{:S(2)}, u32[]{:S(2)}) %collective-permute-start.7) | collective-permute-done | bytes 639008 | tf_op jit(solution)/shard_map/ppermute | solution.py:17
  465.3 4.9 pad.4
  470.2 15.9 %reshape.492 = bf16[32,6,26,1,8,49]{5,4,0,2,1,3:T(8,128)(2,1)} reshape(bf16[32,6,26,1,392]{4,0,2,1,3:T(8,128)(2,1)} %pad.4) | data formatting | bytes 7827456 | tf_op jit(solution)/shard_map/conv_general_dilated | solution.py:45
  486.1 21.0 %copy.169 = bf16[32,6,26,1,8,49]{0,4,5,2,1,3:T(8,128)(2,1)} copy(bf16[32,6,26,1,8,49]{5,4,0,2,1,3:T(8,128)(2,1)} %reshape.492) | data formatting | bytes 7827456 | tf_op jit(solution)/shard_map/conv_general_dilated | solution.py:45
  507.2 1.3 slice.156
  508.5 650.8 %broadcast_select_fusion = f32[4,24,8,49,2]{2,4,3,1,0:T(2,128)} fusion(pred[8,49]{0,1:T(8,128)(4,1)S(1)} %copy-done.15, bf16[3,3,2,3,32]{4,2,3,1,0:T(2,128)(2,1)S(1)} %copy-done.14, bf16[32,6,26,1,7,2]{0,4,5,2,1,3:T(8,128)(2,1)S(1)} %slice.156, bf16[32,6,26,1,8,49]{0,4,5,2,1,3:T(8,128)(2,1)} %copy.169), kind=kOutput, calls=%fused_computation.24 | convolution fusion | flops 142351872 | bytes 4358408 | tf_op jit(solution)/shard_map/conv_general_dilated | solution.py:45
  1159.3 5.8 copy.170
  (64 shorter events, 7.8 us)
Async XLA Ops:
  6.5 349.5 %copy-start = (bf16[3,3,32,3,32]{4,2,3,1,0:T(8,128)(2,1)S(1)}, bf16[3,3,32,3,32]{4,2,3,1,0:T(8,128)(2,1)}, u32[]{:S(2)}) copy-start(bf16[3,3,32,3,32]{4,2,3,1,0:T(8,128)(2,1)} %param.14) | copy-start | bytes 165892
  6.5 33.0 %all-gather.2.cloned.1.call-start = ((), (), s32[]{:S(2)}) async-start(), calls=%async_computation.3 | async-start | bytes 1327104 | tf_op jit(solution)/shard_map/all_gather | solution.py:79
  40.9 1.1 copy-start.7
  40.9 1.2 copy-start.8
  42.2 1.1 copy-start.11
  44.1 10.2 copy-start.12
  46.1 24.2 %all-to-all-start = ((bf16[2,1,4,192,384]{4,2,0,1,3:T(4,128)(2,1)}), bf16[2,1,4,192,384]{4,2,0,1,3:T(4,128)(2,1)}, u32[]{:S(2)}, u32[]{:S(2)}) async-start(bf16[2,1,4,192,384]{4,2,0,1,3:T(4,128)(2,1)} %copy.147), calls=%async_computation | async-start | bytes 2359296 | tf_op jit(solution)/shard_map/all_to_all | solution.py:88
  81.6 36.5 %copy-start.9 = (bf16[1,192,2,192]{3,1,2,0:T(8,128)(2,1)S(1)}, bf16[1,192,2,192]{3,1,2,0:T(8,128)(2,1)}, u32[]{:S(2)}) copy-start(bf16[1,192,2,192]{3,1,2,0:T(8,128)(2,1)} %get-tuple-element.21) | copy-start | bytes 442372
  81.6 34.7 %all-to-all-start.1 = ((bf16[2,1,128,6,384]{4,0,3,1,2:T(2,128)(2,1)}), bf16[2,1,128,6,384]{4,0,3,1,2:T(2,128)(2,1)}, u32[]{:S(2)}, u32[]{:S(2)}) async-start(bf16[2,1,128,6,384]{4,0,3,1,2:T(2,128)(2,1)} %copy.152), calls=%async_computation.1 | async-start | bytes 2359296 | tf_op jit(solution)/shard_map/all_to_all | solution.py:95
  100.6 62.8 %reduce-scatter.4.cloned.1.call-start = ((), (), s32[]{:S(2)}) async-start(), calls=%async_computation.4 | async-start | bytes 1327104
  116.3 1.8 copy-start.10
  118.1 1.1 copy-start.6
  122.0 42.4 %copy-start.2 = (f32[2,4,24,384]{3,2,1,0:T(8,128)S(1)}, f32[2,4,24,384]{3,2,1,0:T(8,128)}, u32[]{:S(2)}) copy-start(f32[2,4,24,384]{3,2,1,0:T(8,128)} %param.8) | copy-start | bytes 884740
  164.4 21.6 %copy-start.4 = (bf16[24,4,2,384]{3,2,1,0:T(2,128)(2,1)}, bf16[24,4,2,384]{3,2,1,0:T(2,128)(2,1)S(1)}, u32[]{:S(2)}) copy-start(bf16[24,4,2,384]{3,2,1,0:T(2,128)(2,1)S(1)} %reshape.534) | copy-start | bytes 442372
  164.5 5.6 collective-permute-start
  168.2 7.3 collective-permute-start.1
  175.5 5.4 collective-permute-start.2
  178.1 7.8 collective-permute-start.3
  194.8 6.4 copy-start.13
  194.8 6.4 copy-start.15
  276.0 19.7 %collective-permute-start.4 = (bf16[32,1,28,384]{3,0,2,1:T(8,128)(2,1)}, bf16[32,1,28,384]{3,0,2,1:T(8,128)(2,1)}, u32[]{:S(2)}, u32[]{:S(2)}) collective-permute-start(bf16[32,1,28,384]{3,0,2,1:T(8,128)(2,1)} %get-tuple-element.9), channel_id=1, source_target_pairs={{0,1},{1,2},{2,3},{3,4},{4,5},{5,6},{6,7},{7,8},{8,9},{9,10},{10,1... | collective-permute-start | bytes 2064392 | tf_op jit(solution)/shard_map/ppermute | solution.py:14
  278.0 29.9 %collective-permute-start.5 = (bf16[32,1,28,384]{3,0,2,1:T(8,128)(2,1)}, bf16[32,1,28,384]{3,0,2,1:T(8,128)(2,1)}, u32[]{:S(2)}, u32[]{:S(2)}) collective-permute-start(bf16[32,1,28,384]{3,0,2,1:T(8,128)(2,1)} %get-tuple-element.10), channel_id=1, source_target_pairs={{1,0},{2,1},{3,2},{4,3},{5,4},{6,5},{7,6},{8,7},{9,8},{10,9},{11,1... | collective-permute-start | bytes 2064392 | tf_op jit(solution)/shard_map/ppermute | solution.py:17
  431.9 18.1 %collective-permute-start.6 = (bf16[32,1,26,384]{3,0,2,1:T(8,128)(2,1)S(1)}, bf16[32,1,26,384]{3,0,2,1:T(8,128)(2,1)S(1)}, u32[]{:S(2)}, u32[]{:S(2)}) collective-permute-start(bf16[32,1,26,384]{3,0,2,1:T(8,128)(2,1)S(1)} %get-tuple-element.11), channel_id=1, source_target_pairs={{0,1},{1,2},{2,3},{3,4},{4,5},{5,6},{6,7},{7,8},{8,9},{9,10},{10,1... | collective-permute-start | bytes 1916936 | tf_op jit(solution)/shard_map/ppermute | solution.py:14
  433.8 31.0 %collective-permute-start.7 = (bf16[32,1,26,384]{3,0,2,1:T(8,128)(2,1)S(1)}, bf16[32,1,26,384]{3,0,2,1:T(8,128)(2,1)S(1)}, u32[]{:S(2)}, u32[]{:S(2)}) collective-permute-start(bf16[32,1,26,384]{3,0,2,1:T(8,128)(2,1)S(1)} %get-tuple-element.12), channel_id=1, source_target_pairs={{1,0},{2,1},{3,2},{4,3},{5,4},{6,5},{7,6},{8,7},{9,8},{10,9},{11,1... | collective-permute-start | bytes 1916936 | tf_op jit(solution)/shard_map/ppermute | solution.py:17
  486.1 22.3 %copy-start.14 = (bf16[3,3,2,3,32]{4,2,3,1,0:T(2,128)(2,1)S(1)}, bf16[3,3,2,3,32]{4,2,3,1,0:T(2,128)(2,1)}, u32[]{:S(2)}) copy-start(bf16[3,3,2,3,32]{4,2,3,1,0:T(2,128)(2,1)} %param.15) | copy-start | bytes 10372
  1159.3 6.1 copy-start.3
  1159.3 6.1 copy-start.5
  1159.3 6.9 copy-start.1
Sparse Core Ops, SparseCore 0:
  9.2 30.2 all-gather.1
  123.9 39.4 reduce-scatter.3
where the time goes:
time: 1190 us; the launch traced here: 1170 us
  matrix products  737 us (62%)
  local copies, waits for them, and re-layouts  189 us (16%)
  waiting for transfers between devices  155 us (13%)
  starting transfers between devices  49.3 us (4%)
  other arithmetic  27.9 us (2%)
  between operations  14.9 us (1%)
    conv_general_dilated x3, matrix products, convolve(): lax.conv_general_dilated(activations[None], kernel, (1, 1, 1), ((0, 0), (...  730 us
    conv_general_dilated x11, local copies, waits for them, and re-layouts, convolve(): lax.conv_general_dilated(activations[None], kernel, (1, 1, 1), ((0, 0), (...  94 us
    max x4, local copies, waits for them, and re-layouts, per_device(): activations = (jax.nn.relu(output) * inside).astype(jnp.bfloat16)  63.9 us
    unnamed x3, waiting for transfers between devices  39.6 us
    ppermute x4, waiting for transfers between devices, padded_2(): lax.ppermute(lax.slice_in_dim(block, 0, width, axis=dim), axis, backward)  37.4 us
    ppermute x4, waiting for transfers between devices, padded_2(): lax.ppermute(lax.slice_in_dim(block, block.shape[dim] - width, None, axis...  26.4 us
  transfers between devices with their start and end apart: 12, of which 10 were waited for; matrix products, arithmetic and copies ran while one was open for 1% of the time, Pallas kernels for 0%

commit v1 on v0

--- a/solution.py
+++ b/solution.py
@@ -3,6 +3,7 @@
 import jax
 import jax.numpy as jnp
 from jax import lax
+from jax.experimental import pallas as pl
 from jax.sharding import PartitionSpec as P
 
 
@@ -40,24 +41,72 @@
     return result.astype(jnp.bfloat16)
 
 
-def convolve(activations, weight):
-    kernel = weight.transpose(2, 4, 0, 1, 3)
-    return lax.conv_general_dilated(
-        activations[None],
-        kernel,
-        (1, 1, 1),
-        ((0, 0), (0, 0), (1, 1)),
-        dimension_numbers=("NCDHW", "OIDHW", "NCDHW"),
-        preferred_element_type=jnp.float32,
-    )[0]
+READ = 384
+CHUNK = 768
+
+def conv_flat(stack, kernel, out_rows):
+    depth_in, width, lanes_in = stack.shape
+    out_depth = depth_in - 2
+    out_channels = kernel.shape[2]
+    lanes = out_rows * READ
+    steps = lanes // CHUNK
+
+    def body(s0, s1, s2, w_ref, o_ref):
+        sources = (s0, s1, s2)
+
+        def chunk(index, carry):
+            start = pl.multiple_of(index * CHUNK, 128)
+            acc = jnp.zeros((out_channels, CHUNK), jnp.float32)
+            for dz in range(3):
+                for dy in range(3):
+                    acc = acc + jnp.dot(
+                        w_ref[dz, dy],
+                        sources[dz][0, :, pl.ds(start + dy * READ, CHUNK)],
+                        preferred_element_type=jnp.float32,
+                    )
+            o_ref[0, :, pl.ds(start, CHUNK)] = acc
+            return carry
+
+        lax.fori_loop(0, steps, chunk, 0)
+
+    in_specs = [
+        pl.BlockSpec((1, width, lanes_in), lambda z, dz=dz: (z + dz, 0, 0)) for dz in range(3)
+    ] + [pl.BlockSpec(kernel.shape, lambda z: (0, 0, 0, 0))]
+    return pl.pallas_call(
+        body,
+        grid=(out_depth,),
+        in_specs=in_specs,
+        out_specs=pl.BlockSpec((1, out_channels, lanes), lambda z: (z, 0, 0)),
+        out_shape=jax.ShapeDtypeStruct((out_depth, out_channels, lanes), jnp.float32),
+    )(stack, stack, stack, kernel)
 
 
-def inside_mask(depth_first, depth_count, row_first, row_count, depth_limit, row_limit):
-    depth_places = depth_first + jnp.arange(depth_count, dtype=jnp.int32)
-    row_places = row_first + jnp.arange(row_count, dtype=jnp.int32)
-    depth_inside = (depth_places >= 0) & (depth_places < depth_limit)
-    row_inside = (row_places >= 0) & (row_places < row_limit)
-    return (depth_inside[:, None] & row_inside[None, :]).astype(jnp.float32)[None, :, :, None]
+def shifted_stack(block):
+    channels = block.shape[1]
+    left = jnp.pad(block, ((0, 0), (0, 0), (1, 0)))[..., :-1]
+    right = jnp.pad(block, ((0, 0), (0, 0), (0, 1)))[..., 1:]
+    place = lax.broadcasted_iota(jnp.int32, block.shape, 2) % READ
+    zero = jnp.zeros((), block.dtype)
+    left = jnp.where(place == 0, zero, left)
+    right = jnp.where(place == READ - 1, zero, right)
+    pieces = [left, block, right]
+    extra = -(3 * channels) % 16
+    if extra:
+        pieces.append(jnp.zeros(block.shape[:1] + (extra,) + block.shape[2:], block.dtype))
+    return jnp.concatenate(pieces, axis=1)
+
+
+def kernel_matrix(weight):
+    out_channels, in_channels = weight.shape[2], weight.shape[4]
+    matrix = weight.reshape(3, 3, out_channels, 3 * in_channels)
+    extra_in = -(3 * in_channels) % 16
+    extra_out = -out_channels % 8
+    return jnp.pad(matrix, ((0, 0), (0, 0), (0, extra_out), (0, extra_in)))
+
+
+def convolve_flat(block, weight, out_rows):
+    out = conv_flat(shifted_stack(block), kernel_matrix(weight), out_rows)
+    return out[:, : weight.shape[2]]
 
 
 def per_device(
@@ -111,21 +160,23 @@
     )
     updated = image_field + scattered.astype(jnp.float32)
     activations = padded_2(updated.astype(jnp.bfloat16), (("coil", 2),), 3)
+    rows = activations.shape[2]
+    activations = activations.transpose(1, 0, 2, 3).reshape(slab_rows, 2, rows * READ)
     for layer_index, weight in enumerate(weights):
-        extended = padded_2(activations, (("slab", 1),), 1)
-        output = convolve(extended, weight)
+        extended = padded_2(activations, (("slab", 0),), 1)
+        rows = rows - 2
+        output = convolve_flat(extended, weight, rows)
         if layer_index < 2:
             margin = 2 - layer_index
-            inside = inside_mask(
-                slab_first,
-                output.shape[1],
-                coil_first - margin,
-                output.shape[2],
-                partitions,
-                phases,
+            depth_places = slab_first + jnp.arange(slab_rows, dtype=jnp.int32)
+            row_places = coil_first - margin + jnp.arange(rows * READ, dtype=jnp.int32) // READ
+            inside = (
+                ((depth_places >= 0) & (depth_places < partitions))[:, None, None]
+                & ((row_places >= 0) & (row_places < phases))[None, None, :]
             )
-            activations = (jax.nn.relu(output) * inside).astype(jnp.bfloat16)
-    return updated + output
+            activations = jnp.where(inside, jax.nn.relu(output), 0.0).astype(jnp.bfloat16)
+    correction = output.reshape(slab_rows, 2, coil_rows, READ).transpose(1, 0, 2, 3)
+    return updated + correction
 
 
 def solution(mesh):

time: 1190 us -> 341 us (0.29); the launches traced: 1170 us -> 338 us
  matrix products: 737 us -> 6.21 us
  local copies, waits for them, and re-layouts: 189 us -> 24.7 us
  Pallas kernels: 0 us -> 57.2 us
  other arithmetic: 27.9 us -> 48.7 us
  starting transfers between devices: 49.3 us -> 36.3 us
    conv_general_dilated x3 -> x0, matrix products: 730 us -> none  [convolve(): lax.conv_general_dilated(activations[None], kernel, (1, 1, 1), ((0, 0), (...]
    conv_general_dilated x11 -> x0, local copies, waits for them, and re-layouts: 94 us -> none  [convolve(): lax.conv_general_dilated(activations[None], kernel, (1, 1, 1), ((0, 0), (...]
    max x4 -> x0, local copies, waits for them, and re-layouts: 63.9 us -> none  [per_device(): activations = (jax.nn.relu(output) * inside).astype(jnp.bfloat16)]
    pallas_call x0 -> x3, Pallas kernels: none -> 57.2 us  [conv_flat(): pl.pallas_call(body, grid=(out_depth,), in_specs=in_specs, out_specs=pl.B...]
    concatenate x0 -> x5, other arithmetic: none -> 18.7 us  [the longest x3 15.7 us: shifted_stack(): return jnp.concatenate(pieces, axis=1)]
    all_to_all x1, starting transfers between devices: 19 us -> 6.69 us  [per_device(): lax.all_to_all(residual, 'slab', split_axis=2, concat_axis=3, tiled=True)]
  transfers between devices with their start and end apart: 12 -> 12, of which waited for: 10 -> 10; matrix products, arithmetic and copies ran while one was open for 1% -> 5% of each run, Pallas kernels for 0% -> 0%
where the time goes in v1:
time: 341 us; the launch traced here: 338 us
  waiting for transfers between devices  150 us (44%)
  Pallas kernels  57.2 us (17%)
  other arithmetic  48.7 us (14%)
  starting transfers between devices  36.3 us (11%)
  local copies, waits for them, and re-layouts  24.7 us (7%)
  between operations  14.7 us (4%)
  matrix products  6.21 us (2%)
    pallas_call x3, Pallas kernels, conv_flat(): pl.pallas_call(body, grid=(out_depth,), in_specs=in_specs, out_specs=pl.B...  57.2 us
    unnamed x3, waiting for transfers between devices  39.7 us
    ppermute x4, waiting for transfers between devices, padded_2(): lax.ppermute(lax.slice_in_dim(block, 0, width, axis=dim), axis, backward)  36.6 us
    ppermute x4, waiting for transfers between devices, padded_2(): lax.ppermute(lax.slice_in_dim(block, block.shape[dim] - width, None, axis...  23.5 us
    all_gather x1, waiting for transfers between devices, per_device(): lax.all_gather(pixels, 'coil', axis=2, tiled=True).astype(jnp.float32)  21.2 us
    concatenate x3, other arithmetic, shifted_stack(): return jnp.concatenate(pieces, axis=1)  15.7 us
    all_to_all x1, waiting for transfers between devices, per_device(): lax.all_to_all(spectrum, 'slab', split_axis=3, concat_axis=2, tiled=True)  14.7 us
    all_to_all x1, waiting for transfers between devices, per_device(): lax.all_to_all(residual, 'slab', split_axis=2, concat_axis=3, tiled=True)  14.2 us
  transfers between devices with their start and end apart: 12, of which 10 were waited for; matrix products, arithmetic and copies ran while one was open for 5% of the time, Pallas kernels for 0%

profile of v1, /device:TPU:121, one launch (start us, length us, event | category | flops | bytes accessed | tf_op | source)
XLA Modules:
  0.0 337.8 jit_solution(16906619326699482014)
XLA Ops:
  6.5 1.6 copy.130
  8.2 1.4 convert_element_type.204
  9.6 0.8 fusion.94
  10.4 0.8 fusion.64
  11.2 2.3 fusion.63
  13.6 2.6 fusion.47
  16.2 0.9 fusion.51
  17.1 1.3 fusion.37
  18.3 21.2 %all-gather.2.cloned.1.call-done = bf16[2,4,192,384]{3,2,0,1:T(8,128)(2,1)} async-done(((bf16[2,4,24,384]{3,2,0,1:T(8,128)(2,1)}), bf16[2,4,192,384]{3,2,0,1:T(8,128)(2,1)}) %all-gather.2.cloned.1.call-update) | async-done | bytes 1179664 | tf_op jit(solution)/shard_map/all_gather | solution.py:128
  39.5 1.4 convert_element_type.210
  41.4 1.1 fusion.11
  42.5 0.8 fusion.7
  43.4 2.0 copy.73
  45.3 8.1 %all-to-all-start = ((bf16[2,1,4,192,384]{4,2,0,1,3:T(4,128)(2,1)}), bf16[2,1,4,192,384]{4,2,0,1,3:T(4,128)(2,1)S(1)}, u32[]{:S(2)}, u32[]{:S(2)}) async-start(bf16[2,1,4,192,384]{4,2,0,1,3:T(4,128)(2,1)} %copy.73), calls=%async_computation | async-start | bytes 2359296 | tf_op jit(solution)/shard_map/all_to_all | solution.py:137
  54.1 0.7 fusion.68
  54.8 14.7 %all-to-all-done = bf16[2,1,4,192,384]{4,2,0,1,3:T(4,128)(2,1)S(1)} async-done(((bf16[2,1,4,192,384]{4,2,0,1,3:T(4,128)(2,1)}), bf16[2,1,4,192,384]{4,2,0,1,3:T(4,128)(2,1)S(1)}, u32[]{:S(2)}, u32[]{:S(2)}) %all-to-all-start) | async-done | bytes 1179680 | tf_op jit(solution)/shard_map/all_to_all | solution.py:137
  69.9 1.6 copy.75
  71.4 2.4 reshape.519
  73.8 1.9 fusion.13
  76.2 2.3 copy.78
  78.5 6.7 %all-to-all-start.1 = ((bf16[2,1,128,6,384]{4,0,3,1,2:T(2,128)(2,1)}), bf16[2,1,128,6,384]{4,0,3,1,2:T(2,128)(2,1)S(1)}, u32[]{:S(2)}, u32[]{:S(2)}) async-start(bf16[2,1,128,6,384]{4,0,3,1,2:T(2,128)(2,1)} %copy.78), calls=%async_computation.1 | async-start | bytes 2359296 | tf_op jit(solution)/shard_map/all_to_all | solution.py:144
  86.0 0.7 iota_remainder_fusion
  86.6 14.2 %all-to-all-done.1 = bf16[2,1,128,6,384]{4,0,3,1,2:T(2,128)(2,1)S(1)} async-done(((bf16[2,1,128,6,384]{4,0,3,1,2:T(2,128)(2,1)}), bf16[2,1,128,6,384]{4,0,3,1,2:T(2,128)(2,1)S(1)}, u32[]{:S(2)}, u32[]{:S(2)}) %all-to-all-start.1) | async-done | bytes 1179680 | tf_op jit(solution)/shard_map/all_to_all | solution.py:144
  101.9 0.8 fusion.8
  102.7 1.1 convert_bitcast_fusion
  104.4 1.2 copy.131
  105.6 1.7 reshape.531
  107.5 39.7 %reduce-scatter.4.cloned.1.call-done = bf16[24,3072]{1,0:T(8,128)(2,1)} async-done(((bf16[192,3072]{1,0:T(8,128)(2,1)}), bf16[24,3072]{1,0:T(8,128)(2,1)}) %reduce-scatter.4.cloned.1.call-update) | async-done | bytes 147472
  147.2 1.0 reshape.532
  148.3 3.5 %collective-permute-start = (bf16[2,4,3,384]{3,2,0,1:T(4,128)(2,1)S(1)}, bf16[2,4,3,384]{3,2,0,1:T(4,128)(2,1)S(1)}, u32[]{:S(2)}, u32[]{:S(2)}) collective-permute-start(bf16[2,4,3,384]{3,2,0,1:T(4,128)(2,1)S(1)} %get-tuple-element.31), channel_id=1, source_target_pairs={{0,32},{32,64},{64,96},{96,128},{128,160},{160,192},{192,224},{1,3... | collective-permute-start | bytes 55304 | tf_op jit(solution)/shard_map/ppermute | solution.py:15
  151.8 1.9 collective-permute-start.1
  153.8 5.3 %collective-permute-done.1 = bf16[2,4,3,384]{3,2,0,1:T(4,128)(2,1)S(1)} collective-permute-done((bf16[2,4,3,384]{3,2,0,1:T(4,128)(2,1)S(1)}, bf16[2,4,3,384]{3,2,0,1:T(4,128)(2,1)S(1)}, u32[]{:S(2)}, u32[]{:S(2)}) %collective-permute-start.1) | collective-permute-done | bytes 18464 | tf_op jit(solution)/shard_map/ppermute | solution.py:18
  159.2 2.7 collective-permute-start.2
  162.1 0.7 pad.34.w_ref
  162.9 2.6 collective-permute-start.3
  165.8 5.0 %collective-permute-done.3 = bf16[1,2,11520]{2,1,0:T(2,128)(2,1)S(1)} collective-permute-done((bf16[1,2,11520]{2,1,0:T(2,128)(2,1)S(1)}, bf16[1,2,11520]{2,1,0:T(2,128)(2,1)S(1)}, u32[]{:S(2)}, u32[]{:S(2)}) %collective-permute-start.3) | collective-permute-done | bytes 46112 | tf_op jit(solution)/shard_map/ppermute | solution.py:18
  170.8 0.9 compare_select_fusion.1
  171.7 2.8 maximum_maximum_fusion.s0.s1.s2
  174.5 16.8 %shard_map.82 = f32[4,32,10752]{2,1,0:T(8,128)} custom-call(bf16[6,16,11520]{2,1,0:T(8,128)(2,1)} %maximum_maximum_fusion.s0.s1.s2, bf16[6,16,11520]{2,1,0:T(8,128)(2,1)} %maximum_maximum_fusion.s0.s1.s2, bf16[6,16,11520]{2,1,0:T(8,128)(2,1)} %maximum_maximum_fusion.s0.s1.s2, bf16[3,3,32,16]{3,2,1,0:T(8,128)(2,1)} %pad.34.w_ref), custom_call_target="tpu_custom_call" | custom-call | tf_op jit(solution)/shard_map/pallas_call | solution.py:75
  191.3 3.1 select_convert_fusion
  194.5 1.2 fusion.104
  195.7 1.9 collective-permute-start.4
  197.6 3.6 %collective-permute-start.5 = (bf16[1,32,10752]{2,1,0:T(8,128)(2,1)}, bf16[1,32,10752]{2,1,0:T(8,128)(2,1)}, u32[]{:S(2)}, u32[]{:S(2)}) collective-permute-start(bf16[1,32,10752]{2,1,0:T(8,128)(2,1)} %get-tuple-element.14), channel_id=1, source_target_pairs={{1,0},{2,1},{3,2},{4,3},{5,4},{6,5},{7,6},{8,7},{9,8},{10,9},{11,1... | collective-permute-start | bytes 2064392 | tf_op jit(solution)/shard_map/ppermute | solution.py:18
  201.3 0.9 copy.88
  202.2 1.8 reshape.507.w_ref
  204.0 11.3 %collective-permute-done.4 = bf16[1,32,10752]{2,1,0:T(8,128)(2,1)S(1)} collective-permute-done((bf16[1,32,10752]{2,1,0:T(8,128)(2,1)}, bf16[1,32,10752]{2,1,0:T(8,128)(2,1)S(1)}, u32[]{:S(2)}, u32[]{:S(2)}) %collective-permute-start.4) | collective-permute-done | bytes 688160 | tf_op jit(solution)/shard_map/ppermute | solution.py:15
  215.3 11.5 %collective-permute-done.5 = bf16[1,32,10752]{2,1,0:T(8,128)(2,1)} collective-permute-done((bf16[1,32,10752]{2,1,0:T(8,128)(2,1)}, bf16[1,32,10752]{2,1,0:T(8,128)(2,1)}, u32[]{:S(2)}, u32[]{:S(2)}) %collective-permute-start.5) | collective-permute-done | bytes 688160 | tf_op jit(solution)/shard_map/ppermute | solution.py:18
  226.9 1.5 pad_maximum_fusion.2
  228.4 4.2 %fusion = (bf16[6,32,10752]{2,1,0:T(8,128)(2,1)S(1)}, bf16[6,32,10752]{2,1,0:T(8,128)(2,1)S(1)}) fusion(bf16[6,32,10752]{2,1,0:T(8,128)(2,1)S(1)} %pad_maximum_fusion.2, s32[10752]{0:T(1024)S(1)} %get-tuple-element.49, s32[10752]{0:T(1024)S(1)} %get-tuple-element.50, pred[10752]{0:T(1024)(128)(4,1)S(1)} %fusion.86), kind=kLoop, calls=%fused_computation.6 | loop fusion | flops 10321920 | bytes 12483072 | tf_op jit(solution)/shard_map/jit(_where)/select_n | solution.py:90
  232.6 6.5 %pad_maximum_fusion.s0.s1.s2 = bf16[6,96,10752]{2,1,0:T(8,128)(2,1)} fusion(bf16[6,32,10752]{2,1,0:T(8,128)(2,1)S(1)} %get-tuple-element.10, bf16[1,32,10752]{2,1,0:T(8,128)(2,1)} %collective-permute-done.5, bf16[4,32,10752]{2,1,0:T(8,128)(2,1)S(1)} %select_convert_fusion, bf16[1,32,10752]{2,1,0:T(8,128)(2,1)S(1)} %collective-permute-done.4, ...), kind=kLoop, calls=%fused_computation | loop fusion | flops 61931520 | bytes 24772608 | tf_op jit(solution)/shard_map/concatenate | solution.py:96
  239.1 21.5 %shard_map.83 = f32[4,32,9984]{2,1,0:T(8,128)} custom-call(bf16[6,96,10752]{2,1,0:T(8,128)(2,1)} %pad_maximum_fusion.s0.s1.s2, bf16[6,96,10752]{2,1,0:T(8,128)(2,1)} %pad_maximum_fusion.s0.s1.s2, bf16[6,96,10752]{2,1,0:T(8,128)(2,1)} %pad_maximum_fusion.s0.s1.s2, bf16[3,3,32,96]{3,2,1,0:T(8,128)(2,1)} %reshape.507.w_ref), custom_call_target="tpu_custom_call" | custom-call | tf_op jit(solution)/shard_map/pallas_call | solution.py:75
  260.7 3.0 select_convert_fusion.1
  263.6 1.2 fusion.105
  264.8 2.2 collective-permute-start.6
  267.0 3.1 collective-permute-start.7
  270.2 0.6 pad.39.w_ref
  270.9 12.1 %collective-permute-done.6 = bf16[1,32,9984]{2,1,0:T(8,128)(2,1)S(1)} collective-permute-done((bf16[1,32,9984]{2,1,0:T(8,128)(2,1)}, bf16[1,32,9984]{2,1,0:T(8,128)(2,1)S(1)}, u32[]{:S(2)}, u32[]{:S(2)}) %collective-permute-start.6) | collective-permute-done | bytes 639008 | tf_op jit(solution)/shard_map/ppermute | solution.py:15
  283.0 14.9 %collective-permute-done.7 = bf16[1,32,9984]{2,1,0:T(8,128)(2,1)} collective-permute-done((bf16[1,32,9984]{2,1,0:T(8,128)(2,1)}, bf16[1,32,9984]{2,1,0:T(8,128)(2,1)}, u32[]{:S(2)}, u32[]{:S(2)}) %collective-permute-start.7) | collective-permute-done | bytes 639008 | tf_op jit(solution)/shard_map/ppermute | solution.py:18
  297.9 1.5 pad_maximum_fusion.3
  299.4 3.9 %fusion.2 = (bf16[6,32,9984]{2,1,0:T(8,128)(2,1)S(1)}, bf16[6,32,9984]{2,1,0:T(8,128)(2,1)S(1)}) fusion(bf16[6,32,9984]{2,1,0:T(8,128)(2,1)S(1)} %pad_maximum_fusion.3, s32[9984]{0:T(1024)S(1)} %get-tuple-element.51, s32[9984]{0:T(1024)S(1)} %get-tuple-element.52, pred[9984]{0:T(1024)(128)(4,1)S(1)} %fusion.93), kind=kLoop, calls=%fused_computation.8 | loop fusion | flops 9584640 | bytes 11591424 | tf_op jit(solution)/shard_map/jit(_where)/select_n | solution.py:90
  303.3 6.4 %pad_maximum_fusion.1.s0.s1.s2 = bf16[6,96,9984]{2,1,0:T(8,128)(2,1)} fusion(bf16[6,32,9984]{2,1,0:T(8,128)(2,1)S(1)} %get-tuple-element.12, bf16[1,32,9984]{2,1,0:T(8,128)(2,1)} %collective-permute-done.7, bf16[4,32,9984]{2,1,0:T(8,128)(2,1)S(1)} %select_convert_fusion.1, bf16[1,32,9984]{2,1,0:T(8,128)(2,1)S(1)} %collective-permute-done.6, ...), kind=kLoop, calls=%fused_computation.3 | loop fusion | flops 57507840 | bytes 23003136 | tf_op jit(solution)/shard_map/concatenate | solution.py:96
  309.7 18.9 %shard_map.84 = f32[4,8,9216]{2,1,0:T(8,128)} custom-call(bf16[6,96,9984]{2,1,0:T(8,128)(2,1)} %pad_maximum_fusion.1.s0.s1.s2, bf16[6,96,9984]{2,1,0:T(8,128)(2,1)} %pad_maximum_fusion.1.s0.s1.s2, bf16[6,96,9984]{2,1,0:T(8,128)(2,1)} %pad_maximum_fusion.1.s0.s1.s2, bf16[3,3,8,96]{3,2,1,0:T(8,128)(2,1)} %pad.39.w_ref), custom_call_target="tpu_custom_call" | custom-call | tf_op jit(solution)/shard_map/pallas_call | solution.py:75
  328.6 1.3 slice.184
  330.2 0.7 copy.90
  (79 shorter events, 5.1 us)
Async XLA Ops:
  6.5 33.0 %all-gather.2.cloned.1.call-start = ((), (), s32[]{:S(2)}) async-start(), calls=%async_computation.3 | async-start | bytes 1327104 | tf_op jit(solution)/shard_map/all_gather | solution.py:128
  41.4 1.2 copy-start.13
  41.4 1.2 copy-start.14
  43.4 10.1 %copy-start.17 = (s32[128,6]{0,1:T(8,128)S(1)}, s32[128,6]{0,1:T(8,128)}, u32[]{:S(2)}) copy-start(s32[128,6]{0,1:T(8,128)} %param.11) | copy-start | bytes 9220
  45.3 24.1 %all-to-all-start = ((bf16[2,1,4,192,384]{4,2,0,1,3:T(4,128)(2,1)}), bf16[2,1,4,192,384]{4,2,0,1,3:T(4,128)(2,1)S(1)}, u32[]{:S(2)}, u32[]{:S(2)}) async-start(bf16[2,1,4,192,384]{4,2,0,1,3:T(4,128)(2,1)} %copy.73), calls=%async_computation | async-start | bytes 2359296 | tf_op jit(solution)/shard_map/all_to_all | solution.py:137
  73.8 1.9 copy-start.6
  73.8 1.9 copy-start.7
  78.5 22.4 %all-to-all-start.1 = ((bf16[2,1,128,6,384]{4,0,3,1,2:T(2,128)(2,1)}), bf16[2,1,128,6,384]{4,0,3,1,2:T(2,128)(2,1)S(1)}, u32[]{:S(2)}, u32[]{:S(2)}) async-start(bf16[2,1,128,6,384]{4,0,3,1,2:T(2,128)(2,1)} %copy.78), calls=%async_computation.1 | async-start | bytes 2359296 | tf_op jit(solution)/shard_map/all_to_all | solution.py:144
  85.2 62.0 %reduce-scatter.4.cloned.1.call-start = ((), (), s32[]{:S(2)}) async-start(), calls=%async_computation.4 | async-start | bytes 1327104
  100.9 0.9 copy-start.11
  100.9 1.0 copy-start.12
  101.3 1.4 copy-start.4
  101.3 1.4 copy-start.5
  105.6 42.6 %copy-start = (f32[2,4,24,384]{3,2,1,0:T(8,128)S(1)}, f32[2,4,24,384]{3,2,1,0:T(8,128)}, u32[]{:S(2)}) copy-start(f32[2,4,24,384]{3,2,1,0:T(8,128)} %param.8) | copy-start | bytes 884740
  105.6 56.3 %copy-start.15 = (bf16[3,3,32,3,2]{2,4,3,1,0:T(2,128)(2,1)S(1)}, bf16[3,3,32,3,2]{2,4,3,1,0:T(2,128)(2,1)}, u32[]{:S(2)}) copy-start(bf16[3,3,32,3,2]{2,4,3,1,0:T(2,128)(2,1)} %param.13) | copy-start | bytes 10372
  107.4 63.4 %copy-start.9 = (s32[11520]{0:T(1024)S(1)}, s32[11520]{0:T(1024)}, u32[]{:S(2)}) copy-start(s32[11520]{0:T(1024)} %get-tuple-element.47) | copy-start | bytes 138244
  107.4 63.5 %copy-start.10 = (s32[11520]{0:T(1024)S(1)}, s32[11520]{0:T(1024)}, u32[]{:S(2)}) copy-start(s32[11520]{0:T(1024)} %get-tuple-element.48) | copy-start | bytes 138244
  148.2 26.3 %copy-start.2 = (bf16[24,4,2,384]{3,2,1,0:T(2,128)(2,1)}, bf16[24,4,2,384]{3,2,1,0:T(2,128)(2,1)S(1)}, u32[]{:S(2)}) copy-start(bf16[24,4,2,384]{3,2,1,0:T(2,128)(2,1)S(1)} %reshape.532) | copy-start | bytes 442372
  148.3 5.5 %collective-permute-start = (bf16[2,4,3,384]{3,2,0,1:T(4,128)(2,1)S(1)}, bf16[2,4,3,384]{3,2,0,1:T(4,128)(2,1)S(1)}, u32[]{:S(2)}, u32[]{:S(2)}) collective-permute-start(bf16[2,4,3,384]{3,2,0,1:T(4,128)(2,1)S(1)} %get-tuple-element.31), channel_id=1, source_target_pairs={{0,32},{32,64},{64,96},{96,128},{128,160},{160,192},{192,224},{1,3... | collective-permute-start | bytes 55304 | tf_op jit(solution)/shard_map/ppermute | solution.py:15
  151.8 7.3 %collective-permute-start.1 = (bf16[2,4,3,384]{3,2,0,1:T(4,128)(2,1)S(1)}, bf16[2,4,3,384]{3,2,0,1:T(4,128)(2,1)S(1)}, u32[]{:S(2)}, u32[]{:S(2)}) collective-permute-start(bf16[2,4,3,384]{3,2,0,1:T(4,128)(2,1)S(1)} %get-tuple-element.32), channel_id=1, source_target_pairs={{32,0},{64,32},{96,64},{128,96},{160,128},{192,160},{224,192},{33,... | collective-permute-start | bytes 55304 | tf_op jit(solution)/shard_map/ppermute | solution.py:18
  159.2 6.4 %collective-permute-start.2 = (bf16[1,2,11520]{2,1,0:T(2,128)(2,1)S(1)}, bf16[1,2,11520]{2,1,0:T(2,128)(2,1)S(1)}, u32[]{:S(2)}, u32[]{:S(2)}) collective-permute-start(bf16[1,2,11520]{2,1,0:T(2,128)(2,1)S(1)} %slice.156), channel_id=1, source_target_pairs={{0,1},{1,2},{2,3},{3,4},{4,5},{5,6},{6,7},{7,8},{8,9},{9,10},{10,1... | collective-permute-start | bytes 138248 | tf_op jit(solution)/shard_map/ppermute | solution.py:15
  162.9 7.8 %collective-permute-start.3 = (bf16[1,2,11520]{2,1,0:T(2,128)(2,1)S(1)}, bf16[1,2,11520]{2,1,0:T(2,128)(2,1)S(1)}, u32[]{:S(2)}, u32[]{:S(2)}) collective-permute-start(bf16[1,2,11520]{2,1,0:T(2,128)(2,1)S(1)} %slice.158), channel_id=1, source_target_pairs={{1,0},{2,1},{3,2},{4,3},{5,4},{6,5},{7,6},{8,7},{9,8},{10,9},{11,1... | collective-permute-start | bytes 138248 | tf_op jit(solution)/shard_map/ppermute | solution.py:18
  194.4 6.9 %copy-start.8 = (bf16[3,3,32,3,32]{4,2,3,1,0:T(8,128)(2,1)S(1)}, bf16[3,3,32,3,32]{4,2,3,1,0:T(8,128)(2,1)}, u32[]{:S(2)}) copy-start(bf16[3,3,32,3,32]{4,2,3,1,0:T(8,128)(2,1)} %param.14) | copy-start | bytes 165892
  195.7 19.6 %collective-permute-start.4 = (bf16[1,32,10752]{2,1,0:T(8,128)(2,1)}, bf16[1,32,10752]{2,1,0:T(8,128)(2,1)S(1)}, u32[]{:S(2)}, u32[]{:S(2)}) collective-permute-start(bf16[1,32,10752]{2,1,0:T(8,128)(2,1)} %get-tuple-element.13), channel_id=1, source_target_pairs={{0,1},{1,2},{2,3},{3,4},{4,5},{5,6},{6,7},{7,8},{8,9},{9,10},{10,1... | collective-permute-start | bytes 2064392 | tf_op jit(solution)/shard_map/ppermute | solution.py:15
  197.6 29.3 %collective-permute-start.5 = (bf16[1,32,10752]{2,1,0:T(8,128)(2,1)}, bf16[1,32,10752]{2,1,0:T(8,128)(2,1)}, u32[]{:S(2)}, u32[]{:S(2)}) collective-permute-start(bf16[1,32,10752]{2,1,0:T(8,128)(2,1)} %get-tuple-element.14), channel_id=1, source_target_pairs={{1,0},{2,1},{3,2},{4,3},{5,4},{6,5},{7,6},{8,7},{9,8},{10,9},{11,1... | collective-permute-start | bytes 2064392 | tf_op jit(solution)/shard_map/ppermute | solution.py:18
  263.6 6.5 %copy-start.16 = (bf16[3,3,2,3,32]{4,2,3,1,0:T(2,128)(2,1)S(1)}, bf16[3,3,2,3,32]{4,2,3,1,0:T(2,128)(2,1)}, u32[]{:S(2)}) copy-start(bf16[3,3,2,3,32]{4,2,3,1,0:T(2,128)(2,1)} %param.15) | copy-start | bytes 10372
  264.8 18.2 %collective-permute-start.6 = (bf16[1,32,9984]{2,1,0:T(8,128)(2,1)}, bf16[1,32,9984]{2,1,0:T(8,128)(2,1)S(1)}, u32[]{:S(2)}, u32[]{:S(2)}) collective-permute-start(bf16[1,32,9984]{2,1,0:T(8,128)(2,1)} %get-tuple-element.15), channel_id=1, source_target_pairs={{0,1},{1,2},{2,3},{3,4},{4,5},{5,6},{6,7},{7,8},{8,9},{9,10},{10,1... | collective-permute-start | bytes 1916936 | tf_op jit(solution)/shard_map/ppermute | solution.py:15
  267.0 30.9 %collective-permute-start.7 = (bf16[1,32,9984]{2,1,0:T(8,128)(2,1)}, bf16[1,32,9984]{2,1,0:T(8,128)(2,1)}, u32[]{:S(2)}, u32[]{:S(2)}) collective-permute-start(bf16[1,32,9984]{2,1,0:T(8,128)(2,1)} %get-tuple-element.16), channel_id=1, source_target_pairs={{1,0},{2,1},{3,2},{4,3},{5,4},{6,5},{7,6},{8,7},{9,8},{10,9},{11,1... | collective-permute-start | bytes 1916936 | tf_op jit(solution)/shard_map/ppermute | solution.py:18
  309.7 20.5 %copy-start.1 = (f32[2,4,24,384]{3,2,1,0:T(8,128)S(1)}, f32[2,4,24,384]{3,2,1,0:T(8,128)}, u32[]{:S(2)}) copy-start(f32[2,4,24,384]{3,2,1,0:T(8,128)} %param.8) | copy-start | bytes 884740
  309.7 20.5 %copy-start.3 = (bf16[24,4,2,384]{3,2,1,0:T(2,128)(2,1)S(1)}, bf16[24,4,2,384]{3,2,1,0:T(2,128)(2,1)}, u32[]{:S(2)}) copy-start(bf16[24,4,2,384]{3,2,1,0:T(2,128)(2,1)} %copy-done.2) | copy-start | bytes 442372
Sparse Core Ops, SparseCore 0:
  9.2 30.2 all-gather.1
  107.5 39.6 reduce-scatter.3

commit v2 on v1

--- a/solution.py
+++ b/solution.py
@@ -160,15 +160,15 @@
     )
     updated = image_field + scattered.astype(jnp.float32)
     activations = padded_2(updated.astype(jnp.bfloat16), (("coil", 2),), 3)
-    rows = activations.shape[2]
-    activations = activations.transpose(1, 0, 2, 3).reshape(slab_rows, 2, rows * READ)
+    activations = padded_2(activations, (("slab", 1),), 3)
+    depth, rows = activations.shape[1], activations.shape[2]
+    activations = activations.transpose(1, 0, 2, 3).reshape(depth, 2, rows * READ)
     for layer_index, weight in enumerate(weights):
-        extended = padded_2(activations, (("slab", 0),), 1)
         rows = rows - 2
-        output = convolve_flat(extended, weight, rows)
+        output = convolve_flat(activations, weight, rows)
         if layer_index < 2:
             margin = 2 - layer_index
-            depth_places = slab_first + jnp.arange(slab_rows, dtype=jnp.int32)
+            depth_places = slab_first - margin + jnp.arange(output.shape[0], dtype=jnp.int32)
             row_places = coil_first - margin + jnp.arange(rows * READ, dtype=jnp.int32) // READ
             inside = (
                 ((depth_places >= 0) & (depth_places < partitions))[:, None, None]

time: 341 us -> 297 us (0.87)
  waiting for transfers between devices: 150 us -> 94.7 us
  Pallas kernels: 57.2 us -> 79.9 us
  starting transfers between devices: 36.3 us -> 25.4 us
  other arithmetic: 48.7 us -> 55.1 us
  local copies, waits for them, and re-layouts: 24.7 us -> 20.4 us
    ppermute x4 -> x2, waiting for transfers between devices: 36.6 us -> 8.27 us  [padded_2(): lax.ppermute(lax.slice_in_dim(block, 0, width, axis=dim), axis, backward)]
    pallas_call x3, Pallas kernels: 57.2 us -> 79.9 us  [conv_flat(): pl.pallas_call(body, grid=(out_depth,), in_specs=in_specs, out_specs=pl.B...]
    ppermute x4 -> x2, waiting for transfers between devices: 23.5 us -> 1.07 us  [padded_2(): lax.ppermute(lax.slice_in_dim(block, block.shape[dim] - width, None, axis...]
    ppermute x4 -> x2, starting transfers between devices: 11.2 us -> 4.26 us  [padded_2(): lax.ppermute(lax.slice_in_dim(block, 0, width, axis=dim), axis, backward)]
    ppermute x4 -> x2, starting transfers between devices: 10.2 us -> 6.25 us  [padded_2(): lax.ppermute(lax.slice_in_dim(block, block.shape[dim] - width, None, axis...]
    all_to_all x1, waiting for transfers between devices: 14.7 us -> 10.9 us  [per_device(): lax.all_to_all(spectrum, 'slab', split_axis=3, concat_axis=2, tiled=True)]
    unnamed x44 -> x50, local copies, waits for them, and re-layouts: 7.23 us -> 6.35 us
  transfers between devices with their start and end apart: 12 -> 8, of which waited for: 10 -> 7; matrix products, arithmetic and copies ran while one was open for 5% -> 7% of each run, Pallas kernels for 0% -> 0%
where the time goes in v2:
time: 297 us; the launch traced here: 296 us
  waiting for transfers between devices  94.7 us (32%)
  Pallas kernels  79.9 us (27%)
  other arithmetic  55.1 us (19%)
  starting transfers between devices  25.4 us (9%)
  local copies, waits for them, and re-layouts  20.4 us (7%)
  between operations  14.7 us (5%)
  matrix products  6.24 us (2%)
    pallas_call x3, Pallas kernels, conv_flat(): pl.pallas_call(body, grid=(out_depth,), in_specs=in_specs, out_specs=pl.B...  79.9 us
    unnamed x3, waiting for transfers between devices  39.8 us
    all_gather x1, waiting for transfers between devices, per_device(): lax.all_gather(pixels, 'coil', axis=2, tiled=True).astype(jnp.float32)  21.2 us
    concatenate x3, other arithmetic, shifted_stack(): return jnp.concatenate(pieces, axis=1)  15.1 us
    all_to_all x1, waiting for transfers between devices, per_device(): lax.all_to_all(residual, 'slab', split_axis=2, concat_axis=3, tiled=True)  13.5 us
    select_n x3, other arithmetic, shifted_stack(): left = jnp.where(place == 0, zero, left)  11.4 us
    all_to_all x1, waiting for transfers between devices, per_device(): lax.all_to_all(spectrum, 'slab', split_axis=3, concat_axis=2, tiled=True)  10.9 us
    convert_element_type x2, other arithmetic, per_device(): jnp.where(inside, jax.nn.relu(output), 0.0).astype(jnp.bfloat16)  9.29 us
  transfers between devices with their start and end apart: 8, of which 7 were waited for; matrix products, arithmetic and copies ran while one was open for 7% of the time, Pallas kernels for 0%

profile of v2, /device:TPU:121, one launch (start us, length us, event | category | flops | bytes accessed | tf_op | source)
XLA Modules:
  0.0 296.3 jit_solution(5259052668057623782)
XLA Ops:
  6.5 1.6 copy.130
  8.2 1.4 convert_element_type.204
  9.6 0.8 fusion.94
  10.4 0.8 fusion.64
  11.2 2.3 fusion.63
  13.6 2.6 fusion.47
  16.2 0.9 fusion.51
  17.1 1.3 fusion.37
  18.3 21.2 %all-gather.2.cloned.1.call-done = bf16[2,4,192,384]{3,2,0,1:T(8,128)(2,1)} async-done(((bf16[2,4,24,384]{3,2,0,1:T(8,128)(2,1)}), bf16[2,4,192,384]{3,2,0,1:T(8,128)(2,1)}) %all-gather.2.cloned.1.call-update) | async-done | bytes 1179664 | tf_op jit(solution)/shard_map/all_gather | solution.py:128
  39.5 1.4 convert_element_type.210
  40.9 0.4 fusion.21
  41.4 1.1 fusion.11
  42.5 0.8 fusion.7
  43.4 2.0 copy.73
  45.3 8.1 %all-to-all-start = ((bf16[2,1,4,192,384]{4,2,0,1,3:T(4,128)(2,1)}), bf16[2,1,4,192,384]{4,2,0,1,3:T(4,128)(2,1)S(1)}, u32[]{:S(2)}, u32[]{:S(2)}) async-start(bf16[2,1,4,192,384]{4,2,0,1,3:T(4,128)(2,1)} %copy.73), calls=%async_computation | async-start | bytes 2359296 | tf_op jit(solution)/shard_map/all_to_all | solution.py:137
  53.5 0.5 compare_and_fusion.2
  54.6 0.7 fusion.68
  55.3 0.6 compare_and_fusion
  56.0 0.6 compare_and_fusion.1
  56.6 0.6 iota_remainder_fusion
  57.2 0.6 iota_remainder_fusion.1
  57.9 0.7 iota_remainder_fusion.2
  58.5 10.9 %all-to-all-done = bf16[2,1,4,192,384]{4,2,0,1,3:T(4,128)(2,1)S(1)} async-done(((bf16[2,1,4,192,384]{4,2,0,1,3:T(4,128)(2,1)}), bf16[2,1,4,192,384]{4,2,0,1,3:T(4,128)(2,1)S(1)}, u32[]{:S(2)}, u32[]{:S(2)}) %all-to-all-start) | async-done | bytes 1179680 | tf_op jit(solution)/shard_map/all_to_all | solution.py:137
  69.4 0.4 copy.74
  69.8 1.6 copy.75
  71.4 2.4 reshape.524
  73.8 1.9 fusion.13
  75.7 0.5 fusion.10
  76.2 2.3 copy.78
  78.5 6.7 %all-to-all-start.1 = ((bf16[2,1,128,6,384]{4,0,3,1,2:T(2,128)(2,1)}), bf16[2,1,128,6,384]{4,0,3,1,2:T(2,128)(2,1)S(1)}, u32[]{:S(2)}, u32[]{:S(2)}) async-start(bf16[2,1,128,6,384]{4,0,3,1,2:T(2,128)(2,1)} %copy.78), calls=%async_computation.1 | async-start | bytes 2359296 | tf_op jit(solution)/shard_map/all_to_all | solution.py:144
  85.9 1.4 broadcast_and_fusion.1
  87.3 13.5 %all-to-all-done.1 = bf16[2,1,128,6,384]{4,0,3,1,2:T(2,128)(2,1)S(1)} async-done(((bf16[2,1,128,6,384]{4,0,3,1,2:T(2,128)(2,1)}), bf16[2,1,128,6,384]{4,0,3,1,2:T(2,128)(2,1)S(1)}, u32[]{:S(2)}, u32[]{:S(2)}) %all-to-all-start.1) | async-done | bytes 1179680 | tf_op jit(solution)/shard_map/all_to_all | solution.py:144
  100.8 0.5 copy.79
  101.3 0.4 copy-done.9
  101.8 0.8 fusion.8
  102.7 1.1 convert_bitcast_fusion
  103.8 0.3 fusion.24
  104.4 1.2 copy.131
  105.7 1.7 reshape.536
  107.6 39.8 %reduce-scatter.4.cloned.1.call-done = bf16[24,3072]{1,0:T(8,128)(2,1)} async-done(((bf16[192,3072]{1,0:T(8,128)(2,1)}), bf16[24,3072]{1,0:T(8,128)(2,1)}) %reduce-scatter.4.cloned.1.call-update) | async-done | bytes 147472
  147.3 1.0 reshape.537
  148.4 3.3 %collective-permute-start = (bf16[2,4,3,384]{3,2,0,1:T(4,128)(2,1)S(1)}, bf16[2,4,3,384]{3,2,0,1:T(4,128)(2,1)S(1)}, u32[]{:S(2)}, u32[]{:S(2)}) collective-permute-start(bf16[2,4,3,384]{3,2,0,1:T(4,128)(2,1)S(1)} %get-tuple-element.27), channel_id=1, source_target_pairs={{0,32},{32,64},{64,96},{96,128},{128,160},{160,192},{192,224},{1,3... | collective-permute-start | bytes 55304 | tf_op jit(solution)/shard_map/ppermute | solution.py:15
  151.7 1.9 collective-permute-start.1
  154.1 0.8 reshape.512.w_ref
  155.0 0.7 pad.34.w_ref
  155.6 0.6 pad.39.w_ref
  156.3 2.7 collective-permute-done.1
  159.1 2.9 collective-permute-start.2
  162.1 2.3 collective-permute-start.3
  164.4 1.1 collective-permute-done.2
  165.5 5.6 %collective-permute-done.3 = bf16[2,3,30,384]{3,2,0,1:T(8,128)(2,1)S(1)} collective-permute-done((bf16[2,3,30,384]{3,2,0,1:T(8,128)(2,1)S(1)}, bf16[2,3,30,384]{3,2,0,1:T(8,128)(2,1)S(1)}, u32[]{:S(2)}, u32[]{:S(2)}) %collective-permute-start.3) | collective-permute-done | bytes 138272 | tf_op jit(solution)/shard_map/ppermute | solution.py:18
  171.4 1.4 compare_select_fusion.1
  172.8 3.6 %maximum_maximum_fusion.s0.s1.s2 = bf16[10,16,11520]{2,1,0:T(8,128)(2,1)} fusion(bf16[10,2,11520]{2,1,0:T(2,128)(2,1)S(1)} %get-tuple-element.18, bf16[10,2,11520]{2,1,0:T(2,128)(2,1)S(1)} %reshape.510, bf16[10,2,11520]{2,1,0:T(2,128)(2,1)S(1)} %get-tuple-element.17, bf16[16]{0:T(256)(128)(2,1)S(1)} %pad.49.clone), kind=kLoop, calls=%fused_computation.16 | loop fusion | flops 14745600 | bytes 5068832 | tf_op jit(solution)/shard_map/concatenate | solution.py:96
  176.4 31.1 %shard_map.82 = f32[8,32,10752]{2,1,0:T(8,128)} custom-call(bf16[10,16,11520]{2,1,0:T(8,128)(2,1)} %maximum_maximum_fusion.s0.s1.s2, bf16[10,16,11520]{2,1,0:T(8,128)(2,1)} %maximum_maximum_fusion.s0.s1.s2, bf16[10,16,11520]{2,1,0:T(8,128)(2,1)} %maximum_maximum_fusion.s0.s1.s2, bf16[3,3,32,16]{3,2,1,0:T(8,128)(2,1)} %pad.34.w_ref), custom_call_target="tpu_custom_call" | custom-call | tf_op jit(solution)/shard_map/pallas_call | solution.py:75
  207.6 5.3 %select_convert_fusion = bf16[8,32,10752]{2,1,0:T(8,128)(2,1)S(1)} fusion(f32[8,32,10752]{2,1,0:T(8,128)} %shard_map.82, pred[8,10752]{1,0:T(8,128)(4,1)S(1)} %broadcast_and_fusion), kind=kLoop, calls=%fused_computation.6 | loop fusion | flops 8257536 | bytes 16601088 | tf_op jit(solution)/shard_map/convert_element_type | solution.py:177
  212.9 6.0 %fusion = (bf16[8,32,10752]{2,1,0:T(8,128)(2,1)S(1)}, bf16[8,32,10752]{2,1,0:T(8,128)(2,1)S(1)}) fusion(bf16[8,32,10752]{2,1,0:T(8,128)(2,1)S(1)} %select_convert_fusion, s32[10752]{0:T(1024)S(1)} %copy-done.13, s32[10752]{0:T(1024)S(1)} %copy-done.14, pred[10752]{0:T(1024)(128)(4,1)S(1)} %fusion.86), kind=kLoop, calls=%fused_computation.7 | loop fusion | flops 13762560 | bytes 16611840 | tf_op jit(solution)/shard_map/jit(_where)/select_n | solution.py:90
  219.0 6.6 %pad_maximum_fusion.s0.s1.s2 = bf16[8,96,10752]{2,1,0:T(8,128)(2,1)} fusion(bf16[8,32,10752]{2,1,0:T(8,128)(2,1)S(1)} %get-tuple-element.6, bf16[8,32,10752]{2,1,0:T(8,128)(2,1)S(1)} %select_convert_fusion, bf16[8,32,10752]{2,1,0:T(8,128)(2,1)S(1)} %get-tuple-element.5), kind=kLoop, calls=%fused_computation | loop fusion | flops 49545216 | bytes 33030144 | tf_op jit(solution)/shard_map/concatenate | solution.py:96
  225.5 29.9 %shard_map.83 = f32[6,32,9984]{2,1,0:T(8,128)} custom-call(bf16[8,96,10752]{2,1,0:T(8,128)(2,1)} %pad_maximum_fusion.s0.s1.s2, bf16[8,96,10752]{2,1,0:T(8,128)(2,1)} %pad_maximum_fusion.s0.s1.s2, bf16[8,96,10752]{2,1,0:T(8,128)(2,1)} %pad_maximum_fusion.s0.s1.s2, bf16[3,3,32,96]{3,2,1,0:T(8,128)(2,1)} %reshape.512.w_ref), custom_call_target="tpu_custom_call" | custom-call | tf_op jit(solution)/shard_map/pallas_call | solution.py:75
  255.5 4.0 %select_convert_fusion.1 = bf16[6,32,9984]{2,1,0:T(8,128)(2,1)S(1)} fusion(f32[6,32,9984]{2,1,0:T(8,128)} %shard_map.83, pred[6,9984]{1,0:T(8,128)(4,1)S(1)} %copy-done.3), kind=kLoop, calls=%fused_computation.9 | loop fusion | flops 5750784 | bytes 11561472 | tf_op jit(solution)/shard_map/convert_element_type | solution.py:177
  259.4 3.9 %fusion.2 = (bf16[6,32,9984]{2,1,0:T(8,128)(2,1)S(1)}, bf16[6,32,9984]{2,1,0:T(8,128)(2,1)S(1)}) fusion(bf16[6,32,9984]{2,1,0:T(8,128)(2,1)S(1)} %select_convert_fusion.1, s32[9984]{0:T(1024)S(1)} %copy-done.15, s32[9984]{0:T(1024)S(1)} %copy-done.16, pred[9984]{0:T(1024)(128)(4,1)S(1)} %fusion.93), kind=kLoop, calls=%fused_computation.10 | loop fusion | flops 9584640 | bytes 11591424 | tf_op jit(solution)/shard_map/jit(_where)/select_n | solution.py:90
  263.4 4.9 %pad_maximum_fusion.1.s0.s1.s2 = bf16[6,96,9984]{2,1,0:T(8,128)(2,1)} fusion(bf16[6,32,9984]{2,1,0:T(8,128)(2,1)S(1)} %get-tuple-element.12, bf16[6,32,9984]{2,1,0:T(8,128)(2,1)S(1)} %select_convert_fusion.1, bf16[6,32,9984]{2,1,0:T(8,128)(2,1)S(1)} %get-tuple-element.11), kind=kLoop, calls=%fused_computation.3 | loop fusion | flops 34504704 | bytes 23003136 | tf_op jit(solution)/shard_map/concatenate | solution.py:96
  268.2 18.9 %shard_map.84 = f32[4,8,9216]{2,1,0:T(8,128)} custom-call(bf16[6,96,9984]{2,1,0:T(8,128)(2,1)} %pad_maximum_fusion.1.s0.s1.s2, bf16[6,96,9984]{2,1,0:T(8,128)(2,1)} %pad_maximum_fusion.1.s0.s1.s2, bf16[6,96,9984]{2,1,0:T(8,128)(2,1)} %pad_maximum_fusion.1.s0.s1.s2, bf16[3,3,8,96]{3,2,1,0:T(8,128)(2,1)} %pad.39.w_ref), custom_call_target="tpu_custom_call" | custom-call | tf_op jit(solution)/shard_map/pallas_call | solution.py:75
  287.1 1.3 slice.156
  288.8 0.7 copy.90
  (72 shorter events, 2.4 us)
Async XLA Ops:
  6.5 33.0 %all-gather.2.cloned.1.call-start = ((), (), s32[]{:S(2)}) async-start(), calls=%async_computation.3 | async-start | bytes 1327104 | tf_op jit(solution)/shard_map/all_gather | solution.py:128
  41.4 1.2 copy-start.11
  41.4 1.2 copy-start.12
  43.4 10.1 %copy-start.20 = (s32[128,6]{0,1:T(8,128)S(1)}, s32[128,6]{0,1:T(8,128)}, u32[]{:S(2)}) copy-start(s32[128,6]{0,1:T(8,128)} %param.11) | copy-start | bytes 9220
  45.3 24.1 %all-to-all-start = ((bf16[2,1,4,192,384]{4,2,0,1,3:T(4,128)(2,1)}), bf16[2,1,4,192,384]{4,2,0,1,3:T(4,128)(2,1)S(1)}, u32[]{:S(2)}, u32[]{:S(2)}) async-start(bf16[2,1,4,192,384]{4,2,0,1,3:T(4,128)(2,1)} %copy.73), calls=%async_computation | async-start | bytes 2359296 | tf_op jit(solution)/shard_map/all_to_all | solution.py:137
  73.8 1.9 copy-start.4
  73.8 1.9 copy-start.5
  78.5 22.3 %all-to-all-start.1 = ((bf16[2,1,128,6,384]{4,0,3,1,2:T(2,128)(2,1)}), bf16[2,1,128,6,384]{4,0,3,1,2:T(2,128)(2,1)S(1)}, u32[]{:S(2)}, u32[]{:S(2)}) async-start(bf16[2,1,128,6,384]{4,0,3,1,2:T(2,128)(2,1)} %copy.78), calls=%async_computation.1 | async-start | bytes 2359296 | tf_op jit(solution)/shard_map/all_to_all | solution.py:144
  85.2 62.1 %reduce-scatter.4.cloned.1.call-start = ((), (), s32[]{:S(2)}) async-start(), calls=%async_computation.4 | async-start | bytes 1327104
  100.8 0.9 copy-start.9
  100.8 1.0 copy-start.10
  101.3 1.4 copy-start.1
  101.3 1.4 copy-start.2
  105.6 1.8 copy-start.17
  105.6 1.8 copy-start.21
  105.6 42.7 %copy-start = (f32[2,4,24,384]{3,2,1,0:T(8,128)S(1)}, f32[2,4,24,384]{3,2,1,0:T(8,128)}, u32[]{:S(2)}) copy-start(f32[2,4,24,384]{3,2,1,0:T(8,128)} %param.8) | copy-start | bytes 884740
  105.7 48.0 %copy-start.18 = (bf16[3,3,32,3,2]{2,4,3,1,0:T(2,128)(2,1)S(1)}, bf16[3,3,32,3,2]{2,4,3,1,0:T(2,128)(2,1)}, u32[]{:S(2)}) copy-start(bf16[3,3,32,3,2]{2,4,3,1,0:T(2,128)(2,1)} %param.13) | copy-start | bytes 10372
  105.7 48.2 %copy-start.6 = (bf16[3,3,32,3,32]{4,2,3,1,0:T(8,128)(2,1)S(1)}, bf16[3,3,32,3,32]{4,2,3,1,0:T(8,128)(2,1)}, u32[]{:S(2)}) copy-start(bf16[3,3,32,3,32]{4,2,3,1,0:T(8,128)(2,1)} %param.14) | copy-start | bytes 165892
  105.7 49.2 %copy-start.19 = (bf16[3,3,2,3,32]{4,2,3,1,0:T(2,128)(2,1)S(1)}, bf16[3,3,2,3,32]{4,2,3,1,0:T(2,128)(2,1)}, u32[]{:S(2)}) copy-start(bf16[3,3,2,3,32]{4,2,3,1,0:T(2,128)(2,1)} %param.15) | copy-start | bytes 10372
  148.3 23.0 %copy-start.7 = (s32[11520]{0:T(1024)S(1)}, s32[11520]{0:T(1024)}, u32[]{:S(2)}) copy-start(s32[11520]{0:T(1024)} %get-tuple-element.43) | copy-start | bytes 138244
  148.4 23.0 %copy-start.8 = (s32[11520]{0:T(1024)S(1)}, s32[11520]{0:T(1024)}, u32[]{:S(2)}) copy-start(s32[11520]{0:T(1024)} %get-tuple-element.44) | copy-start | bytes 138244
  148.4 7.9 %collective-permute-start = (bf16[2,4,3,384]{3,2,0,1:T(4,128)(2,1)S(1)}, bf16[2,4,3,384]{3,2,0,1:T(4,128)(2,1)S(1)}, u32[]{:S(2)}, u32[]{:S(2)}) collective-permute-start(bf16[2,4,3,384]{3,2,0,1:T(4,128)(2,1)S(1)} %get-tuple-element.27), channel_id=1, source_target_pairs={{0,32},{32,64},{64,96},{96,128},{128,160},{160,192},{192,224},{1,3... | collective-permute-start | bytes 55304 | tf_op jit(solution)/shard_map/ppermute | solution.py:15
  151.7 7.3 %collective-permute-start.1 = (bf16[2,4,3,384]{3,2,0,1:T(4,128)(2,1)S(1)}, bf16[2,4,3,384]{3,2,0,1:T(4,128)(2,1)S(1)}, u32[]{:S(2)}, u32[]{:S(2)}) collective-permute-start(bf16[2,4,3,384]{3,2,0,1:T(4,128)(2,1)S(1)} %get-tuple-element.28), channel_id=1, source_target_pairs={{32,0},{64,32},{96,64},{128,96},{160,128},{192,160},{224,192},{33,... | collective-permute-start | bytes 55304 | tf_op jit(solution)/shard_map/ppermute | solution.py:18
  159.1 6.4 %collective-permute-start.2 = (bf16[2,3,30,384]{3,2,0,1:T(8,128)(2,1)S(1)}, bf16[2,3,30,384]{3,2,0,1:T(8,128)(2,1)S(1)}, u32[]{:S(2)}, u32[]{:S(2)}) collective-permute-start(bf16[2,3,30,384]{3,2,0,1:T(8,128)(2,1)S(1)} %get-tuple-element.21), channel_id=1, source_target_pairs={{0,1},{1,2},{2,3},{3,4},{4,5},{5,6},{6,7},{7,8},{8,9},{9,10},{10,1... | collective-permute-start | bytes 414728 | tf_op jit(solution)/shard_map/ppermute | solution.py:15
  162.1 9.0 %collective-permute-start.3 = (bf16[2,3,30,384]{3,2,0,1:T(8,128)(2,1)S(1)}, bf16[2,3,30,384]{3,2,0,1:T(8,128)(2,1)S(1)}, u32[]{:S(2)}, u32[]{:S(2)}) collective-permute-start(bf16[2,3,30,384]{3,2,0,1:T(8,128)(2,1)S(1)} %get-tuple-element.22), channel_id=1, source_target_pairs={{1,0},{2,1},{3,2},{4,3},{5,4},{6,5},{7,6},{8,7},{9,8},{10,9},{11,1... | collective-permute-start | bytes 414728 | tf_op jit(solution)/shard_map/ppermute | solution.py:18
  207.6 5.3 %copy-start.13 = (s32[10752]{0:T(1024)S(1)}, s32[10752]{0:T(1024)}, u32[]{:S(2)}) copy-start(s32[10752]{0:T(1024)} %get-tuple-element.45) | copy-start | bytes 129028
  207.6 5.4 %copy-start.14 = (s32[10752]{0:T(1024)S(1)}, s32[10752]{0:T(1024)}, u32[]{:S(2)}) copy-start(s32[10752]{0:T(1024)} %get-tuple-element.46) | copy-start | bytes 129028
  225.5 29.9 %copy-start.3 = (pred[6,9984]{1,0:T(8,128)(4,1)S(1)}, pred[6,9984]{1,0:T(8,128)(4,1)}, u32[]{:S(2)}) copy-start(pred[6,9984]{1,0:T(8,128)(4,1)} %broadcast_and_fusion.1) | copy-start | bytes 179716
  255.4 4.0 %copy-start.15 = (s32[9984]{0:T(1024)S(1)}, s32[9984]{0:T(1024)}, u32[]{:S(2)}) copy-start(s32[9984]{0:T(1024)} %get-tuple-element.47) | copy-start | bytes 119812
  255.4 4.0 %copy-start.16 = (s32[9984]{0:T(1024)S(1)}, s32[9984]{0:T(1024)}, u32[]{:S(2)}) copy-start(s32[9984]{0:T(1024)} %get-tuple-element.48) | copy-start | bytes 119812
Sparse Core Ops, SparseCore 0:
  9.2 30.2 all-gather.1
  107.5 39.7 reduce-scatter.3

commit v3 on v2

--- a/solution.py
+++ b/solution.py
@@ -42,32 +42,28 @@
 
 
 READ = 384
-CHUNK = 768
+CHUNK = 1536
 
 def conv_flat(stack, kernel, out_rows):
     depth_in, width, lanes_in = stack.shape
     out_depth = depth_in - 2
     out_channels = kernel.shape[2]
     lanes = out_rows * READ
-    steps = lanes // CHUNK
+    starts = range(0, lanes, CHUNK)
 
     def body(s0, s1, s2, w_ref, o_ref):
         sources = (s0, s1, s2)
-
-        def chunk(index, carry):
-            start = pl.multiple_of(index * CHUNK, 128)
-            acc = jnp.zeros((out_channels, CHUNK), jnp.float32)
+        for start in starts:
+            size = min(CHUNK, lanes - start)
+            acc = jnp.zeros((out_channels, size), jnp.float32)
             for dz in range(3):
                 for dy in range(3):
                     acc = acc + jnp.dot(
                         w_ref[dz, dy],
-                        sources[dz][0, :, pl.ds(start + dy * READ, CHUNK)],
+                        sources[dz][0, :, pl.ds(start + dy * READ, size)],
                         preferred_element_type=jnp.float32,
                     )
-            o_ref[0, :, pl.ds(start, CHUNK)] = acc
-            return carry
-
-        lax.fori_loop(0, steps, chunk, 0)
+            o_ref[0, :, pl.ds(start, size)] = acc
 
     in_specs = [
         pl.BlockSpec((1, width, lanes_in), lambda z, dz=dz: (z + dz, 0, 0)) for dz in range(3)

time: 297 us -> 270 us (0.909)
  Pallas kernels: 79.9 us -> 52.6 us
    pallas_call x3, Pallas kernels: 79.9 us -> 52.6 us  [conv_flat(): pl.pallas_call(body, grid=(out_depth,), in_specs=in_specs, out_specs=pl.B...]
where the time goes in v3:
time: 270 us; the launch traced here: 269 us
  waiting for transfers between devices  94.7 us (35%)
  other arithmetic  55.3 us (20%)
  Pallas kernels  52.6 us (19%)
  starting transfers between devices  25.4 us (9%)
  local copies, waits for them, and re-layouts  20.4 us (8%)
  between operations  14.7 us (5%)
  matrix products  6.24 us (2%)
    pallas_call x3, Pallas kernels, conv_flat(): pl.pallas_call(body, grid=(out_depth,), in_specs=in_specs, out_specs=pl.B...  52.6 us
    unnamed x3, waiting for transfers between devices  39.8 us
    all_gather x1, waiting for transfers between devices, per_device(): lax.all_gather(pixels, 'coil', axis=2, tiled=True).astype(jnp.float32)  21.2 us
    concatenate x3, other arithmetic, shifted_stack(): return jnp.concatenate(pieces, axis=1)  15.3 us
    all_to_all x1, waiting for transfers between devices, per_device(): lax.all_to_all(residual, 'slab', split_axis=2, concat_axis=3, tiled=True)  13.5 us
    select_n x3, other arithmetic, shifted_stack(): left = jnp.where(place == 0, zero, left)  11.4 us
    all_to_all x1, waiting for transfers between devices, per_device(): lax.all_to_all(spectrum, 'slab', split_axis=3, concat_axis=2, tiled=True)  10.9 us
    convert_element_type x2, other arithmetic, per_device(): jnp.where(inside, jax.nn.relu(output), 0.0).astype(jnp.bfloat16)  9.29 us
  transfers between devices with their start and end apart: 8, of which 7 were waited for; matrix products, arithmetic and copies ran while one was open for 7% of the time, Pallas kernels for 0%

profile of v3, /device:TPU:121, one launch (start us, length us, event | category | flops | bytes accessed | tf_op | source)
XLA Modules:
  0.0 269.3 jit_solution(11490283249886171596)
XLA Ops:
  6.5 1.6 copy.130
  8.2 1.4 convert_element_type.204
  9.6 0.8 fusion.94
  10.4 0.8 fusion.64
  11.2 2.3 fusion.63
  13.6 2.6 fusion.47
  16.2 0.9 fusion.51
  17.1 1.3 fusion.37
  18.3 21.2 %all-gather.2.cloned.1.call-done = bf16[2,4,192,384]{3,2,0,1:T(8,128)(2,1)} async-done(((bf16[2,4,24,384]{3,2,0,1:T(8,128)(2,1)}), bf16[2,4,192,384]{3,2,0,1:T(8,128)(2,1)}) %all-gather.2.cloned.1.call-update) | async-done | bytes 1179664 | tf_op jit(solution)/shard_map/all_gather | solution.py:124
  39.5 1.4 convert_element_type.210
  40.9 0.4 fusion.21
  41.4 1.1 fusion.11
  42.5 0.8 fusion.7
  43.4 2.0 copy.73
  45.3 8.1 %all-to-all-start = ((bf16[2,1,4,192,384]{4,2,0,1,3:T(4,128)(2,1)}), bf16[2,1,4,192,384]{4,2,0,1,3:T(4,128)(2,1)S(1)}, u32[]{:S(2)}, u32[]{:S(2)}) async-start(bf16[2,1,4,192,384]{4,2,0,1,3:T(4,128)(2,1)} %copy.73), calls=%async_computation | async-start | bytes 2359296 | tf_op jit(solution)/shard_map/all_to_all | solution.py:133
  53.5 0.5 compare_and_fusion.2
  54.6 0.7 fusion.68
  55.3 0.6 compare_and_fusion
  56.0 0.6 compare_and_fusion.1
  56.6 0.6 iota_remainder_fusion
  57.2 0.6 iota_remainder_fusion.1
  57.9 0.7 iota_remainder_fusion.2
  58.5 10.9 %all-to-all-done = bf16[2,1,4,192,384]{4,2,0,1,3:T(4,128)(2,1)S(1)} async-done(((bf16[2,1,4,192,384]{4,2,0,1,3:T(4,128)(2,1)}), bf16[2,1,4,192,384]{4,2,0,1,3:T(4,128)(2,1)S(1)}, u32[]{:S(2)}, u32[]{:S(2)}) %all-to-all-start) | async-done | bytes 1179680 | tf_op jit(solution)/shard_map/all_to_all | solution.py:133
  69.4 0.4 copy.74
  69.8 1.6 copy.75
  71.4 2.4 reshape.524
  73.8 1.9 fusion.13
  75.7 0.5 fusion.10
  76.2 2.3 copy.78
  78.5 6.7 %all-to-all-start.1 = ((bf16[2,1,128,6,384]{4,0,3,1,2:T(2,128)(2,1)}), bf16[2,1,128,6,384]{4,0,3,1,2:T(2,128)(2,1)S(1)}, u32[]{:S(2)}, u32[]{:S(2)}) async-start(bf16[2,1,128,6,384]{4,0,3,1,2:T(2,128)(2,1)} %copy.78), calls=%async_computation.1 | async-start | bytes 2359296 | tf_op jit(solution)/shard_map/all_to_all | solution.py:140
  85.9 1.4 broadcast_and_fusion.1
  87.3 13.5 %all-to-all-done.1 = bf16[2,1,128,6,384]{4,0,3,1,2:T(2,128)(2,1)S(1)} async-done(((bf16[2,1,128,6,384]{4,0,3,1,2:T(2,128)(2,1)}), bf16[2,1,128,6,384]{4,0,3,1,2:T(2,128)(2,1)S(1)}, u32[]{:S(2)}, u32[]{:S(2)}) %all-to-all-start.1) | async-done | bytes 1179680 | tf_op jit(solution)/shard_map/all_to_all | solution.py:140
  100.8 0.5 copy.79
  101.3 0.4 copy-done.9
  101.8 0.8 fusion.8
  102.7 1.1 convert_bitcast_fusion
  103.8 0.3 fusion.24
  104.4 1.2 copy.131
  105.7 1.7 reshape.536
  107.6 39.8 %reduce-scatter.4.cloned.1.call-done = bf16[24,3072]{1,0:T(8,128)(2,1)} async-done(((bf16[192,3072]{1,0:T(8,128)(2,1)}), bf16[24,3072]{1,0:T(8,128)(2,1)}) %reduce-scatter.4.cloned.1.call-update) | async-done | bytes 147472
  147.3 1.0 reshape.537
  148.4 3.3 %collective-permute-start = (bf16[2,4,3,384]{3,2,0,1:T(4,128)(2,1)S(1)}, bf16[2,4,3,384]{3,2,0,1:T(4,128)(2,1)S(1)}, u32[]{:S(2)}, u32[]{:S(2)}) collective-permute-start(bf16[2,4,3,384]{3,2,0,1:T(4,128)(2,1)S(1)} %get-tuple-element.27), channel_id=1, source_target_pairs={{0,32},{32,64},{64,96},{96,128},{128,160},{160,192},{192,224},{1,3... | collective-permute-start | bytes 55304 | tf_op jit(solution)/shard_map/ppermute | solution.py:15
  151.7 1.9 collective-permute-start.1
  154.1 0.8 reshape.512.w_ref
  155.0 0.7 pad.34.w_ref
  155.6 0.6 pad.39.w_ref
  156.3 2.7 collective-permute-done.1
  159.1 2.9 %collective-permute-start.2 = (bf16[2,3,30,384]{3,2,0,1:T(8,128)(2,1)S(1)}, bf16[2,3,30,384]{3,2,0,1:T(8,128)(2,1)S(1)}, u32[]{:S(2)}, u32[]{:S(2)}) collective-permute-start(bf16[2,3,30,384]{3,2,0,1:T(8,128)(2,1)S(1)} %get-tuple-element.21), channel_id=1, source_target_pairs={{0,1},{1,2},{2,3},{3,4},{4,5},{5,6},{6,7},{7,8},{8,9},{9,10},{10,1... | collective-permute-start | bytes 414728 | tf_op jit(solution)/shard_map/ppermute | solution.py:15
  162.1 2.3 collective-permute-start.3
  164.4 1.1 collective-permute-done.2
  165.5 5.6 %collective-permute-done.3 = bf16[2,3,30,384]{3,2,0,1:T(8,128)(2,1)S(1)} collective-permute-done((bf16[2,3,30,384]{3,2,0,1:T(8,128)(2,1)S(1)}, bf16[2,3,30,384]{3,2,0,1:T(8,128)(2,1)S(1)}, u32[]{:S(2)}, u32[]{:S(2)}) %collective-permute-start.3) | collective-permute-done | bytes 138272 | tf_op jit(solution)/shard_map/ppermute | solution.py:18
  171.4 1.4 compare_select_fusion.1
  172.8 3.9 %maximum_maximum_fusion.s0.s1.s2 = bf16[10,16,11520]{2,1,0:T(8,128)(2,1)} fusion(bf16[10,2,11520]{2,1,0:T(2,128)(2,1)S(1)} %get-tuple-element.18, bf16[10,2,11520]{2,1,0:T(2,128)(2,1)S(1)} %reshape.510, bf16[10,2,11520]{2,1,0:T(2,128)(2,1)S(1)} %get-tuple-element.17, bf16[16]{0:T(256)(128)(2,1)S(1)} %pad.49.clone), kind=kLoop, calls=%fused_computation.16 | loop fusion | flops 14745600 | bytes 5068832 | tf_op jit(solution)/shard_map/concatenate | solution.py:92
  176.7 16.5 %shard_map.82 = f32[8,32,10752]{2,1,0:T(8,128)} custom-call(bf16[10,16,11520]{2,1,0:T(8,128)(2,1)} %maximum_maximum_fusion.s0.s1.s2, bf16[10,16,11520]{2,1,0:T(8,128)(2,1)} %maximum_maximum_fusion.s0.s1.s2, bf16[10,16,11520]{2,1,0:T(8,128)(2,1)} %maximum_maximum_fusion.s0.s1.s2, bf16[3,3,32,16]{3,2,1,0:T(8,128)(2,1)} %pad.34.w_ref), custom_call_target="tpu_custom_call" | custom-call | tf_op jit(solution)/shard_map/pallas_call | solution.py:71
  193.1 5.3 %select_convert_fusion = bf16[8,32,10752]{2,1,0:T(8,128)(2,1)S(1)} fusion(f32[8,32,10752]{2,1,0:T(8,128)} %shard_map.82, pred[8,10752]{1,0:T(8,128)(4,1)S(1)} %broadcast_and_fusion), kind=kLoop, calls=%fused_computation.6 | loop fusion | flops 8257536 | bytes 16601088 | tf_op jit(solution)/shard_map/convert_element_type | solution.py:173
  198.5 6.0 %fusion = (bf16[8,32,10752]{2,1,0:T(8,128)(2,1)S(1)}, bf16[8,32,10752]{2,1,0:T(8,128)(2,1)S(1)}) fusion(bf16[8,32,10752]{2,1,0:T(8,128)(2,1)S(1)} %select_convert_fusion, s32[10752]{0:T(1024)S(1)} %copy-done.13, s32[10752]{0:T(1024)S(1)} %copy-done.14, pred[10752]{0:T(1024)(128)(4,1)S(1)} %fusion.86), kind=kLoop, calls=%fused_computation.7 | loop fusion | flops 13762560 | bytes 16611840 | tf_op jit(solution)/shard_map/jit(_where)/select_n | solution.py:86
  204.6 6.6 %pad_maximum_fusion.s0.s1.s2 = bf16[8,96,10752]{2,1,0:T(8,128)(2,1)} fusion(bf16[8,32,10752]{2,1,0:T(8,128)(2,1)S(1)} %get-tuple-element.6, bf16[8,32,10752]{2,1,0:T(8,128)(2,1)S(1)} %select_convert_fusion, bf16[8,32,10752]{2,1,0:T(8,128)(2,1)S(1)} %get-tuple-element.5), kind=kLoop, calls=%fused_computation | loop fusion | flops 49545216 | bytes 33030144 | tf_op jit(solution)/shard_map/concatenate | solution.py:92
  211.1 21.8 %shard_map.83 = f32[6,32,9984]{2,1,0:T(8,128)} custom-call(bf16[8,96,10752]{2,1,0:T(8,128)(2,1)} %pad_maximum_fusion.s0.s1.s2, bf16[8,96,10752]{2,1,0:T(8,128)(2,1)} %pad_maximum_fusion.s0.s1.s2, bf16[8,96,10752]{2,1,0:T(8,128)(2,1)} %pad_maximum_fusion.s0.s1.s2, bf16[3,3,32,96]{3,2,1,0:T(8,128)(2,1)} %reshape.512.w_ref), custom_call_target="tpu_custom_call" | custom-call | tf_op jit(solution)/shard_map/pallas_call | solution.py:71
  233.0 4.0 %select_convert_fusion.1 = bf16[6,32,9984]{2,1,0:T(8,128)(2,1)S(1)} fusion(f32[6,32,9984]{2,1,0:T(8,128)} %shard_map.83, pred[6,9984]{1,0:T(8,128)(4,1)S(1)} %copy-done.3), kind=kLoop, calls=%fused_computation.9 | loop fusion | flops 5750784 | bytes 11561472 | tf_op jit(solution)/shard_map/convert_element_type | solution.py:173
  236.9 3.9 %fusion.2 = (bf16[6,32,9984]{2,1,0:T(8,128)(2,1)S(1)}, bf16[6,32,9984]{2,1,0:T(8,128)(2,1)S(1)}) fusion(bf16[6,32,9984]{2,1,0:T(8,128)(2,1)S(1)} %select_convert_fusion.1, s32[9984]{0:T(1024)S(1)} %copy-done.15, s32[9984]{0:T(1024)S(1)} %copy-done.16, pred[9984]{0:T(1024)(128)(4,1)S(1)} %fusion.93), kind=kLoop, calls=%fused_computation.10 | loop fusion | flops 9584640 | bytes 11591424 | tf_op jit(solution)/shard_map/jit(_where)/select_n | solution.py:86
  240.9 4.9 %pad_maximum_fusion.1.s0.s1.s2 = bf16[6,96,9984]{2,1,0:T(8,128)(2,1)} fusion(bf16[6,32,9984]{2,1,0:T(8,128)(2,1)S(1)} %get-tuple-element.12, bf16[6,32,9984]{2,1,0:T(8,128)(2,1)S(1)} %select_convert_fusion.1, bf16[6,32,9984]{2,1,0:T(8,128)(2,1)S(1)} %get-tuple-element.11), kind=kLoop, calls=%fused_computation.3 | loop fusion | flops 34504704 | bytes 23003136 | tf_op jit(solution)/shard_map/concatenate | solution.py:92
  245.7 14.3 %shard_map.84 = f32[4,8,9216]{2,1,0:T(8,128)} custom-call(bf16[6,96,9984]{2,1,0:T(8,128)(2,1)} %pad_maximum_fusion.1.s0.s1.s2, bf16[6,96,9984]{2,1,0:T(8,128)(2,1)} %pad_maximum_fusion.1.s0.s1.s2, bf16[6,96,9984]{2,1,0:T(8,128)(2,1)} %pad_maximum_fusion.1.s0.s1.s2, bf16[3,3,8,96]{3,2,1,0:T(8,128)(2,1)} %pad.39.w_ref), custom_call_target="tpu_custom_call" | custom-call | tf_op jit(solution)/shard_map/pallas_call | solution.py:71
  260.1 1.3 slice.156
  261.7 0.7 copy.90
  (72 shorter events, 2.4 us)
Async XLA Ops:
  6.5 33.0 %all-gather.2.cloned.1.call-start = ((), (), s32[]{:S(2)}) async-start(), calls=%async_computation.3 | async-start | bytes 1327104 | tf_op jit(solution)/shard_map/all_gather | solution.py:124
  41.4 1.2 copy-start.11
  41.4 1.2 copy-start.12
  43.4 10.1 %copy-start.20 = (s32[128,6]{0,1:T(8,128)S(1)}, s32[128,6]{0,1:T(8,128)}, u32[]{:S(2)}) copy-start(s32[128,6]{0,1:T(8,128)} %param.11) | copy-start | bytes 9220
  45.3 24.1 %all-to-all-start = ((bf16[2,1,4,192,384]{4,2,0,1,3:T(4,128)(2,1)}), bf16[2,1,4,192,384]{4,2,0,1,3:T(4,128)(2,1)S(1)}, u32[]{:S(2)}, u32[]{:S(2)}) async-start(bf16[2,1,4,192,384]{4,2,0,1,3:T(4,128)(2,1)} %copy.73), calls=%async_computation | async-start | bytes 2359296 | tf_op jit(solution)/shard_map/all_to_all | solution.py:133
  73.8 1.9 copy-start.4
  73.8 1.9 copy-start.5
  78.5 22.3 %all-to-all-start.1 = ((bf16[2,1,128,6,384]{4,0,3,1,2:T(2,128)(2,1)}), bf16[2,1,128,6,384]{4,0,3,1,2:T(2,128)(2,1)S(1)}, u32[]{:S(2)}, u32[]{:S(2)}) async-start(bf16[2,1,128,6,384]{4,0,3,1,2:T(2,128)(2,1)} %copy.78), calls=%async_computation.1 | async-start | bytes 2359296 | tf_op jit(solution)/shard_map/all_to_all | solution.py:140
  85.2 62.1 %reduce-scatter.4.cloned.1.call-start = ((), (), s32[]{:S(2)}) async-start(), calls=%async_computation.4 | async-start | bytes 1327104
  100.8 0.9 copy-start.9
  100.8 1.0 copy-start.10
  101.3 1.4 copy-start.1
  101.3 1.4 copy-start.2
  105.6 1.8 copy-start.17
  105.6 1.8 copy-start.21
  105.6 42.7 %copy-start = (f32[2,4,24,384]{3,2,1,0:T(8,128)S(1)}, f32[2,4,24,384]{3,2,1,0:T(8,128)}, u32[]{:S(2)}) copy-start(f32[2,4,24,384]{3,2,1,0:T(8,128)} %param.8) | copy-start | bytes 884740
  105.7 48.0 %copy-start.18 = (bf16[3,3,32,3,2]{2,4,3,1,0:T(2,128)(2,1)S(1)}, bf16[3,3,32,3,2]{2,4,3,1,0:T(2,128)(2,1)}, u32[]{:S(2)}) copy-start(bf16[3,3,32,3,2]{2,4,3,1,0:T(2,128)(2,1)} %param.13) | copy-start | bytes 10372
  105.7 48.2 %copy-start.6 = (bf16[3,3,32,3,32]{4,2,3,1,0:T(8,128)(2,1)S(1)}, bf16[3,3,32,3,32]{4,2,3,1,0:T(8,128)(2,1)}, u32[]{:S(2)}) copy-start(bf16[3,3,32,3,32]{4,2,3,1,0:T(8,128)(2,1)} %param.14) | copy-start | bytes 165892
  105.7 49.2 %copy-start.19 = (bf16[3,3,2,3,32]{4,2,3,1,0:T(2,128)(2,1)S(1)}, bf16[3,3,2,3,32]{4,2,3,1,0:T(2,128)(2,1)}, u32[]{:S(2)}) copy-start(bf16[3,3,2,3,32]{4,2,3,1,0:T(2,128)(2,1)} %param.15) | copy-start | bytes 10372
  148.3 23.0 %copy-start.7 = (s32[11520]{0:T(1024)S(1)}, s32[11520]{0:T(1024)}, u32[]{:S(2)}) copy-start(s32[11520]{0:T(1024)} %get-tuple-element.43) | copy-start | bytes 138244
  148.4 23.0 %copy-start.8 = (s32[11520]{0:T(1024)S(1)}, s32[11520]{0:T(1024)}, u32[]{:S(2)}) copy-start(s32[11520]{0:T(1024)} %get-tuple-element.44) | copy-start | bytes 138244
  148.4 7.9 %collective-permute-start = (bf16[2,4,3,384]{3,2,0,1:T(4,128)(2,1)S(1)}, bf16[2,4,3,384]{3,2,0,1:T(4,128)(2,1)S(1)}, u32[]{:S(2)}, u32[]{:S(2)}) collective-permute-start(bf16[2,4,3,384]{3,2,0,1:T(4,128)(2,1)S(1)} %get-tuple-element.27), channel_id=1, source_target_pairs={{0,32},{32,64},{64,96},{96,128},{128,160},{160,192},{192,224},{1,3... | collective-permute-start | bytes 55304 | tf_op jit(solution)/shard_map/ppermute | solution.py:15
  151.7 7.3 %collective-permute-start.1 = (bf16[2,4,3,384]{3,2,0,1:T(4,128)(2,1)S(1)}, bf16[2,4,3,384]{3,2,0,1:T(4,128)(2,1)S(1)}, u32[]{:S(2)}, u32[]{:S(2)}) collective-permute-start(bf16[2,4,3,384]{3,2,0,1:T(4,128)(2,1)S(1)} %get-tuple-element.28), channel_id=1, source_target_pairs={{32,0},{64,32},{96,64},{128,96},{160,128},{192,160},{224,192},{33,... | collective-permute-start | bytes 55304 | tf_op jit(solution)/shard_map/ppermute | solution.py:18
  159.1 6.4 %collective-permute-start.2 = (bf16[2,3,30,384]{3,2,0,1:T(8,128)(2,1)S(1)}, bf16[2,3,30,384]{3,2,0,1:T(8,128)(2,1)S(1)}, u32[]{:S(2)}, u32[]{:S(2)}) collective-permute-start(bf16[2,3,30,384]{3,2,0,1:T(8,128)(2,1)S(1)} %get-tuple-element.21), channel_id=1, source_target_pairs={{0,1},{1,2},{2,3},{3,4},{4,5},{5,6},{6,7},{7,8},{8,9},{9,10},{10,1... | collective-permute-start | bytes 414728 | tf_op jit(solution)/shard_map/ppermute | solution.py:15
  162.1 9.0 %collective-permute-start.3 = (bf16[2,3,30,384]{3,2,0,1:T(8,128)(2,1)S(1)}, bf16[2,3,30,384]{3,2,0,1:T(8,128)(2,1)S(1)}, u32[]{:S(2)}, u32[]{:S(2)}) collective-permute-start(bf16[2,3,30,384]{3,2,0,1:T(8,128)(2,1)S(1)} %get-tuple-element.22), channel_id=1, source_target_pairs={{1,0},{2,1},{3,2},{4,3},{5,4},{6,5},{7,6},{8,7},{9,8},{10,9},{11,1... | collective-permute-start | bytes 414728 | tf_op jit(solution)/shard_map/ppermute | solution.py:18
  193.1 5.3 %copy-start.13 = (s32[10752]{0:T(1024)S(1)}, s32[10752]{0:T(1024)}, u32[]{:S(2)}) copy-start(s32[10752]{0:T(1024)} %get-tuple-element.45) | copy-start | bytes 129028
  193.1 5.4 %copy-start.14 = (s32[10752]{0:T(1024)S(1)}, s32[10752]{0:T(1024)}, u32[]{:S(2)}) copy-start(s32[10752]{0:T(1024)} %get-tuple-element.46) | copy-start | bytes 129028
  211.1 21.8 %copy-start.3 = (pred[6,9984]{1,0:T(8,128)(4,1)S(1)}, pred[6,9984]{1,0:T(8,128)(4,1)}, u32[]{:S(2)}) copy-start(pred[6,9984]{1,0:T(8,128)(4,1)} %broadcast_and_fusion.1) | copy-start | bytes 179716
  233.0 4.0 %copy-start.15 = (s32[9984]{0:T(1024)S(1)}, s32[9984]{0:T(1024)}, u32[]{:S(2)}) copy-start(s32[9984]{0:T(1024)} %get-tuple-element.47) | copy-start | bytes 119812
  233.0 4.0 %copy-start.16 = (s32[9984]{0:T(1024)S(1)}, s32[9984]{0:T(1024)}, u32[]{:S(2)}) copy-start(s32[9984]{0:T(1024)} %get-tuple-element.48) | copy-start | bytes 119812
Sparse Core Ops, SparseCore 0:
  9.2 30.2 all-gather.1
  107.5 39.7 reduce-scatter.3

commit v4 on v3

--- a/solution.py
+++ b/solution.py
@@ -4,6 +4,7 @@
 import jax.numpy as jnp
 from jax import lax
 from jax.experimental import pallas as pl
+from jax.experimental.pallas import tpu as pltpu
 from jax.sharding import PartitionSpec as P
 
 
@@ -102,6 +103,68 @@
 
 def convolve_flat(block, weight, out_rows):
     out = conv_flat(shifted_stack(block), kernel_matrix(weight), out_rows)
+    return out[:, : weight.shape[2]]
+
+
+def conv_roll(block, kernel, out_rows):
+    depth_in, width, lanes_in = block.shape
+    out_depth = depth_in - 2
+    out_channels = kernel.shape[2] // 3
+    lanes = out_rows * READ
+    starts = range(0, lanes, CHUNK)
+
+    def body(s0, s1, s2, w_ref, o_ref):
+        sources = (s0, s1, s2)
+        for start in starts:
+            size = min(CHUNK, lanes - start)
+            acc = jnp.zeros((3 * out_channels, size), jnp.float32)
+            for dz in range(3):
+                for dy in range(3):
+                    acc = acc + jnp.dot(
+                        w_ref[dz, dy],
+                        sources[dz][0, :, pl.ds(start + dy * READ, size)],
+                        preferred_element_type=jnp.float32,
+                    )
+            place = lax.broadcasted_iota(jnp.int32, (out_channels, size), 1) % READ
+            left = pltpu.roll(acc[:out_channels], 1, 1)
+            right = pltpu.roll(acc[2 * out_channels :], size - 1, 1)
+            o_ref[0, :, pl.ds(start, size)] = (
+                acc[out_channels : 2 * out_channels]
+                + jnp.where(place == 0, 0.0, left)
+                + jnp.where(place == READ - 1, 0.0, right)
+            )
+
+    in_specs = [
+        pl.BlockSpec((1, width, lanes_in), lambda z, dz=dz: (z + dz, 0, 0)) for dz in range(3)
+    ] + [pl.BlockSpec(kernel.shape, lambda z: (0, 0, 0, 0))]
+    return pl.pallas_call(
+        body,
+        grid=(out_depth,),
+        in_specs=in_specs,
+        out_specs=pl.BlockSpec((1, out_channels, lanes), lambda z: (z, 0, 0)),
+        out_shape=jax.ShapeDtypeStruct((out_depth, out_channels, lanes), jnp.float32),
+    )(block, block, block, kernel)
+
+
+def tap_matrix(weight):
+    out_channels, in_channels = weight.shape[2], weight.shape[4]
+    extra_out = -out_channels % 8
+    extra_in = -in_channels % 16
+    matrix = jnp.pad(
+        weight.transpose(0, 1, 3, 2, 4), ((0, 0), (0, 0), (0, 0), (0, extra_out), (0, extra_in))
+    )
+    return matrix.reshape(3, 3, 3 * (out_channels + extra_out), in_channels + extra_in)
+
+
+def padded_channels(block):
+    extra = -block.shape[1] % 16
+    if extra:
+        block = jnp.pad(block, ((0, 0), (0, extra), (0, 0)))
+    return block
+
+
+def convolve_roll(block, weight, out_rows):
+    out = conv_roll(padded_channels(block), tap_matrix(weight), out_rows)
     return out[:, : weight.shape[2]]
 
 
@@ -161,7 +224,10 @@
     activations = activations.transpose(1, 0, 2, 3).reshape(depth, 2, rows * READ)
     for layer_index, weight in enumerate(weights):
         rows = rows - 2
-        output = convolve_flat(activations, weight, rows)
+        if layer_index == 0:
+            output = convolve_flat(activations, weight, rows)
+        else:
+            output = convolve_roll(activations, weight, rows)
         if layer_index < 2:
             margin = 2 - layer_index
             depth_places = slab_first - margin + jnp.arange(output.shape[0], dtype=jnp.int32)

time: 270 us -> 257 us (0.952)
  other arithmetic: 55.3 us -> 35.5 us
  Pallas kernels: 52.6 us -> 56.6 us
    pallas_call x0 -> x2, Pallas kernels: none -> 40.1 us  [conv_roll(): pl.pallas_call(body, grid=(out_depth,), in_specs=in_specs, out_specs=pl.B...]
    pallas_call x3 -> x1, Pallas kernels: 52.6 us -> 16.5 us  [conv_flat(): pl.pallas_call(body, grid=(out_depth,), in_specs=in_specs, out_specs=pl.B...]
    concatenate x3 -> x1, other arithmetic: 15.3 us -> 3.65 us  [shifted_stack(): return jnp.concatenate(pieces, axis=1)]
    select_n x3 -> x1, other arithmetic: 11.4 us -> 1.4 us  [shifted_stack(): left = jnp.where(place == 0, zero, left)]
    convert_element_type x2, other arithmetic: 9.29 us -> 13.6 us  [per_device(): jnp.where(inside, jax.nn.relu(output), 0.0).astype(jnp.bfloat16)]
    unnamed x50 -> x32, local copies, waits for them, and re-layouts: 6.35 us -> 7.24 us
  transfers between devices with their start and end apart: 8 -> 8, of which waited for: 7 -> 7; matrix products, arithmetic and copies ran while one was open for 7% -> 6% of each run, Pallas kernels for 0% -> 0%
where the time goes in v4:
time: 257 us; the launch traced here: 256 us
  waiting for transfers between devices  97.1 us (38%)
  Pallas kernels  56.6 us (22%)
  other arithmetic  35.5 us (14%)
  starting transfers between devices  25.8 us (10%)
  local copies, waits for them, and re-layouts  20.3 us (8%)
  between operations  14.5 us (6%)
  matrix products  6.22 us (2%)
    pallas_call x2, Pallas kernels, conv_roll(): pl.pallas_call(body, grid=(out_depth,), in_specs=in_specs, out_specs=pl.B...  40.1 us
    unnamed x3, waiting for transfers between devices  39.1 us
    all_gather x1, waiting for transfers between devices, per_device(): lax.all_gather(pixels, 'coil', axis=2, tiled=True).astype(jnp.float32)  21.2 us
    pallas_call x1, Pallas kernels, conv_flat(): pl.pallas_call(body, grid=(out_depth,), in_specs=in_specs, out_specs=pl.B...  16.5 us
    convert_element_type x2, other arithmetic, per_device(): jnp.where(inside, jax.nn.relu(output), 0.0).astype(jnp.bfloat16)  13.6 us
    all_to_all x1, waiting for transfers between devices, per_device(): lax.all_to_all(residual, 'slab', split_axis=2, concat_axis=3, tiled=True)  13.5 us
    all_to_all x1, waiting for transfers between devices, per_device(): lax.all_to_all(spectrum, 'slab', split_axis=3, concat_axis=2, tiled=True)  13.4 us
    ppermute x2, waiting for transfers between devices, padded_2(): lax.ppermute(lax.slice_in_dim(block, 0, width, axis=dim), axis, backward)  9.13 us
  transfers between devices with their start and end apart: 8, of which 7 were waited for; matrix products, arithmetic and copies ran while one was open for 6% of the time, Pallas kernels for 0%

profile of v4, /device:TPU:121, one launch (start us, length us, event | category | flops | bytes accessed | tf_op | source)
XLA Modules:
  0.0 256.0 jit_solution(4624154295388685753)
XLA Ops:
  6.5 1.6 copy.122
  8.2 1.4 convert_element_type.196
  9.6 0.8 fusion.84
  10.4 0.8 fusion.60
  11.2 2.3 fusion.59
  13.6 2.6 %fusion.43 = (bf16[384,1,384]{2,0,1:T(8,128)(2,1)S(1)}, bf16[384,1,384]{2,0,1:T(8,128)(2,1)S(1)}) fusion(), kind=kLoop, calls=%fused_computation.86 | loop fusion | flops 1916928 | bytes 589824 | tf_op jit(solution)/shard_map/stack;squeeze | solution.py:37
  16.2 0.9 fusion.47
  17.1 1.2 fusion.33
  18.3 21.2 %all-gather.2.cloned.1.call-done = bf16[2,4,192,384]{3,2,0,1:T(8,128)(2,1)} async-done(((bf16[2,4,24,384]{3,2,0,1:T(8,128)(2,1)}), bf16[2,4,192,384]{3,2,0,1:T(8,128)(2,1)}) %all-gather.2.cloned.1.call-update) | async-done | bytes 1179664 | tf_op jit(solution)/shard_map/all_gather | solution.py:187
  39.5 1.4 convert_element_type.202
  40.9 0.4 fusion.17
  41.4 1.1 fusion.7
  42.5 0.8 fusion.3
  43.4 2.0 copy.67
  45.3 8.3 %all-to-all-start = ((bf16[2,1,4,192,384]{4,2,0,1,3:T(4,128)(2,1)}), bf16[2,1,4,192,384]{4,2,0,1,3:T(4,128)(2,1)S(1)}, u32[]{:S(2)}, u32[]{:S(2)}) async-start(bf16[2,1,4,192,384]{4,2,0,1,3:T(4,128)(2,1)} %copy.67), calls=%async_computation | async-start | bytes 2359296 | tf_op jit(solution)/shard_map/all_to_all | solution.py:196
  53.6 0.6 compare_and_fusion.2
  54.2 0.3 fusion.87
  54.5 0.3 fusion.85
  54.8 0.7 fusion.64
  55.5 0.6 compare_and_fusion.1
  56.1 13.4 %all-to-all-done = bf16[2,1,4,192,384]{4,2,0,1,3:T(4,128)(2,1)S(1)} async-done(((bf16[2,1,4,192,384]{4,2,0,1,3:T(4,128)(2,1)}), bf16[2,1,4,192,384]{4,2,0,1,3:T(4,128)(2,1)S(1)}, u32[]{:S(2)}, u32[]{:S(2)}) %all-to-all-start) | async-done | bytes 1179680 | tf_op jit(solution)/shard_map/all_to_all | solution.py:196
  69.5 0.4 copy.68
  69.9 1.6 copy.69
  71.5 2.4 reshape.524
  73.9 1.9 fusion.9
  75.8 0.5 fusion.6
  76.3 2.3 copy.72
  78.6 6.6 %all-to-all-start.1 = ((bf16[2,1,128,6,384]{4,0,3,1,2:T(2,128)(2,1)}), bf16[2,1,128,6,384]{4,0,3,1,2:T(2,128)(2,1)S(1)}, u32[]{:S(2)}, u32[]{:S(2)}) async-start(bf16[2,1,128,6,384]{4,0,3,1,2:T(2,128)(2,1)} %copy.72), calls=%async_computation.1 | async-start | bytes 2359296 | tf_op jit(solution)/shard_map/all_to_all | solution.py:203
  85.9 1.4 broadcast_and_fusion.1
  87.3 13.5 %all-to-all-done.1 = bf16[2,1,128,6,384]{4,0,3,1,2:T(2,128)(2,1)S(1)} async-done(((bf16[2,1,128,6,384]{4,0,3,1,2:T(2,128)(2,1)}), bf16[2,1,128,6,384]{4,0,3,1,2:T(2,128)(2,1)S(1)}, u32[]{:S(2)}, u32[]{:S(2)}) %all-to-all-start.1) | async-done | bytes 1179680 | tf_op jit(solution)/shard_map/all_to_all | solution.py:203
  100.8 0.5 copy.73
  101.3 0.5 copy-done.6
  101.9 0.8 fusion.4
  102.7 0.2 copy-done.1
  102.9 0.2 copy-done.2
  103.1 1.1 convert_bitcast_fusion
  104.2 0.3 fusion.20
  104.5 0.2 fusion
  104.8 1.2 copy.123
  106.0 1.7 reshape.536
  107.8 0.6 copy-done.13
  108.5 39.0 %reduce-scatter.4.cloned.1.call-done = bf16[24,3072]{1,0:T(8,128)(2,1)} async-done(((bf16[192,3072]{1,0:T(8,128)(2,1)}), bf16[24,3072]{1,0:T(8,128)(2,1)}) %reduce-scatter.4.cloned.1.call-update) | async-done | bytes 147472
  147.6 1.0 reshape.537
  148.7 3.7 %collective-permute-start = (bf16[2,4,3,384]{3,2,0,1:T(4,128)(2,1)S(1)}, bf16[2,4,3,384]{3,2,0,1:T(4,128)(2,1)S(1)}, u32[]{:S(2)}, u32[]{:S(2)}) collective-permute-start(bf16[2,4,3,384]{3,2,0,1:T(4,128)(2,1)S(1)} %get-tuple-element.23), channel_id=1, source_target_pairs={{0,32},{32,64},{64,96},{96,128},{128,160},{160,192},{192,224},{1,3... | collective-permute-start | bytes 55304 | tf_op jit(solution)/shard_map/ppermute | solution.py:16
  152.3 1.9 collective-permute-start.1
  154.3 5.3 %collective-permute-done.1 = bf16[2,4,3,384]{3,2,0,1:T(4,128)(2,1)S(1)} collective-permute-done((bf16[2,4,3,384]{3,2,0,1:T(4,128)(2,1)S(1)}, bf16[2,4,3,384]{3,2,0,1:T(4,128)(2,1)S(1)}, u32[]{:S(2)}, u32[]{:S(2)}) %collective-permute-start.1) | collective-permute-done | bytes 18464 | tf_op jit(solution)/shard_map/ppermute | solution.py:19
  159.7 2.6 %collective-permute-start.2 = (bf16[2,3,30,384]{3,2,0,1:T(8,128)(2,1)S(1)}, bf16[2,3,30,384]{3,2,0,1:T(8,128)(2,1)S(1)}, u32[]{:S(2)}, u32[]{:S(2)}) collective-permute-start(bf16[2,3,30,384]{3,2,0,1:T(8,128)(2,1)S(1)} %get-tuple-element.17), channel_id=1, source_target_pairs={{0,1},{1,2},{2,3},{3,4},{4,5},{5,6},{6,7},{7,8},{8,9},{9,10},{10,1... | collective-permute-start | bytes 414728 | tf_op jit(solution)/shard_map/ppermute | solution.py:16
  162.3 2.6 %collective-permute-start.3 = (bf16[2,3,30,384]{3,2,0,1:T(8,128)(2,1)S(1)}, bf16[2,3,30,384]{3,2,0,1:T(8,128)(2,1)S(1)}, u32[]{:S(2)}, u32[]{:S(2)}) collective-permute-start(bf16[2,3,30,384]{3,2,0,1:T(8,128)(2,1)S(1)} %get-tuple-element.18), channel_id=1, source_target_pairs={{1,0},{2,1},{3,2},{4,3},{5,4},{6,5},{7,6},{8,7},{9,8},{10,9},{11,1... | collective-permute-start | bytes 414728 | tf_op jit(solution)/shard_map/ppermute | solution.py:19
  165.1 0.1 copy.81
  165.2 0.7 pad.18.w_ref
  166.0 0.6 pad_bitcast_fusion.w_ref
  166.6 0.8 collective-permute-done.2
  167.4 3.8 %collective-permute-done.3 = bf16[2,3,30,384]{3,2,0,1:T(8,128)(2,1)S(1)} collective-permute-done((bf16[2,3,30,384]{3,2,0,1:T(8,128)(2,1)S(1)}, bf16[2,3,30,384]{3,2,0,1:T(8,128)(2,1)S(1)}, u32[]{:S(2)}, u32[]{:S(2)}) %collective-permute-start.3) | collective-permute-done | bytes 138272 | tf_op jit(solution)/shard_map/ppermute | solution.py:19
  171.3 0.2 reshape.510
  171.5 1.4 compare_select_fusion.1
  172.9 3.6 %maximum_maximum_fusion.s0.s1.s2 = bf16[10,16,11520]{2,1,0:T(8,128)(2,1)} fusion(bf16[10,2,11520]{2,1,0:T(2,128)(2,1)S(1)} %get-tuple-element.14, bf16[10,2,11520]{2,1,0:T(2,128)(2,1)S(1)} %reshape.510, bf16[10,2,11520]{2,1,0:T(2,128)(2,1)S(1)} %get-tuple-element.13, bf16[16]{0:T(256)(128)(2,1)S(1)} %pad.23.clone), kind=kLoop, calls=%fused_computation.2 | loop fusion | flops 14745600 | bytes 5068832 | tf_op jit(solution)/shard_map/concatenate | solution.py:93
  176.6 16.5 %shard_map.82 = f32[8,32,10752]{2,1,0:T(8,128)} custom-call(bf16[10,16,11520]{2,1,0:T(8,128)(2,1)} %maximum_maximum_fusion.s0.s1.s2, bf16[10,16,11520]{2,1,0:T(8,128)(2,1)} %maximum_maximum_fusion.s0.s1.s2, bf16[10,16,11520]{2,1,0:T(8,128)(2,1)} %maximum_maximum_fusion.s0.s1.s2, bf16[3,3,32,16]{3,2,1,0:T(8,128)(2,1)} %pad.18.w_ref), custom_call_target="tpu_custom_call" | custom-call | tf_op jit(solution)/shard_map/pallas_call | solution.py:72
  193.0 7.7 %select_convert_fusion.s0.s1.s2 = bf16[8,32,10752]{2,1,0:T(8,128)(2,1)} fusion(f32[8,32,10752]{2,1,0:T(8,128)} %shard_map.82, pred[8,10752]{1,0:T(8,128)(4,1)S(1)} %broadcast_and_fusion), kind=kLoop, calls=%fused_computation | loop fusion | flops 8257536 | bytes 16601088 | tf_op jit(solution)/shard_map/convert_element_type | solution.py:239
  200.7 31.2 %shard_map.83 = f32[6,32,9984]{2,1,0:T(8,128)} custom-call(bf16[8,32,10752]{2,1,0:T(8,128)(2,1)} %select_convert_fusion.s0.s1.s2, bf16[8,32,10752]{2,1,0:T(8,128)(2,1)} %select_convert_fusion.s0.s1.s2, bf16[8,32,10752]{2,1,0:T(8,128)(2,1)} %select_convert_fusion.s0.s1.s2, bf16[3,3,96,32]{3,2,1,0:T(8,128)(2,1)} %bitcast.249), custom_call_target="tpu_custom_call" | custom-call | tf_op jit(solution)/shard_map/pallas_call | solution.py:140
  232.0 5.9 %select_convert_fusion.1.s0.s1.s2 = bf16[6,32,9984]{2,1,0:T(8,128)(2,1)} fusion(f32[6,32,9984]{2,1,0:T(8,128)} %shard_map.83, pred[6,9984]{1,0:T(8,128)(4,1)S(1)} %copy-done.3), kind=kLoop, calls=%fused_computation.1 | loop fusion | flops 5750784 | bytes 11561472 | tf_op jit(solution)/shard_map/convert_element_type | solution.py:239
  237.8 8.9 %shard_map.84 = f32[4,8,9216]{2,1,0:T(8,128)} custom-call(bf16[6,32,9984]{2,1,0:T(8,128)(2,1)} %select_convert_fusion.1.s0.s1.s2, bf16[6,32,9984]{2,1,0:T(8,128)(2,1)} %select_convert_fusion.1.s0.s1.s2, bf16[6,32,9984]{2,1,0:T(8,128)(2,1)} %select_convert_fusion.1.s0.s1.s2, bf16[3,3,24,32]{3,2,1,0:T(8,128)(2,1)} %pad_bitcast_fusion.w_ref), custom_call_target="tpu_custom_call" | custom-call | tf_op jit(solution)/shard_map/pallas_call | solution.py:140
  246.7 1.3 slice.140
  248.1 0.2 reshape.514
  248.4 0.7 copy.82
  (44 shorter events, 0.8 us)
Async XLA Ops:
  6.5 33.0 %all-gather.2.cloned.1.call-start = ((), (), s32[]{:S(2)}) async-start(), calls=%async_computation.3 | async-start | bytes 1327104 | tf_op jit(solution)/shard_map/all_gather | solution.py:187
  41.4 1.2 copy-start.8
  41.4 1.2 copy-start.9
  45.3 8.3 %copy-start.12 = (s32[128,6]{0,1:T(8,128)S(1)}, s32[128,6]{0,1:T(8,128)}, u32[]{:S(2)}) copy-start(s32[128,6]{0,1:T(8,128)} %param.11) | copy-start | bytes 9220
  45.3 24.2 %all-to-all-start = ((bf16[2,1,4,192,384]{4,2,0,1,3:T(4,128)(2,1)}), bf16[2,1,4,192,384]{4,2,0,1,3:T(4,128)(2,1)S(1)}, u32[]{:S(2)}, u32[]{:S(2)}) async-start(bf16[2,1,4,192,384]{4,2,0,1,3:T(4,128)(2,1)} %copy.67), calls=%async_computation | async-start | bytes 2359296 | tf_op jit(solution)/shard_map/all_to_all | solution.py:196
  73.9 1.9 copy-start.4
  73.9 1.9 copy-start.5
  78.6 22.3 %all-to-all-start.1 = ((bf16[2,1,128,6,384]{4,0,3,1,2:T(2,128)(2,1)}), bf16[2,1,128,6,384]{4,0,3,1,2:T(2,128)(2,1)S(1)}, u32[]{:S(2)}, u32[]{:S(2)}) async-start(bf16[2,1,128,6,384]{4,0,3,1,2:T(2,128)(2,1)} %copy.72), calls=%async_computation.1 | async-start | bytes 2359296 | tf_op jit(solution)/shard_map/all_to_all | solution.py:203
  85.2 62.4 %reduce-scatter.4.cloned.1.call-start = ((), (), s32[]{:S(2)}) async-start(), calls=%async_computation.4 | async-start | bytes 1327104
  100.8 0.9 copy-start.6
  100.8 1.0 copy-start.7
  101.8 1.1 copy-start.1
  101.9 1.2 copy-start.2
  107.7 0.7 copy-start.13
  107.7 40.8 %copy-start = (f32[2,4,24,384]{3,2,1,0:T(8,128)S(1)}, f32[2,4,24,384]{3,2,1,0:T(8,128)}, u32[]{:S(2)}) copy-start(f32[2,4,24,384]{3,2,1,0:T(8,128)} %param.8) | copy-start | bytes 884740
  108.4 56.6 %copy-start.10 = (bf16[3,3,32,3,2]{2,4,3,1,0:T(2,128)(2,1)S(1)}, bf16[3,3,32,3,2]{2,4,3,1,0:T(2,128)(2,1)}, u32[]{:S(2)}) copy-start(bf16[3,3,32,3,2]{2,4,3,1,0:T(2,128)(2,1)} %param.13) | copy-start | bytes 10372
  108.5 57.4 %copy-start.11 = (bf16[3,3,2,3,32]{4,2,3,1,0:T(2,128)(2,1)S(1)}, bf16[3,3,2,3,32]{4,2,3,1,0:T(2,128)(2,1)}, u32[]{:S(2)}) copy-start(bf16[3,3,2,3,32]{4,2,3,1,0:T(2,128)(2,1)} %param.15) | copy-start | bytes 10372
  148.7 5.6 %collective-permute-start = (bf16[2,4,3,384]{3,2,0,1:T(4,128)(2,1)S(1)}, bf16[2,4,3,384]{3,2,0,1:T(4,128)(2,1)S(1)}, u32[]{:S(2)}, u32[]{:S(2)}) collective-permute-start(bf16[2,4,3,384]{3,2,0,1:T(4,128)(2,1)S(1)} %get-tuple-element.23), channel_id=1, source_target_pairs={{0,32},{32,64},{64,96},{96,128},{128,160},{160,192},{192,224},{1,3... | collective-permute-start | bytes 55304 | tf_op jit(solution)/shard_map/ppermute | solution.py:16
  152.3 7.3 %collective-permute-start.1 = (bf16[2,4,3,384]{3,2,0,1:T(4,128)(2,1)S(1)}, bf16[2,4,3,384]{3,2,0,1:T(4,128)(2,1)S(1)}, u32[]{:S(2)}, u32[]{:S(2)}) collective-permute-start(bf16[2,4,3,384]{3,2,0,1:T(4,128)(2,1)S(1)} %get-tuple-element.24), channel_id=1, source_target_pairs={{32,0},{64,32},{96,64},{128,96},{160,128},{192,160},{224,192},{33,... | collective-permute-start | bytes 55304 | tf_op jit(solution)/shard_map/ppermute | solution.py:19
  159.7 7.7 %collective-permute-start.2 = (bf16[2,3,30,384]{3,2,0,1:T(8,128)(2,1)S(1)}, bf16[2,3,30,384]{3,2,0,1:T(8,128)(2,1)S(1)}, u32[]{:S(2)}, u32[]{:S(2)}) collective-permute-start(bf16[2,3,30,384]{3,2,0,1:T(8,128)(2,1)S(1)} %get-tuple-element.17), channel_id=1, source_target_pairs={{0,1},{1,2},{2,3},{3,4},{4,5},{5,6},{6,7},{7,8},{8,9},{9,10},{10,1... | collective-permute-start | bytes 414728 | tf_op jit(solution)/shard_map/ppermute | solution.py:16
  162.3 8.9 %collective-permute-start.3 = (bf16[2,3,30,384]{3,2,0,1:T(8,128)(2,1)S(1)}, bf16[2,3,30,384]{3,2,0,1:T(8,128)(2,1)S(1)}, u32[]{:S(2)}, u32[]{:S(2)}) collective-permute-start(bf16[2,3,30,384]{3,2,0,1:T(8,128)(2,1)S(1)} %get-tuple-element.18), channel_id=1, source_target_pairs={{1,0},{2,1},{3,2},{4,3},{5,4},{6,5},{7,6},{8,7},{9,8},{10,9},{11,1... | collective-permute-start | bytes 414728 | tf_op jit(solution)/shard_map/ppermute | solution.py:19
  200.7 31.2 %copy-start.3 = (pred[6,9984]{1,0:T(8,128)(4,1)S(1)}, pred[6,9984]{1,0:T(8,128)(4,1)}, u32[]{:S(2)}) copy-start(pred[6,9984]{1,0:T(8,128)(4,1)} %broadcast_and_fusion.1) | copy-start | bytes 179716
Sparse Core Ops, SparseCore 0:
  9.2 30.2 all-gather.1
  107.9 39.6 reduce-scatter.3

commit v5 on v4

--- a/solution.py
+++ b/solution.py
@@ -45,14 +45,22 @@
 READ = 384
 CHUNK = 1536
 
-def conv_flat(stack, kernel, out_rows):
+def finish(total, refs, start, size):
+    if len(refs) == 1:
+        return total
+    keep = refs[0][0, :, pl.ds(start, size)] > 0
+    return jnp.where(keep, jnp.maximum(total, 0.0), 0.0).astype(jnp.bfloat16)
+
+
+def conv_flat(stack, kernel, out_rows, inside=None):
     depth_in, width, lanes_in = stack.shape
     out_depth = depth_in - 2
     out_channels = kernel.shape[2]
     lanes = out_rows * READ
     starts = range(0, lanes, CHUNK)
 
-    def body(s0, s1, s2, w_ref, o_ref):
+    def body(s0, s1, s2, w_ref, *refs):
+        o_ref = refs[-1]
         sources = (s0, s1, s2)
         for start in starts:
             size = min(CHUNK, lanes - start)
@@ -64,18 +72,24 @@
                         sources[dz][0, :, pl.ds(start + dy * READ, size)],
                         preferred_element_type=jnp.float32,
                     )
-            o_ref[0, :, pl.ds(start, size)] = acc
+            o_ref[0, :, pl.ds(start, size)] = finish(acc, refs, start, size)
 
     in_specs = [
         pl.BlockSpec((1, width, lanes_in), lambda z, dz=dz: (z + dz, 0, 0)) for dz in range(3)
     ] + [pl.BlockSpec(kernel.shape, lambda z: (0, 0, 0, 0))]
+    extra = ()
+    kind = jnp.float32
+    if inside is not None:
+        in_specs.append(pl.BlockSpec((1, 1, lanes), lambda z: (z, 0, 0)))
+        extra = (inside,)
+        kind = jnp.bfloat16
     return pl.pallas_call(
         body,
         grid=(out_depth,),
         in_specs=in_specs,
         out_specs=pl.BlockSpec((1, out_channels, lanes), lambda z: (z, 0, 0)),
-        out_shape=jax.ShapeDtypeStruct((out_depth, out_channels, lanes), jnp.float32),
-    )(stack, stack, stack, kernel)
+        out_shape=jax.ShapeDtypeStruct((out_depth, out_channels, lanes), kind),
+    )(stack, stack, stack, kernel, *extra)
 
 
 def shifted_stack(block):
@@ -101,19 +115,20 @@
     return jnp.pad(matrix, ((0, 0), (0, 0), (0, extra_out), (0, extra_in)))
 
 
-def convolve_flat(block, weight, out_rows):
-    out = conv_flat(shifted_stack(block), kernel_matrix(weight), out_rows)
+def convolve_flat(block, weight, out_rows, inside=None):
+    out = conv_flat(shifted_stack(block), kernel_matrix(weight), out_rows, inside)
     return out[:, : weight.shape[2]]
 
 
-def conv_roll(block, kernel, out_rows):
+def conv_roll(block, kernel, out_rows, inside=None):
     depth_in, width, lanes_in = block.shape
     out_depth = depth_in - 2
     out_channels = kernel.shape[2] // 3
     lanes = out_rows * READ
     starts = range(0, lanes, CHUNK)
 
-    def body(s0, s1, s2, w_ref, o_ref):
+    def body(s0, s1, s2, w_ref, *refs):
+        o_ref = refs[-1]
         sources = (s0, s1, s2)
         for start in starts:
             size = min(CHUNK, lanes - start)
@@ -128,22 +143,29 @@
             place = lax.broadcasted_iota(jnp.int32, (out_channels, size), 1) % READ
             left = pltpu.roll(acc[:out_channels], 1, 1)
             right = pltpu.roll(acc[2 * out_channels :], size - 1, 1)
-            o_ref[0, :, pl.ds(start, size)] = (
+            total = (
                 acc[out_channels : 2 * out_channels]
                 + jnp.where(place == 0, 0.0, left)
                 + jnp.where(place == READ - 1, 0.0, right)
             )
+            o_ref[0, :, pl.ds(start, size)] = finish(total, refs, start, size)
 
     in_specs = [
         pl.BlockSpec((1, width, lanes_in), lambda z, dz=dz: (z + dz, 0, 0)) for dz in range(3)
     ] + [pl.BlockSpec(kernel.shape, lambda z: (0, 0, 0, 0))]
+    extra = ()
+    kind = jnp.float32
+    if inside is not None:
+        in_specs.append(pl.BlockSpec((1, 1, lanes), lambda z: (z, 0, 0)))
+        extra = (inside,)
+        kind = jnp.bfloat16
     return pl.pallas_call(
         body,
         grid=(out_depth,),
         in_specs=in_specs,
         out_specs=pl.BlockSpec((1, out_channels, lanes), lambda z: (z, 0, 0)),
-        out_shape=jax.ShapeDtypeStruct((out_depth, out_channels, lanes), jnp.float32),
-    )(block, block, block, kernel)
+        out_shape=jax.ShapeDtypeStruct((out_depth, out_channels, lanes), kind),
+    )(block, block, block, kernel, *extra)
 
 
 def tap_matrix(weight):
@@ -163,8 +185,8 @@
     return block
 
 
-def convolve_roll(block, weight, out_rows):
-    out = conv_roll(padded_channels(block), tap_matrix(weight), out_rows)
+def convolve_roll(block, weight, out_rows, inside=None):
+    out = conv_roll(padded_channels(block), tap_matrix(weight), out_rows, inside)
     return out[:, : weight.shape[2]]
 
 
@@ -224,19 +246,21 @@
     activations = activations.transpose(1, 0, 2, 3).reshape(depth, 2, rows * READ)
     for layer_index, weight in enumerate(weights):
         rows = rows - 2
-        if layer_index == 0:
-            output = convolve_flat(activations, weight, rows)
-        else:
-            output = convolve_roll(activations, weight, rows)
+        inside = None
         if layer_index < 2:
             margin = 2 - layer_index
-            depth_places = slab_first - margin + jnp.arange(output.shape[0], dtype=jnp.int32)
+            depth_places = slab_first - margin + jnp.arange(depth - 2, dtype=jnp.int32)
             row_places = coil_first - margin + jnp.arange(rows * READ, dtype=jnp.int32) // READ
             inside = (
                 ((depth_places >= 0) & (depth_places < partitions))[:, None, None]
                 & ((row_places >= 0) & (row_places < phases))[None, None, :]
-            )
-            activations = jnp.where(inside, jax.nn.relu(output), 0.0).astype(jnp.bfloat16)
+            ).astype(jnp.float32)
+        depth = depth - 2
+        if layer_index == 0:
+            output = convolve_flat(activations, weight, rows, inside)
+        else:
+            output = convolve_roll(activations, weight, rows, inside)
+        activations = output
     correction = output.reshape(slab_rows, 2, coil_rows, READ).transpose(1, 0, 2, 3)
     return updated + correction
 

time: 257 us -> 243 us (0.946)
  other arithmetic: 35.5 us -> 21.8 us
    convert_element_type x2, other arithmetic: 13.6 us -> 1.9 us  [per_device(): inside = (((depth_places >= 0) & (depth_places < partitions))[:, None, No...]
    unnamed x32 -> x30, local copies, waits for them, and re-layouts: 7.24 us -> 6.58 us
where the time goes in v5:
time: 243 us; the launch traced here: 242 us
  waiting for transfers between devices  97.8 us (40%)
  Pallas kernels  56.4 us (23%)
  starting transfers between devices  26.1 us (11%)
  other arithmetic  21.8 us (9%)
  local copies, waits for them, and re-layouts  19.6 us (8%)
  between operations  14.5 us (6%)
  matrix products  6.22 us (3%)
    pallas_call x2, Pallas kernels, conv_roll(): pl.pallas_call(body, grid=(out_depth,), in_specs=in_specs, out_specs=pl.B...  39.9 us
    unnamed x3, waiting for transfers between devices  38.6 us
    all_gather x1, waiting for transfers between devices, per_device(): lax.all_gather(pixels, 'coil', axis=2, tiled=True).astype(jnp.float32)  21.2 us
    pallas_call x1, Pallas kernels, conv_flat(): pl.pallas_call(body, grid=(out_depth,), in_specs=in_specs, out_specs=pl.B...  16.5 us
    all_to_all x1, waiting for transfers between devices, per_device(): lax.all_to_all(residual, 'slab', split_axis=2, concat_axis=3, tiled=True)  14.6 us
    all_to_all x1, waiting for transfers between devices, per_device(): lax.all_to_all(spectrum, 'slab', split_axis=3, concat_axis=2, tiled=True)  13.3 us
    ppermute x2, waiting for transfers between devices, padded_2(): lax.ppermute(lax.slice_in_dim(block, 0, width, axis=dim), axis, backward)  9.61 us
    all_to_all x1, starting transfers between devices, per_device(): lax.all_to_all(spectrum, 'slab', split_axis=3, concat_axis=2, tiled=True)  8.26 us
  transfers between devices with their start and end apart: 8, of which 7 were waited for; matrix products, arithmetic and copies ran while one was open for 6% of the time, Pallas kernels for 0%

profile of v5, /device:TPU:121, one launch (start us, length us, event | category | flops | bytes accessed | tf_op | source)
XLA Modules:
  0.0 242.4 jit_solution(11506802620476938768)
XLA Ops:
  6.5 1.6 copy.122
  8.2 1.4 convert_element_type.196
  9.6 0.8 fusion.84
  10.4 0.8 fusion.60
  11.2 2.3 fusion.59
  13.6 2.6 %fusion.43 = (bf16[384,1,384]{2,0,1:T(8,128)(2,1)S(1)}, bf16[384,1,384]{2,0,1:T(8,128)(2,1)S(1)}) fusion(), kind=kLoop, calls=%fused_computation.86 | loop fusion | flops 1916928 | bytes 589824 | tf_op jit(solution)/shard_map/stack;squeeze | solution.py:37
  16.2 0.9 fusion.47
  17.1 1.2 fusion.33
  18.3 21.2 %all-gather.2.cloned.1.call-done = bf16[2,4,192,384]{3,2,0,1:T(8,128)(2,1)} async-done(((bf16[2,4,24,384]{3,2,0,1:T(8,128)(2,1)}), bf16[2,4,192,384]{3,2,0,1:T(8,128)(2,1)}) %all-gather.2.cloned.1.call-update) | async-done | bytes 1179664 | tf_op jit(solution)/shard_map/all_gather | solution.py:209
  39.5 1.4 convert_element_type.202
  40.9 0.4 fusion.17
  41.4 1.1 fusion.7
  42.5 0.8 fusion.3
  43.4 1.9 copy.67
  45.3 8.3 %all-to-all-start = ((bf16[2,1,4,192,384]{4,2,0,1,3:T(4,128)(2,1)}), bf16[2,1,4,192,384]{4,2,0,1,3:T(4,128)(2,1)S(1)}, u32[]{:S(2)}, u32[]{:S(2)}) async-start(bf16[2,1,4,192,384]{4,2,0,1,3:T(4,128)(2,1)} %copy.67), calls=%async_computation | async-start | bytes 2359296 | tf_op jit(solution)/shard_map/all_to_all | solution.py:218
  54.3 0.6 compare_and_fusion.3
  54.9 0.3 fusion.87
  55.1 0.3 fusion.85
  55.4 0.7 fusion.64
  56.2 13.3 %all-to-all-done = bf16[2,1,4,192,384]{4,2,0,1,3:T(4,128)(2,1)S(1)} async-done(((bf16[2,1,4,192,384]{4,2,0,1,3:T(4,128)(2,1)}), bf16[2,1,4,192,384]{4,2,0,1,3:T(4,128)(2,1)S(1)}, u32[]{:S(2)}, u32[]{:S(2)}) %all-to-all-start) | async-done | bytes 1179680 | tf_op jit(solution)/shard_map/all_to_all | solution.py:218
  69.5 0.4 copy.68
  69.9 1.6 copy.69
  71.5 2.4 reshape.564
  73.9 1.9 fusion.9
  75.8 0.5 fusion.6
  76.3 2.2 copy.72
  78.5 6.8 %all-to-all-start.1 = ((bf16[2,1,128,6,384]{4,0,3,1,2:T(2,128)(2,1)}), bf16[2,1,128,6,384]{4,0,3,1,2:T(2,128)(2,1)S(1)}, u32[]{:S(2)}, u32[]{:S(2)}) async-start(bf16[2,1,128,6,384]{4,0,3,1,2:T(2,128)(2,1)} %copy.72), calls=%async_computation.1 | async-start | bytes 2359296 | tf_op jit(solution)/shard_map/all_to_all | solution.py:225
  85.4 1.0 and_convert_fusion.refs_0_
  86.4 14.6 %all-to-all-done.1 = bf16[2,1,128,6,384]{4,0,3,1,2:T(2,128)(2,1)S(1)} async-done(((bf16[2,1,128,6,384]{4,0,3,1,2:T(2,128)(2,1)}), bf16[2,1,128,6,384]{4,0,3,1,2:T(2,128)(2,1)S(1)}, u32[]{:S(2)}, u32[]{:S(2)}) %all-to-all-start.1) | async-done | bytes 1179680 | tf_op jit(solution)/shard_map/all_to_all | solution.py:225
  101.0 0.5 copy.73
  101.5 0.5 copy-done.5
  101.9 0.1 copy-done.6
  102.0 0.8 fusion.4
  102.9 0.2 copy-done.1
  103.1 0.2 copy-done.2
  103.3 1.1 convert_bitcast_fusion
  104.4 0.3 fusion.20
  104.7 0.2 fusion
  104.9 1.2 copy.123
  106.2 1.7 reshape.576
  108.0 0.9 and_convert_fusion.1.refs_0_
  108.9 38.6 %reduce-scatter.4.cloned.1.call-done = bf16[24,3072]{1,0:T(8,128)(2,1)} async-done(((bf16[192,3072]{1,0:T(8,128)(2,1)}), bf16[24,3072]{1,0:T(8,128)(2,1)}) %reduce-scatter.4.cloned.1.call-update) | async-done | bytes 147472
  147.4 1.0 reshape.577
  148.5 3.7 %collective-permute-start = (bf16[2,4,3,384]{3,2,0,1:T(4,128)(2,1)S(1)}, bf16[2,4,3,384]{3,2,0,1:T(4,128)(2,1)S(1)}, u32[]{:S(2)}, u32[]{:S(2)}) collective-permute-start(bf16[2,4,3,384]{3,2,0,1:T(4,128)(2,1)S(1)} %get-tuple-element.23), channel_id=1, source_target_pairs={{0,32},{32,64},{64,96},{96,128},{128,160},{160,192},{192,224},{1,3... | collective-permute-start | bytes 55304 | tf_op jit(solution)/shard_map/ppermute | solution.py:16
  152.2 1.9 collective-permute-start.1
  154.2 5.3 %collective-permute-done.1 = bf16[2,4,3,384]{3,2,0,1:T(4,128)(2,1)S(1)} collective-permute-done((bf16[2,4,3,384]{3,2,0,1:T(4,128)(2,1)S(1)}, bf16[2,4,3,384]{3,2,0,1:T(4,128)(2,1)S(1)}, u32[]{:S(2)}, u32[]{:S(2)}) %collective-permute-start.1) | collective-permute-done | bytes 18464 | tf_op jit(solution)/shard_map/ppermute | solution.py:19
  159.6 2.8 %collective-permute-start.2 = (bf16[2,3,30,384]{3,2,0,1:T(8,128)(2,1)S(1)}, bf16[2,3,30,384]{3,2,0,1:T(8,128)(2,1)S(1)}, u32[]{:S(2)}, u32[]{:S(2)}) collective-permute-start(bf16[2,3,30,384]{3,2,0,1:T(8,128)(2,1)S(1)} %get-tuple-element.17), channel_id=1, source_target_pairs={{0,1},{1,2},{2,3},{3,4},{4,5},{5,6},{6,7},{7,8},{8,9},{9,10},{10,1... | collective-permute-start | bytes 414728 | tf_op jit(solution)/shard_map/ppermute | solution.py:16
  162.5 2.4 %collective-permute-start.3 = (bf16[2,3,30,384]{3,2,0,1:T(8,128)(2,1)S(1)}, bf16[2,3,30,384]{3,2,0,1:T(8,128)(2,1)S(1)}, u32[]{:S(2)}, u32[]{:S(2)}) collective-permute-start(bf16[2,3,30,384]{3,2,0,1:T(8,128)(2,1)S(1)} %get-tuple-element.18), channel_id=1, source_target_pairs={{1,0},{2,1},{3,2},{4,3},{5,4},{6,5},{7,6},{8,7},{9,8},{10,9},{11,1... | collective-permute-start | bytes 414728 | tf_op jit(solution)/shard_map/ppermute | solution.py:19
  165.0 0.1 copy.81
  165.1 0.6 pad.18.w_ref
  165.8 0.1 pad.23.clone
  165.9 0.6 pad_bitcast_fusion.w_ref
  166.5 0.5 collective-permute-done.2
  167.0 4.3 %collective-permute-done.3 = bf16[2,3,30,384]{3,2,0,1:T(8,128)(2,1)S(1)} collective-permute-done((bf16[2,3,30,384]{3,2,0,1:T(8,128)(2,1)S(1)}, bf16[2,3,30,384]{3,2,0,1:T(8,128)(2,1)S(1)}, u32[]{:S(2)}, u32[]{:S(2)}) %collective-permute-start.3) | collective-permute-done | bytes 138272 | tf_op jit(solution)/shard_map/ppermute | solution.py:19
  171.4 0.1 maximum_bitcast_fusion.6
  171.5 0.2 reshape.550
  171.6 1.4 compare_select_fusion.1
  173.0 3.7 %maximum_maximum_fusion.s0.s1.s2 = bf16[10,16,11520]{2,1,0:T(8,128)(2,1)} fusion(bf16[10,2,11520]{2,1,0:T(2,128)(2,1)S(1)} %get-tuple-element.14, bf16[10,2,11520]{2,1,0:T(2,128)(2,1)S(1)} %reshape.550, bf16[10,2,11520]{2,1,0:T(2,128)(2,1)S(1)} %get-tuple-element.13, bf16[16]{0:T(256)(128)(2,1)S(1)} %pad.23.clone), kind=kLoop, calls=%fused_computation | loop fusion | flops 14745600 | bytes 5068832 | tf_op jit(solution)/shard_map/concatenate | solution.py:107
  176.8 16.5 %shard_map.82.s0.s1.s2 = bf16[8,32,10752]{2,1,0:T(8,128)(2,1)} custom-call(bf16[10,16,11520]{2,1,0:T(8,128)(2,1)} %maximum_maximum_fusion.s0.s1.s2, bf16[10,16,11520]{2,1,0:T(8,128)(2,1)} %maximum_maximum_fusion.s0.s1.s2, bf16[10,16,11520]{2,1,0:T(8,128)(2,1)} %maximum_maximum_fusion.s0.s1.s2, bf16[3,3,32,16]{3,2,1,0:T(8,128)(2,1)} %pad.18.w_ref, ...), custom_call_target="tpu_custom_call" | custom-call | tf_op jit(solution)/shard_map/pallas_call | solution.py:86
  193.3 31.0 %shard_map.83.s0.s1.s2 = bf16[6,32,9984]{2,1,0:T(8,128)(2,1)} custom-call(bf16[8,32,10752]{2,1,0:T(8,128)(2,1)} %shard_map.82.s0.s1.s2, bf16[8,32,10752]{2,1,0:T(8,128)(2,1)} %shard_map.82.s0.s1.s2, bf16[8,32,10752]{2,1,0:T(8,128)(2,1)} %shard_map.82.s0.s1.s2, bf16[3,3,96,32]{3,2,1,0:T(8,128)(2,1)} %bitcast.249, f32[6,1,9984]{2,1,0:T(1,128)} %and_convert_fusion.1.refs_0_), custom_call_target="tpu_custom_call" | custom-call | tf_op jit(solution)/shard_map/pallas_call | solution.py:162
  224.3 8.9 %shard_map.84 = f32[4,8,9216]{2,1,0:T(8,128)} custom-call(bf16[6,32,9984]{2,1,0:T(8,128)(2,1)} %shard_map.83.s0.s1.s2, bf16[6,32,9984]{2,1,0:T(8,128)(2,1)} %shard_map.83.s0.s1.s2, bf16[6,32,9984]{2,1,0:T(8,128)(2,1)} %shard_map.83.s0.s1.s2, bf16[3,3,24,32]{3,2,1,0:T(8,128)(2,1)} %pad_bitcast_fusion.w_ref), custom_call_target="tpu_custom_call" | custom-call | tf_op jit(solution)/shard_map/pallas_call | solution.py:162
  233.2 1.3 slice.140
  234.6 0.2 reshape.554
  234.9 0.7 copy.82
  (40 shorter events, 0.5 us)
Async XLA Ops:
  6.5 33.0 %all-gather.2.cloned.1.call-start = ((), (), s32[]{:S(2)}) async-start(), calls=%async_computation.3 | async-start | bytes 1327104 | tf_op jit(solution)/shard_map/all_gather | solution.py:209
  41.4 1.2 copy-start.7
  41.4 1.2 copy-start.8
  45.3 8.3 %copy-start.11 = (s32[128,6]{0,1:T(8,128)S(1)}, s32[128,6]{0,1:T(8,128)}, u32[]{:S(2)}) copy-start(s32[128,6]{0,1:T(8,128)} %param.11) | copy-start | bytes 9220
  45.3 24.2 %all-to-all-start = ((bf16[2,1,4,192,384]{4,2,0,1,3:T(4,128)(2,1)}), bf16[2,1,4,192,384]{4,2,0,1,3:T(4,128)(2,1)S(1)}, u32[]{:S(2)}, u32[]{:S(2)}) async-start(bf16[2,1,4,192,384]{4,2,0,1,3:T(4,128)(2,1)} %copy.67), calls=%async_computation | async-start | bytes 2359296 | tf_op jit(solution)/shard_map/all_to_all | solution.py:218
  73.9 1.9 copy-start.3
  73.9 1.9 copy-start.4
  78.5 6.9 %copy-start.12 = (pred[8]{0:T(512)(128)(4,1)S(1)}, pred[8]{0:T(512)(128)(4,1)}, u32[]{:S(2)}) copy-start(pred[8]{0:T(512)(128)(4,1)} %compare_and_fusion.3) | copy-start | bytes 28
  78.5 22.5 %all-to-all-start.1 = ((bf16[2,1,128,6,384]{4,0,3,1,2:T(2,128)(2,1)}), bf16[2,1,128,6,384]{4,0,3,1,2:T(2,128)(2,1)S(1)}, u32[]{:S(2)}, u32[]{:S(2)}) async-start(bf16[2,1,128,6,384]{4,0,3,1,2:T(2,128)(2,1)} %copy.72), calls=%async_computation.1 | async-start | bytes 2359296 | tf_op jit(solution)/shard_map/all_to_all | solution.py:225
  85.4 62.1 %reduce-scatter.4.cloned.1.call-start = ((), (), s32[]{:S(2)}) async-start(), calls=%async_computation.4 | async-start | bytes 1327104
  101.0 0.9 copy-start.5
  101.0 1.0 copy-start.6
  102.0 1.1 copy-start.1
  102.0 1.2 copy-start.2
  107.9 40.5 %copy-start = (f32[2,4,24,384]{3,2,1,0:T(8,128)S(1)}, f32[2,4,24,384]{3,2,1,0:T(8,128)}, u32[]{:S(2)}) copy-start(f32[2,4,24,384]{3,2,1,0:T(8,128)} %param.8) | copy-start | bytes 884740
  107.9 57.0 %copy-start.9 = (bf16[3,3,32,3,2]{2,4,3,1,0:T(2,128)(2,1)S(1)}, bf16[3,3,32,3,2]{2,4,3,1,0:T(2,128)(2,1)}, u32[]{:S(2)}) copy-start(bf16[3,3,32,3,2]{2,4,3,1,0:T(2,128)(2,1)} %param.13) | copy-start | bytes 10372
  108.9 57.0 %copy-start.10 = (bf16[3,3,2,3,32]{4,2,3,1,0:T(2,128)(2,1)S(1)}, bf16[3,3,2,3,32]{4,2,3,1,0:T(2,128)(2,1)}, u32[]{:S(2)}) copy-start(bf16[3,3,2,3,32]{4,2,3,1,0:T(2,128)(2,1)} %param.15) | copy-start | bytes 10372
  148.5 5.7 %collective-permute-start = (bf16[2,4,3,384]{3,2,0,1:T(4,128)(2,1)S(1)}, bf16[2,4,3,384]{3,2,0,1:T(4,128)(2,1)S(1)}, u32[]{:S(2)}, u32[]{:S(2)}) collective-permute-start(bf16[2,4,3,384]{3,2,0,1:T(4,128)(2,1)S(1)} %get-tuple-element.23), channel_id=1, source_target_pairs={{0,32},{32,64},{64,96},{96,128},{128,160},{160,192},{192,224},{1,3... | collective-permute-start | bytes 55304 | tf_op jit(solution)/shard_map/ppermute | solution.py:16
  152.2 7.3 %collective-permute-start.1 = (bf16[2,4,3,384]{3,2,0,1:T(4,128)(2,1)S(1)}, bf16[2,4,3,384]{3,2,0,1:T(4,128)(2,1)S(1)}, u32[]{:S(2)}, u32[]{:S(2)}) collective-permute-start(bf16[2,4,3,384]{3,2,0,1:T(4,128)(2,1)S(1)} %get-tuple-element.24), channel_id=1, source_target_pairs={{32,0},{64,32},{96,64},{128,96},{160,128},{192,160},{224,192},{33,... | collective-permute-start | bytes 55304 | tf_op jit(solution)/shard_map/ppermute | solution.py:19
  159.6 7.4 %collective-permute-start.2 = (bf16[2,3,30,384]{3,2,0,1:T(8,128)(2,1)S(1)}, bf16[2,3,30,384]{3,2,0,1:T(8,128)(2,1)S(1)}, u32[]{:S(2)}, u32[]{:S(2)}) collective-permute-start(bf16[2,3,30,384]{3,2,0,1:T(8,128)(2,1)S(1)} %get-tuple-element.17), channel_id=1, source_target_pairs={{0,1},{1,2},{2,3},{3,4},{4,5},{5,6},{6,7},{7,8},{8,9},{9,10},{10,1... | collective-permute-start | bytes 414728 | tf_op jit(solution)/shard_map/ppermute | solution.py:16
  162.5 8.9 %collective-permute-start.3 = (bf16[2,3,30,384]{3,2,0,1:T(8,128)(2,1)S(1)}, bf16[2,3,30,384]{3,2,0,1:T(8,128)(2,1)S(1)}, u32[]{:S(2)}, u32[]{:S(2)}) collective-permute-start(bf16[2,3,30,384]{3,2,0,1:T(8,128)(2,1)S(1)} %get-tuple-element.18), channel_id=1, source_target_pairs={{1,0},{2,1},{3,2},{4,3},{5,4},{6,5},{7,6},{8,7},{9,8},{10,9},{11,1... | collective-permute-start | bytes 414728 | tf_op jit(solution)/shard_map/ppermute | solution.py:19
Sparse Core Ops, SparseCore 0:
  9.2 30.2 all-gather.1
  108.0 39.3 reduce-scatter.3

commit v6 on v5

--- a/solution.py
+++ b/solution.py
@@ -223,22 +223,32 @@
     ).astype(jnp.bfloat16)
     residual = fourier_section(residual, 2, True)
     residual = lax.all_to_all(residual, "slab", split_axis=2, concat_axis=3, tiled=True)
-    residual = fourier_section(residual, 3, True)
-    restored = fourier_section(residual, 4, True).astype(jnp.float32)
-    sensitivity = coil_maps.astype(jnp.float32)
-    partial_value = jnp.stack(
-        [
-            jnp.sum(sensitivity[0] * restored[0] + sensitivity[1] * restored[1], axis=0),
-            jnp.sum(sensitivity[0] * restored[1] - sensitivity[1] * restored[0], axis=0),
-        ]
-    )
     step_size = consistency_weight[0]
     coil_first = lax.axis_index("coil") * coil_rows
     slab_first = lax.axis_index("slab") * slab_rows
     weights = (conv_first, conv_middle, conv_last)
-    scattered = lax.psum_scatter(
-        (-step_size * partial_value).astype(jnp.bfloat16), "coil", scatter_dimension=2, tiled=True
-    )
+    half = slab_rows // 2
+    pieces = []
+    for first in (0, half):
+        part = lax.slice_in_dim(residual, first, first + half, axis=2)
+        part = fourier_section(part, 3, True)
+        restored = fourier_section(part, 4, True).astype(jnp.float32)
+        sensitivity = lax.slice_in_dim(coil_maps, first, first + half, axis=2).astype(jnp.float32)
+        partial_value = jnp.stack(
+            [
+                jnp.sum(sensitivity[0] * restored[0] + sensitivity[1] * restored[1], axis=0),
+                jnp.sum(sensitivity[0] * restored[1] - sensitivity[1] * restored[0], axis=0),
+            ]
+        )
+        pieces.append(
+            lax.psum_scatter(
+                (-step_size * partial_value).astype(jnp.bfloat16),
+                "coil",
+                scatter_dimension=2,
+                tiled=True,
+            )
+        )
+    scattered = jnp.concatenate(pieces, axis=1)
     updated = image_field + scattered.astype(jnp.float32)
     activations = padded_2(updated.astype(jnp.bfloat16), (("coil", 2),), 3)
     activations = padded_2(activations, (("slab", 1),), 3)

time: 243 us -> 280 us (1.15)
  waiting for transfers between devices: 97.8 us -> 129 us
  local copies, waits for them, and re-layouts: 19.6 us -> 23.2 us
    unnamed x3 -> x5, waiting for transfers between devices: 38.6 us -> 70.3 us
    dot_general x6 -> x8, matrix products: 6.22 us -> 7.66 us  [fourier_section(): lax.dot_general(matrix, values, (((2, 3), (0, along)), ((), ())), preferr...]
    unnamed x30 -> x39, local copies, waits for them, and re-layouts: 6.58 us -> 7.86 us
  transfers between devices with their start and end apart: 8 -> 9, of which waited for: 7 -> 8; matrix products, arithmetic and copies ran while one was open for 6% -> 7% of each run, Pallas kernels for 0% -> 0%
where the time goes in v6:
time: 280 us; the launch traced here: 279 us
  waiting for transfers between devices  129 us (46%)
  Pallas kernels  56.4 us (20%)
  starting transfers between devices  25.7 us (9%)
  local copies, waits for them, and re-layouts  23.2 us (8%)
  other arithmetic  22.7 us (8%)
  between operations  14.3 us (5%)
  matrix products  7.66 us (3%)
    unnamed x5, waiting for transfers between devices  70.3 us
    pallas_call x2, Pallas kernels, conv_roll(): pl.pallas_call(body, grid=(out_depth,), in_specs=in_specs, out_specs=pl.B...  39.9 us
    all_gather x1, waiting for transfers between devices, per_device(): lax.all_gather(pixels, 'coil', axis=2, tiled=True).astype(jnp.float32)  21.2 us
    pallas_call x1, Pallas kernels, conv_flat(): pl.pallas_call(body, grid=(out_depth,), in_specs=in_specs, out_specs=pl.B...  16.5 us
    all_to_all x1, waiting for transfers between devices, per_device(): lax.all_to_all(residual, 'slab', split_axis=2, concat_axis=3, tiled=True)  14.6 us
    all_to_all x1, waiting for transfers between devices, per_device(): lax.all_to_all(spectrum, 'slab', split_axis=3, concat_axis=2, tiled=True)  13.3 us
    ppermute x2, waiting for transfers between devices, padded_2(): lax.ppermute(lax.slice_in_dim(block, 0, width, axis=dim), axis, backward)  9.72 us
    all_to_all x1, starting transfers between devices, per_device(): lax.all_to_all(spectrum, 'slab', split_axis=3, concat_axis=2, tiled=True)  8.32 us
  transfers between devices with their start and end apart: 9, of which 8 were waited for; matrix products, arithmetic and copies ran while one was open for 7% of the time, Pallas kernels for 0%

profile of v6, /device:TPU:121, one launch (start us, length us, event | category | flops | bytes accessed | tf_op | source)
XLA Modules:
  0.0 279.1 jit_solution(6114759033425963469)
XLA Ops:
  6.5 1.6 copy.134
  8.2 1.4 convert_element_type.236
  9.6 0.8 fusion.86
  10.4 0.8 fusion.62
  11.2 2.3 fusion.61
  13.6 2.6 fusion.45
  16.2 0.9 fusion.50
  17.1 1.2 fusion.30
  18.3 21.2 %all-gather.2.cloned.1.call-done = bf16[2,4,192,384]{3,2,0,1:T(8,128)(2,1)} async-done(((bf16[2,4,24,384]{3,2,0,1:T(8,128)(2,1)}), bf16[2,4,192,384]{3,2,0,1:T(8,128)(2,1)}) %all-gather.2.cloned.1.call-update) | async-done | bytes 1179664 | tf_op jit(solution)/shard_map/all_gather | solution.py:209
  39.5 1.4 convert_element_type.238
  40.9 0.4 subtract_convert_fusion
  41.4 1.1 fusion.5
  42.5 0.8 fusion.2
  43.4 1.9 copy.72
  45.3 8.3 %all-to-all-start = ((bf16[2,1,4,192,384]{4,2,0,1,3:T(4,128)(2,1)}), bf16[2,1,4,192,384]{4,2,0,1,3:T(4,128)(2,1)}, u32[]{:S(2)}, u32[]{:S(2)}) async-start(bf16[2,1,4,192,384]{4,2,0,1,3:T(4,128)(2,1)} %copy.72), calls=%async_computation | async-start | bytes 2359296 | tf_op jit(solution)/shard_map/all_to_all | solution.py:218
  54.3 0.5 compare_and_fusion.3
  54.8 0.3 fusion.89
  55.1 0.3 fusion.87
  55.4 0.7 fusion.66
  56.3 13.3 %all-to-all-done = bf16[2,1,4,192,384]{4,2,0,1,3:T(4,128)(2,1)} async-done(((bf16[2,1,4,192,384]{4,2,0,1,3:T(4,128)(2,1)}), bf16[2,1,4,192,384]{4,2,0,1,3:T(4,128)(2,1)}, u32[]{:S(2)}, u32[]{:S(2)}) %all-to-all-start) | async-done | bytes 1179680 | tf_op jit(solution)/shard_map/all_to_all | solution.py:218
  69.6 1.7 copy.73
  71.3 1.6 copy.74
  72.9 2.4 reshape.690
  75.3 1.9 fusion.10
  77.2 0.5 fusion.4
  77.7 2.3 copy.77
  79.9 6.6 %all-to-all-start.1 = ((bf16[2,1,128,6,384]{4,0,3,1,2:T(2,128)(2,1)}), bf16[2,1,128,6,384]{4,0,3,1,2:T(2,128)(2,1)S(1)}, u32[]{:S(2)}, u32[]{:S(2)}) async-start(bf16[2,1,128,6,384]{4,0,3,1,2:T(2,128)(2,1)} %copy.77), calls=%async_computation.1 | async-start | bytes 2359296 | tf_op jit(solution)/shard_map/all_to_all | solution.py:225
  86.6 1.0 and_convert_fusion.refs_0_
  87.6 14.6 %all-to-all-done.1 = bf16[2,1,128,6,384]{4,0,3,1,2:T(2,128)(2,1)S(1)} async-done(((bf16[2,1,128,6,384]{4,0,3,1,2:T(2,128)(2,1)}), bf16[2,1,128,6,384]{4,0,3,1,2:T(2,128)(2,1)S(1)}, u32[]{:S(2)}, u32[]{:S(2)}) %all-to-all-start.1) | async-done | bytes 1179680 | tf_op jit(solution)/shard_map/all_to_all | solution.py:225
  102.2 0.5 copy.78
  102.7 1.7 fusion.98
  104.4 0.5 fusion.16
  104.9 0.5 copy-done.2
  105.4 0.2 copy-done.3
  105.6 0.7 convert_bitcast_fusion
  106.3 0.2 fusion.36
  106.4 0.2 fusion.34
  106.7 0.6 copy.138
  107.3 1.2 reshape.706
  108.7 1.5 fusion.15
  110.2 0.7 fusion.13
  111.1 0.6 copy.137
  111.7 1.2 reshape.708
  113.0 0.9 and_convert_fusion.1.refs_0_
  113.9 32.4 %reduce-scatter.7.cloned.1.call-done = bf16[24,1536]{1,0:T(8,128)(2,1)} async-done(((bf16[192,1536]{1,0:T(8,128)(2,1)}), bf16[24,1536]{1,0:T(8,128)(2,1)}) %reduce-scatter.7.cloned.1.call-update) | async-done | bytes 73744
  146.3 0.9 reshape.707
  147.3 37.8 %reduce-scatter.9.cloned.1.call-done = bf16[24,1536]{1,0:T(8,128)(2,1)} async-done(((bf16[192,1536]{1,0:T(8,128)(2,1)}), bf16[24,1536]{1,0:T(8,128)(2,1)}) %reduce-scatter.9.cloned.1.call-update) | async-done | bytes 73744
  185.0 0.9 reshape.709
  186.1 3.2 %collective-permute-start = (bf16[2,4,3,384]{3,2,1,0:T(4,128)(2,1)S(1)}, bf16[2,4,3,384]{3,2,1,0:T(4,128)(2,1)S(1)}, u32[]{:S(2)}, u32[]{:S(2)}) collective-permute-start(bf16[2,4,3,384]{3,2,1,0:T(4,128)(2,1)S(1)} %get-tuple-element.29), channel_id=1, source_target_pairs={{0,32},{32,64},{64,96},{96,128},{128,160},{160,192},{192,224},{1,3... | collective-permute-start | bytes 55304 | tf_op jit(solution)/shard_map/ppermute | solution.py:16
  189.3 1.9 collective-permute-start.1
  191.2 5.3 %collective-permute-done.1 = bf16[2,4,3,384]{3,2,1,0:T(4,128)(2,1)S(1)} collective-permute-done((bf16[2,4,3,384]{3,2,1,0:T(4,128)(2,1)S(1)}, bf16[2,4,3,384]{3,2,1,0:T(4,128)(2,1)S(1)}, u32[]{:S(2)}, u32[]{:S(2)}) %collective-permute-start.1) | collective-permute-done | bytes 18464 | tf_op jit(solution)/shard_map/ppermute | solution.py:19
  196.6 2.7 collective-permute-start.2
  199.4 2.8 collective-permute-start.3
  202.4 0.6 pad.18.w_ref
  203.1 0.7 pad_bitcast_fusion.w_ref
  203.8 4.4 %collective-permute-done.3 = bf16[2,3,30,384]{3,2,1,0:T(8,128)(2,1)S(1)} collective-permute-done((bf16[2,3,30,384]{3,2,1,0:T(8,128)(2,1)S(1)}, bf16[2,3,30,384]{3,2,1,0:T(8,128)(2,1)S(1)}, u32[]{:S(2)}, u32[]{:S(2)}) %collective-permute-start.3) | collective-permute-done | bytes 138272 | tf_op jit(solution)/shard_map/ppermute | solution.py:19
  208.6 1.4 compare_select_fusion.1
  210.0 3.8 %maximum_maximum_fusion.s0.s1.s2 = bf16[10,16,11520]{2,1,0:T(8,128)(2,1)} fusion(bf16[10,2,11520]{2,1,0:T(2,128)(2,1)S(1)} %get-tuple-element.20, bf16[10,2,11520]{2,1,0:T(2,128)(2,1)S(1)} %reshape.675, bf16[10,2,11520]{2,1,0:T(2,128)(2,1)S(1)} %get-tuple-element.19, bf16[16]{0:T(256)(128)(2,1)S(1)} %pad.23.clone), kind=kLoop, calls=%fused_computation | loop fusion | flops 14745600 | bytes 5068832 | tf_op jit(solution)/shard_map/concatenate | solution.py:107
  213.8 16.5 %shard_map.82.s0.s1.s2 = bf16[8,32,10752]{2,1,0:T(8,128)(2,1)} custom-call(bf16[10,16,11520]{2,1,0:T(8,128)(2,1)} %maximum_maximum_fusion.s0.s1.s2, bf16[10,16,11520]{2,1,0:T(8,128)(2,1)} %maximum_maximum_fusion.s0.s1.s2, bf16[10,16,11520]{2,1,0:T(8,128)(2,1)} %maximum_maximum_fusion.s0.s1.s2, bf16[3,3,32,16]{3,2,1,0:T(8,128)(2,1)} %pad.18.w_ref, ...), custom_call_target="tpu_custom_call" | custom-call | tf_op jit(solution)/shard_map/pallas_call | solution.py:86
  230.3 31.1 %shard_map.83.s0.s1.s2 = bf16[6,32,9984]{2,1,0:T(8,128)(2,1)} custom-call(bf16[8,32,10752]{2,1,0:T(8,128)(2,1)} %shard_map.82.s0.s1.s2, bf16[8,32,10752]{2,1,0:T(8,128)(2,1)} %shard_map.82.s0.s1.s2, bf16[8,32,10752]{2,1,0:T(8,128)(2,1)} %shard_map.82.s0.s1.s2, bf16[3,3,96,32]{3,2,1,0:T(8,128)(2,1)} %bitcast.288, f32[6,1,9984]{2,1,0:T(1,128)} %and_convert_fusion.1.refs_0_), custom_call_target="tpu_custom_call" | custom-call | tf_op jit(solution)/shard_map/pallas_call | solution.py:162
  261.3 8.9 %shard_map.84 = f32[4,8,9216]{2,1,0:T(8,128)} custom-call(bf16[6,32,9984]{2,1,0:T(8,128)(2,1)} %shard_map.83.s0.s1.s2, bf16[6,32,9984]{2,1,0:T(8,128)(2,1)} %shard_map.83.s0.s1.s2, bf16[6,32,9984]{2,1,0:T(8,128)(2,1)} %shard_map.83.s0.s1.s2, bf16[3,3,24,32]{3,2,1,0:T(8,128)(2,1)} %pad_bitcast_fusion.w_ref), custom_call_target="tpu_custom_call" | custom-call | tf_op jit(solution)/shard_map/pallas_call | solution.py:162
  270.2 1.3 slice.194
  271.5 0.2 reshape.679
  271.8 0.8 bitcast_add_fusion
  (59 shorter events, 1.6 us)
Async XLA Ops:
  6.5 33.0 %all-gather.2.cloned.1.call-start = ((), (), s32[]{:S(2)}) async-start(), calls=%async_computation.4 | async-start | bytes 1327104 | tf_op jit(solution)/shard_map/all_gather | solution.py:209
  41.4 1.2 copy-start.9
  41.4 1.2 copy-start.10
  45.3 8.3 %copy-start.13 = (s32[128,6]{0,1:T(8,128)S(1)}, s32[128,6]{0,1:T(8,128)}, u32[]{:S(2)}) copy-start(s32[128,6]{0,1:T(8,128)} %param.11) | copy-start | bytes 9220
  45.3 10.8 %copy-start = (bf16[2,1,4,192,384]{4,3,2,1,0:T(8,128)(2,1)S(1)}, bf16[2,1,4,192,384]{4,3,2,1,0:T(8,128)(2,1)}, u32[]{:S(2)}) copy-start(bf16[2,1,4,192,384]{4,3,2,1,0:T(8,128)(2,1)} %param.9) | copy-start | bytes 3538948
  45.3 24.3 %all-to-all-start = ((bf16[2,1,4,192,384]{4,2,0,1,3:T(4,128)(2,1)}), bf16[2,1,4,192,384]{4,2,0,1,3:T(4,128)(2,1)}, u32[]{:S(2)}, u32[]{:S(2)}) async-start(bf16[2,1,4,192,384]{4,2,0,1,3:T(4,128)(2,1)} %copy.72), calls=%async_computation | async-start | bytes 2359296 | tf_op jit(solution)/shard_map/all_to_all | solution.py:218
  75.3 1.9 copy-start.5
  75.3 1.9 copy-start.6
  79.9 6.7 %copy-start.14 = (pred[8]{0:T(512)(128)(4,1)S(1)}, pred[8]{0:T(512)(128)(4,1)}, u32[]{:S(2)}) copy-start(pred[8]{0:T(512)(128)(4,1)} %compare_and_fusion.3) | copy-start | bytes 28
  79.9 22.3 %all-to-all-start.1 = ((bf16[2,1,128,6,384]{4,0,3,1,2:T(2,128)(2,1)}), bf16[2,1,128,6,384]{4,0,3,1,2:T(2,128)(2,1)S(1)}, u32[]{:S(2)}, u32[]{:S(2)}) async-start(bf16[2,1,128,6,384]{4,0,3,1,2:T(2,128)(2,1)} %copy.77), calls=%async_computation.1 | async-start | bytes 2359296 | tf_op jit(solution)/shard_map/all_to_all | solution.py:225
  86.6 59.8 %reduce-scatter.7.cloned.1.call-start = ((), (), s32[]{:S(2)}) async-start(), calls=%async_computation.5 | async-start | bytes 663552
  102.7 1.7 copy-start.7
  102.7 1.7 copy-start.8
  104.4 1.1 copy-start.2
  104.4 1.2 copy-start.3
  107.3 1.3 copy-start.4
  108.6 76.5 %reduce-scatter.9.cloned.1.call-start = ((), (), s32[]{:S(2)}) async-start(), calls=%async_computation.6 | async-start | bytes 663552
  111.7 74.2 %copy-start.1 = (f32[2,4,24,384]{3,2,1,0:T(8,128)S(1)}, f32[2,4,24,384]{3,2,1,0:T(8,128)}, u32[]{:S(2)}) copy-start(f32[2,4,24,384]{3,2,1,0:T(8,128)} %param.8) | copy-start | bytes 884740
  113.9 88.3 %copy-start.11 = (bf16[3,3,32,3,2]{2,4,3,1,0:T(2,128)(2,1)S(1)}, bf16[3,3,32,3,2]{2,4,3,1,0:T(2,128)(2,1)}, u32[]{:S(2)}) copy-start(bf16[3,3,32,3,2]{2,4,3,1,0:T(2,128)(2,1)} %param.13) | copy-start | bytes 10372
  147.2 55.8 %copy-start.12 = (bf16[3,3,2,3,32]{4,2,3,1,0:T(2,128)(2,1)S(1)}, bf16[3,3,2,3,32]{4,2,3,1,0:T(2,128)(2,1)}, u32[]{:S(2)}) copy-start(bf16[3,3,2,3,32]{4,2,3,1,0:T(2,128)(2,1)} %param.15) | copy-start | bytes 10372
  186.1 5.2 %collective-permute-start = (bf16[2,4,3,384]{3,2,1,0:T(4,128)(2,1)S(1)}, bf16[2,4,3,384]{3,2,1,0:T(4,128)(2,1)S(1)}, u32[]{:S(2)}, u32[]{:S(2)}) collective-permute-start(bf16[2,4,3,384]{3,2,1,0:T(4,128)(2,1)S(1)} %get-tuple-element.29), channel_id=1, source_target_pairs={{0,32},{32,64},{64,96},{96,128},{128,160},{160,192},{192,224},{1,3... | collective-permute-start | bytes 55304 | tf_op jit(solution)/shard_map/ppermute | solution.py:16
  189.3 7.3 %collective-permute-start.1 = (bf16[2,4,3,384]{3,2,1,0:T(4,128)(2,1)S(1)}, bf16[2,4,3,384]{3,2,1,0:T(4,128)(2,1)S(1)}, u32[]{:S(2)}, u32[]{:S(2)}) collective-permute-start(bf16[2,4,3,384]{3,2,1,0:T(4,128)(2,1)S(1)} %get-tuple-element.30), channel_id=1, source_target_pairs={{32,0},{64,32},{96,64},{128,96},{160,128},{192,160},{224,192},{33,... | collective-permute-start | bytes 55304 | tf_op jit(solution)/shard_map/ppermute | solution.py:19
  196.6 7.2 %collective-permute-start.2 = (bf16[2,3,30,384]{3,2,1,0:T(8,128)(2,1)S(1)}, bf16[2,3,30,384]{3,2,1,0:T(8,128)(2,1)S(1)}, u32[]{:S(2)}, u32[]{:S(2)}) collective-permute-start(bf16[2,3,30,384]{3,2,1,0:T(8,128)(2,1)S(1)} %get-tuple-element.23), channel_id=1, source_target_pairs={{0,1},{1,2},{2,3},{3,4},{4,5},{5,6},{6,7},{7,8},{8,9},{9,10},{10,1... | collective-permute-start | bytes 414728 | tf_op jit(solution)/shard_map/ppermute | solution.py:16
  199.4 8.9 %collective-permute-start.3 = (bf16[2,3,30,384]{3,2,1,0:T(8,128)(2,1)S(1)}, bf16[2,3,30,384]{3,2,1,0:T(8,128)(2,1)S(1)}, u32[]{:S(2)}, u32[]{:S(2)}) collective-permute-start(bf16[2,3,30,384]{3,2,1,0:T(8,128)(2,1)S(1)} %get-tuple-element.24), channel_id=1, source_target_pairs={{1,0},{2,1},{3,2},{4,3},{5,4},{6,5},{7,6},{8,7},{9,8},{10,9},{11,1... | collective-permute-start | bytes 414728 | tf_op jit(solution)/shard_map/ppermute | solution.py:19
Sparse Core Ops, SparseCore 0:
  9.2 30.2 all-gather.1
  108.7 37.6 reduce-scatter.6
  148.9 36.1 reduce-scatter.8

commit v7 on v5

--- a/solution.py
+++ b/solution.py
@@ -236,10 +236,14 @@
     coil_first = lax.axis_index("coil") * coil_rows
     slab_first = lax.axis_index("slab") * slab_rows
     weights = (conv_first, conv_middle, conv_last)
-    scattered = lax.psum_scatter(
-        (-step_size * partial_value).astype(jnp.bfloat16), "coil", scatter_dimension=2, tiled=True
-    )
-    updated = image_field + scattered.astype(jnp.float32)
+    gathered = lax.all_to_all(
+        (-step_size * partial_value).astype(jnp.bfloat16), "coil", 2, 2, tiled=True
+    )
+    coils = lax.axis_size("coil")
+    scattered = jnp.sum(
+        gathered.astype(jnp.float32).reshape(2, slab_rows, coils, coil_rows, READ), axis=2
+    )
+    updated = image_field + scattered
     activations = padded_2(updated.astype(jnp.bfloat16), (("coil", 2),), 3)
     activations = padded_2(activations, (("slab", 1),), 3)
     depth, rows = activations.shape[1], activations.shape[2]

time: 243 us -> 242 us (level); the launches traced: 242 us -> 239 us
  waiting for transfers between devices: 97.8 us -> 85.2 us
  starting transfers between devices: 26.1 us -> 34.5 us
    unnamed x3 -> x1, waiting for transfers between devices: 38.6 us -> 0.02 us
    all_to_all x0 -> x1, waiting for transfers between devices: none -> 26.8 us  [per_device(): lax.all_to_all((-step_size * partial_value).astype(jnp.bfloat16), 'coil',...]
    all_to_all x0 -> x1, starting transfers between devices: none -> 7.62 us  [per_device(): lax.all_to_all((-step_size * partial_value).astype(jnp.bfloat16), 'coil',...]
    unnamed x30 -> x31, local copies, waits for them, and re-layouts: 6.58 us -> 2.68 us
  transfers between devices with their start and end apart: 8 -> 8, of which waited for: 7 -> 7; matrix products, arithmetic and copies ran while one was open for 6% -> 7% of each run, Pallas kernels for 0% -> 0%
where the time goes in v7:
time: 242 us; the launch traced here: 239 us
  waiting for transfers between devices  85.2 us (35%)
  Pallas kernels  56.4 us (23%)
  starting transfers between devices  34.5 us (14%)
  other arithmetic  24 us (10%)
  local copies, waits for them, and re-layouts  18 us (7%)
  between operations  14.5 us (6%)
  matrix products  6.2 us (3%)
    pallas_call x2, Pallas kernels, conv_roll(): pl.pallas_call(body, grid=(out_depth,), in_specs=in_specs, out_specs=pl.B...  39.9 us
    all_to_all x1, waiting for transfers between devices, per_device(): lax.all_to_all((-step_size * partial_value).astype(jnp.bfloat16), 'coil',...  26.8 us
    all_gather x1, waiting for transfers between devices, per_device(): lax.all_gather(pixels, 'coil', axis=2, tiled=True).astype(jnp.float32)  21.2 us
    pallas_call x1, Pallas kernels, conv_flat(): pl.pallas_call(body, grid=(out_depth,), in_specs=in_specs, out_specs=pl.B...  16.5 us
    all_to_all x1, waiting for transfers between devices, per_device(): lax.all_to_all(residual, 'slab', split_axis=2, concat_axis=3, tiled=True)  14.6 us
    all_to_all x1, waiting for transfers between devices, per_device(): lax.all_to_all(spectrum, 'slab', split_axis=3, concat_axis=2, tiled=True)  12.2 us
    ppermute x2, waiting for transfers between devices, padded_2(): lax.ppermute(lax.slice_in_dim(block, 0, width, axis=dim), axis, backward)  10.2 us
    all_to_all x1, starting transfers between devices, per_device(): lax.all_to_all(spectrum, 'slab', split_axis=3, concat_axis=2, tiled=True)  8.26 us
  transfers between devices with their start and end apart: 8, of which 7 were waited for; matrix products, arithmetic and copies ran while one was open for 7% of the time, Pallas kernels for 0%

profile of v7, /device:TPU:121, one launch (start us, length us, event | category | flops | bytes accessed | tf_op | source)
XLA Modules:
  0.0 238.8 jit_solution(4722931687182405103)
XLA Ops:
  6.5 1.6 copy.127
  8.2 1.4 convert_element_type.194
  9.6 0.8 fusion.84
  10.4 0.8 fusion.59
  11.2 2.3 fusion.58
  13.6 2.6 %fusion.43 = (bf16[384,1,384]{2,0,1:T(8,128)(2,1)S(1)}, bf16[384,1,384]{2,0,1:T(8,128)(2,1)S(1)}) fusion(), kind=kLoop, calls=%fused_computation.86 | loop fusion | flops 1916928 | bytes 589824 | tf_op jit(solution)/shard_map/stack;squeeze | solution.py:37
  16.2 0.9 fusion.47
  17.1 1.2 fusion.33
  18.3 21.2 %all-gather.2.cloned.1.call-done = bf16[2,4,192,384]{3,2,0,1:T(8,128)(2,1)} async-done(((bf16[2,4,24,384]{3,2,0,1:T(8,128)(2,1)}), bf16[2,4,192,384]{3,2,0,1:T(8,128)(2,1)}) %all-gather.2.cloned.1.call-update) | async-done | bytes 1179664 | tf_op jit(solution)/shard_map/all_gather | solution.py:209
  39.5 1.4 convert_element_type.200
  40.9 0.4 fusion.17
  41.4 1.1 fusion.7
  42.5 0.8 fusion.3
  43.4 2.0 copy.69
  45.3 8.3 %all-to-all-start = ((bf16[2,1,4,192,384]{4,2,0,1,3:T(4,128)(2,1)}), bf16[2,1,4,192,384]{4,2,0,1,3:T(4,128)(2,1)S(1)}, u32[]{:S(2)}, u32[]{:S(2)}) async-start(bf16[2,1,4,192,384]{4,2,0,1,3:T(4,128)(2,1)} %copy.69), calls=%async_computation | async-start | bytes 2359296 | tf_op jit(solution)/shard_map/all_to_all | solution.py:218
  54.3 0.6 compare_and_fusion.3
  54.9 0.6 compare_and_fusion.2
  55.4 0.3 fusion.87
  55.7 0.3 fusion.85
  56.0 0.7 fusion.64
  56.7 0.6 compare_and_fusion.1
  57.4 12.2 %all-to-all-done = bf16[2,1,4,192,384]{4,2,0,1,3:T(4,128)(2,1)S(1)} async-done(((bf16[2,1,4,192,384]{4,2,0,1,3:T(4,128)(2,1)}), bf16[2,1,4,192,384]{4,2,0,1,3:T(4,128)(2,1)S(1)}, u32[]{:S(2)}, u32[]{:S(2)}) %all-to-all-start) | async-done | bytes 1179680 | tf_op jit(solution)/shard_map/all_to_all | solution.py:218
  69.5 0.4 copy.70
  70.0 1.6 copy.71
  71.5 2.4 reshape.574
  73.9 1.9 fusion.9
  75.8 0.5 fusion.6
  76.3 2.3 copy.74
  78.6 6.8 %all-to-all-start.1 = ((bf16[2,1,128,6,384]{4,0,3,1,2:T(2,128)(2,1)}), bf16[2,1,128,6,384]{4,0,3,1,2:T(2,128)(2,1)S(1)}, u32[]{:S(2)}, u32[]{:S(2)}) async-start(bf16[2,1,128,6,384]{4,0,3,1,2:T(2,128)(2,1)} %copy.74), calls=%async_computation.1 | async-start | bytes 2359296 | tf_op jit(solution)/shard_map/all_to_all | solution.py:225
  85.4 1.0 and_convert_fusion.refs_0_
  86.4 14.6 %all-to-all-done.1 = bf16[2,1,128,6,384]{4,0,3,1,2:T(2,128)(2,1)S(1)} async-done(((bf16[2,1,128,6,384]{4,0,3,1,2:T(2,128)(2,1)}), bf16[2,1,128,6,384]{4,0,3,1,2:T(2,128)(2,1)S(1)}, u32[]{:S(2)}, u32[]{:S(2)}) %all-to-all-start.1) | async-done | bytes 1179680 | tf_op jit(solution)/shard_map/all_to_all | solution.py:225
  101.0 0.5 copy.75
  101.5 0.5 copy-done.5
  102.1 0.8 fusion.4
  102.9 0.3 copy-done.1
  103.1 0.2 copy-done.2
  103.3 1.1 convert_bitcast_fusion
  104.4 0.3 fusion.20
  104.7 0.2 fusion
  105.0 2.3 copy.82
  107.2 7.6 %all-to-all-start.2 = ((bf16[2,4,192,384]{3,0,1,2:T(2,128)(2,1)}), bf16[2,4,192,384]{3,0,1,2:T(2,128)(2,1)S(1)}, u32[]{:S(2)}, u32[]{:S(2)}) async-start(bf16[2,4,192,384]{3,0,1,2:T(2,128)(2,1)} %copy.82), calls=%async_computation.2 | async-start | bytes 2359296 | tf_op jit(solution)/shard_map/all_to_all | solution.py:239
  114.9 0.9 and_convert_fusion.1.refs_0_
  115.8 26.8 %all-to-all-done.2 = bf16[2,4,192,384]{3,0,1,2:T(2,128)(2,1)S(1)} async-done(((bf16[2,4,192,384]{3,0,1,2:T(2,128)(2,1)}), bf16[2,4,192,384]{3,0,1,2:T(2,128)(2,1)S(1)}, u32[]{:S(2)}, u32[]{:S(2)}) %all-to-all-start.2) | async-done | bytes 1179680 | tf_op jit(solution)/shard_map/all_to_all | solution.py:239
  142.6 1.0 convert_reduce_fusion
  143.8 4.6 %collective-permute-start = (bf16[2,4,3,384]{3,2,0,1:T(4,128)(2,1)S(1)}, bf16[2,4,3,384]{3,2,0,1:T(4,128)(2,1)S(1)}, u32[]{:S(2)}, u32[]{:S(2)}) collective-permute-start(bf16[2,4,3,384]{3,2,0,1:T(4,128)(2,1)S(1)} %get-tuple-element.23), channel_id=1, source_target_pairs={{0,32},{32,64},{64,96},{96,128},{128,160},{160,192},{192,224},{1,3... | collective-permute-start | bytes 55304 | tf_op jit(solution)/shard_map/ppermute | solution.py:16
  148.4 1.9 collective-permute-start.1
  150.4 5.3 %collective-permute-done.1 = bf16[2,4,3,384]{3,2,0,1:T(4,128)(2,1)S(1)} collective-permute-done((bf16[2,4,3,384]{3,2,0,1:T(4,128)(2,1)S(1)}, bf16[2,4,3,384]{3,2,0,1:T(4,128)(2,1)S(1)}, u32[]{:S(2)}, u32[]{:S(2)}) %collective-permute-start.1) | collective-permute-done | bytes 18464 | tf_op jit(solution)/shard_map/ppermute | solution.py:19
  155.8 2.2 collective-permute-start.2
  158.0 3.1 %collective-permute-start.3 = (bf16[2,3,30,384]{3,2,0,1:T(8,128)(2,1)S(1)}, bf16[2,3,30,384]{3,2,0,1:T(8,128)(2,1)S(1)}, u32[]{:S(2)}, u32[]{:S(2)}) collective-permute-start(bf16[2,3,30,384]{3,2,0,1:T(8,128)(2,1)S(1)} %get-tuple-element.18), channel_id=1, source_target_pairs={{1,0},{2,1},{3,2},{4,3},{5,4},{6,5},{7,6},{8,7},{9,8},{10,9},{11,1... | collective-permute-start | bytes 414728 | tf_op jit(solution)/shard_map/ppermute | solution.py:19
  161.1 0.1 copy.85
  161.3 0.6 pad.18.w_ref
  162.0 0.6 pad_bitcast_fusion.w_ref
  162.7 0.1 collective-permute-done.2
  162.8 4.9 %collective-permute-done.3 = bf16[2,3,30,384]{3,2,0,1:T(8,128)(2,1)S(1)} collective-permute-done((bf16[2,3,30,384]{3,2,0,1:T(8,128)(2,1)S(1)}, bf16[2,3,30,384]{3,2,0,1:T(8,128)(2,1)S(1)}, u32[]{:S(2)}, u32[]{:S(2)}) %collective-permute-start.3) | collective-permute-done | bytes 138272 | tf_op jit(solution)/shard_map/ppermute | solution.py:19
  167.7 0.1 maximum_bitcast_fusion.6
  167.8 0.2 reshape.558
  168.0 1.4 compare_select_fusion.1
  169.4 3.7 %maximum_maximum_fusion.s0.s1.s2 = bf16[10,16,11520]{2,1,0:T(8,128)(2,1)} fusion(bf16[10,2,11520]{2,1,0:T(2,128)(2,1)S(1)} %get-tuple-element.14, bf16[10,2,11520]{2,1,0:T(2,128)(2,1)S(1)} %reshape.558, bf16[10,2,11520]{2,1,0:T(2,128)(2,1)S(1)} %get-tuple-element.13, bf16[16]{0:T(256)(128)(2,1)S(1)} %pad.23.clone), kind=kLoop, calls=%fused_computation | loop fusion | flops 14745600 | bytes 5068832 | tf_op jit(solution)/shard_map/concatenate | solution.py:107
  173.1 16.5 %shard_map.82.s0.s1.s2 = bf16[8,32,10752]{2,1,0:T(8,128)(2,1)} custom-call(bf16[10,16,11520]{2,1,0:T(8,128)(2,1)} %maximum_maximum_fusion.s0.s1.s2, bf16[10,16,11520]{2,1,0:T(8,128)(2,1)} %maximum_maximum_fusion.s0.s1.s2, bf16[10,16,11520]{2,1,0:T(8,128)(2,1)} %maximum_maximum_fusion.s0.s1.s2, bf16[3,3,32,16]{3,2,1,0:T(8,128)(2,1)} %pad.18.w_ref, ...), custom_call_target="tpu_custom_call" | custom-call | tf_op jit(solution)/shard_map/pallas_call | solution.py:86
  189.6 31.0 %shard_map.83.s0.s1.s2 = bf16[6,32,9984]{2,1,0:T(8,128)(2,1)} custom-call(bf16[8,32,10752]{2,1,0:T(8,128)(2,1)} %shard_map.82.s0.s1.s2, bf16[8,32,10752]{2,1,0:T(8,128)(2,1)} %shard_map.82.s0.s1.s2, bf16[8,32,10752]{2,1,0:T(8,128)(2,1)} %shard_map.82.s0.s1.s2, bf16[3,3,96,32]{3,2,1,0:T(8,128)(2,1)} %bitcast.244, f32[6,1,9984]{2,1,0:T(1,128)} %and_convert_fusion.1.refs_0_), custom_call_target="tpu_custom_call" | custom-call | tf_op jit(solution)/shard_map/pallas_call | solution.py:162
  220.6 8.9 %shard_map.84 = f32[4,8,9216]{2,1,0:T(8,128)} custom-call(bf16[6,32,9984]{2,1,0:T(8,128)(2,1)} %shard_map.83.s0.s1.s2, bf16[6,32,9984]{2,1,0:T(8,128)(2,1)} %shard_map.83.s0.s1.s2, bf16[6,32,9984]{2,1,0:T(8,128)(2,1)} %shard_map.83.s0.s1.s2, bf16[3,3,24,32]{3,2,1,0:T(8,128)(2,1)} %pad_bitcast_fusion.w_ref), custom_call_target="tpu_custom_call" | custom-call | tf_op jit(solution)/shard_map/pallas_call | solution.py:162
  229.5 1.3 slice.140
  230.8 0.2 reshape.562
  231.2 0.7 copy.86
  (42 shorter events, 0.6 us)
Async XLA Ops:
  6.5 33.0 %all-gather.2.cloned.1.call-start = ((), (), s32[]{:S(2)}) async-start(), calls=%async_computation.3 | async-start | bytes 1327104 | tf_op jit(solution)/shard_map/all_gather | solution.py:209
  41.4 1.2 copy-start.7
  41.4 1.2 copy-start.8
  45.3 8.3 %copy-start.12 = (s32[128,6]{0,1:T(8,128)S(1)}, s32[128,6]{0,1:T(8,128)}, u32[]{:S(2)}) copy-start(s32[128,6]{0,1:T(8,128)} %param.11) | copy-start | bytes 9220
  45.3 24.2 %all-to-all-start = ((bf16[2,1,4,192,384]{4,2,0,1,3:T(4,128)(2,1)}), bf16[2,1,4,192,384]{4,2,0,1,3:T(4,128)(2,1)S(1)}, u32[]{:S(2)}, u32[]{:S(2)}) async-start(bf16[2,1,4,192,384]{4,2,0,1,3:T(4,128)(2,1)} %copy.69), calls=%async_computation | async-start | bytes 2359296 | tf_op jit(solution)/shard_map/all_to_all | solution.py:218
  73.9 1.9 copy-start.3
  73.9 1.9 copy-start.4
  78.6 6.8 %copy-start.14 = (pred[8]{0:T(512)(128)(4,1)S(1)}, pred[8]{0:T(512)(128)(4,1)}, u32[]{:S(2)}) copy-start(pred[8]{0:T(512)(128)(4,1)} %compare_and_fusion.3) | copy-start | bytes 28
  78.6 22.5 %all-to-all-start.1 = ((bf16[2,1,128,6,384]{4,0,3,1,2:T(2,128)(2,1)}), bf16[2,1,128,6,384]{4,0,3,1,2:T(2,128)(2,1)S(1)}, u32[]{:S(2)}, u32[]{:S(2)}) async-start(bf16[2,1,128,6,384]{4,0,3,1,2:T(2,128)(2,1)} %copy.74), calls=%async_computation.1 | async-start | bytes 2359296 | tf_op jit(solution)/shard_map/all_to_all | solution.py:225
  101.0 0.9 copy-start.5
  101.0 1.0 copy-start.6
  102.1 1.1 copy-start.1
  102.1 1.2 copy-start.2
  107.2 7.6 %copy-start.9 = (pred[9984]{0:T(1024)(128)(4,1)S(1)}, pred[9984]{0:T(1024)(128)(4,1)}, u32[]{:S(2)}) copy-start(pred[9984]{0:T(1024)(128)(4,1)} %compare_and_fusion.1) | copy-start | bytes 29956
  107.2 7.6 %copy-start.13 = (pred[6]{0:T(512)(128)(4,1)S(1)}, pred[6]{0:T(512)(128)(4,1)}, u32[]{:S(2)}) copy-start(pred[6]{0:T(512)(128)(4,1)} %compare_and_fusion.2) | copy-start | bytes 22
  107.2 35.4 %all-to-all-start.2 = ((bf16[2,4,192,384]{3,0,1,2:T(2,128)(2,1)}), bf16[2,4,192,384]{3,0,1,2:T(2,128)(2,1)S(1)}, u32[]{:S(2)}, u32[]{:S(2)}) async-start(bf16[2,4,192,384]{3,0,1,2:T(2,128)(2,1)} %copy.82), calls=%async_computation.2 | async-start | bytes 2359296 | tf_op jit(solution)/shard_map/all_to_all | solution.py:239
  114.9 28.8 %copy-start = (f32[2,4,24,384]{3,2,1,0:T(8,128)S(1)}, f32[2,4,24,384]{3,2,1,0:T(8,128)}, u32[]{:S(2)}) copy-start(f32[2,4,24,384]{3,2,1,0:T(8,128)} %param.8) | copy-start | bytes 884740
  143.6 17.5 %copy-start.10 = (bf16[3,3,32,3,2]{2,4,3,1,0:T(2,128)(2,1)S(1)}, bf16[3,3,32,3,2]{2,4,3,1,0:T(2,128)(2,1)}, u32[]{:S(2)}) copy-start(bf16[3,3,32,3,2]{2,4,3,1,0:T(2,128)(2,1)} %param.13) | copy-start | bytes 10372
  143.6 18.4 %copy-start.11 = (bf16[3,3,2,3,32]{4,2,3,1,0:T(2,128)(2,1)S(1)}, bf16[3,3,2,3,32]{4,2,3,1,0:T(2,128)(2,1)}, u32[]{:S(2)}) copy-start(bf16[3,3,2,3,32]{4,2,3,1,0:T(2,128)(2,1)} %param.15) | copy-start | bytes 10372
  143.8 6.6 %collective-permute-start = (bf16[2,4,3,384]{3,2,0,1:T(4,128)(2,1)S(1)}, bf16[2,4,3,384]{3,2,0,1:T(4,128)(2,1)S(1)}, u32[]{:S(2)}, u32[]{:S(2)}) collective-permute-start(bf16[2,4,3,384]{3,2,0,1:T(4,128)(2,1)S(1)} %get-tuple-element.23), channel_id=1, source_target_pairs={{0,32},{32,64},{64,96},{96,128},{128,160},{160,192},{192,224},{1,3... | collective-permute-start | bytes 55304 | tf_op jit(solution)/shard_map/ppermute | solution.py:16
  148.4 7.3 %collective-permute-start.1 = (bf16[2,4,3,384]{3,2,0,1:T(4,128)(2,1)S(1)}, bf16[2,4,3,384]{3,2,0,1:T(4,128)(2,1)S(1)}, u32[]{:S(2)}, u32[]{:S(2)}) collective-permute-start(bf16[2,4,3,384]{3,2,0,1:T(4,128)(2,1)S(1)} %get-tuple-element.24), channel_id=1, source_target_pairs={{32,0},{64,32},{96,64},{128,96},{160,128},{192,160},{224,192},{33,... | collective-permute-start | bytes 55304 | tf_op jit(solution)/shard_map/ppermute | solution.py:19
  155.8 7.0 %collective-permute-start.2 = (bf16[2,3,30,384]{3,2,0,1:T(8,128)(2,1)S(1)}, bf16[2,3,30,384]{3,2,0,1:T(8,128)(2,1)S(1)}, u32[]{:S(2)}, u32[]{:S(2)}) collective-permute-start(bf16[2,3,30,384]{3,2,0,1:T(8,128)(2,1)S(1)} %get-tuple-element.17), channel_id=1, source_target_pairs={{0,1},{1,2},{2,3},{3,4},{4,5},{5,6},{6,7},{7,8},{8,9},{9,10},{10,1... | collective-permute-start | bytes 414728 | tf_op jit(solution)/shard_map/ppermute | solution.py:16
  158.0 9.7 %collective-permute-start.3 = (bf16[2,3,30,384]{3,2,0,1:T(8,128)(2,1)S(1)}, bf16[2,3,30,384]{3,2,0,1:T(8,128)(2,1)S(1)}, u32[]{:S(2)}, u32[]{:S(2)}) collective-permute-start(bf16[2,3,30,384]{3,2,0,1:T(8,128)(2,1)S(1)} %get-tuple-element.18), channel_id=1, source_target_pairs={{1,0},{2,1},{3,2},{4,3},{5,4},{6,5},{7,6},{8,7},{9,8},{10,9},{11,1... | collective-permute-start | bytes 414728 | tf_op jit(solution)/shard_map/ppermute | solution.py:19
Sparse Core Ops, SparseCore 0:
  9.2 30.2 all-gather.1

commit v8 on v7

--- a/solution.py
+++ b/solution.py
@@ -45,14 +45,20 @@
 READ = 384
 CHUNK = 1536
 
-def finish(total, refs, start, size):
+def finish(total, refs, start, size, spread):
     if len(refs) == 1:
         return total
     keep = refs[0][0, :, pl.ds(start, size)] > 0
-    return jnp.where(keep, jnp.maximum(total, 0.0), 0.0).astype(jnp.bfloat16)
-
-
-def conv_flat(stack, kernel, out_rows, inside=None):
+    kept = jnp.where(keep, jnp.maximum(total, 0.0), 0.0)
+    if not spread:
+        return kept.astype(jnp.bfloat16)
+    place = lax.broadcasted_iota(jnp.int32, kept.shape, 1) % READ
+    left = jnp.where(place == 0, 0.0, pltpu.roll(kept, 1, 1))
+    right = jnp.where(place == READ - 1, 0.0, pltpu.roll(kept, size - 1, 1))
+    return jnp.concatenate([left, kept, right], axis=0).astype(jnp.bfloat16)
+
+
+def conv_flat(stack, kernel, out_rows, inside=None, spread=False):
     depth_in, width, lanes_in = stack.shape
     out_depth = depth_in - 2
     out_channels = kernel.shape[2]
@@ -72,13 +78,14 @@
                         sources[dz][0, :, pl.ds(start + dy * READ, size)],
                         preferred_element_type=jnp.float32,
                     )
-            o_ref[0, :, pl.ds(start, size)] = finish(acc, refs, start, size)
+            o_ref[0, :, pl.ds(start, size)] = finish(acc, refs, start, size, spread)
 
     in_specs = [
         pl.BlockSpec((1, width, lanes_in), lambda z, dz=dz: (z + dz, 0, 0)) for dz in range(3)
     ] + [pl.BlockSpec(kernel.shape, lambda z: (0, 0, 0, 0))]
     extra = ()
     kind = jnp.float32
+    stored = 3 * out_channels if spread else out_channels
     if inside is not None:
         in_specs.append(pl.BlockSpec((1, 1, lanes), lambda z: (z, 0, 0)))
         extra = (inside,)
@@ -87,8 +94,8 @@
         body,
         grid=(out_depth,),
         in_specs=in_specs,
-        out_specs=pl.BlockSpec((1, out_channels, lanes), lambda z: (z, 0, 0)),
-        out_shape=jax.ShapeDtypeStruct((out_depth, out_channels, lanes), kind),
+        out_specs=pl.BlockSpec((1, stored, lanes), lambda z: (z, 0, 0)),
+        out_shape=jax.ShapeDtypeStruct((out_depth, stored, lanes), kind),
     )(stack, stack, stack, kernel, *extra)
 
 
@@ -148,7 +155,7 @@
                 + jnp.where(place == 0, 0.0, left)
                 + jnp.where(place == READ - 1, 0.0, right)
             )
-            o_ref[0, :, pl.ds(start, size)] = finish(total, refs, start, size)
+            o_ref[0, :, pl.ds(start, size)] = finish(total, refs, start, size, False)
 
     in_specs = [
         pl.BlockSpec((1, width, lanes_in), lambda z, dz=dz: (z + dz, 0, 0)) for dz in range(3)
@@ -261,7 +268,11 @@
             ).astype(jnp.float32)
         depth = depth - 2
         if layer_index == 0:
-            output = convolve_flat(activations, weight, rows, inside)
+            output = conv_flat(
+                shifted_stack(activations), kernel_matrix(weight), rows, inside, spread=True
+            )
+        elif layer_index == 1:
+            output = conv_flat(activations, kernel_matrix(weight), rows, inside)
         else:
             output = convolve_roll(activations, weight, rows, inside)
         activations = output

time: 242 us -> 234 us (0.967)
  Pallas kernels: 56.4 us -> 48.4 us
    pallas_call x2 -> x1, Pallas kernels: 39.9 us -> 8.88 us  [conv_roll(): pl.pallas_call(body, grid=(out_depth,), in_specs=in_specs, out_specs=pl.B...]
    pallas_call x1 -> x2, Pallas kernels: 16.5 us -> 39.5 us  [conv_flat(): pl.pallas_call(body, grid=(out_depth,), in_specs=in_specs, out_specs=pl.B...]
  transfers between devices with their start and end apart: 8 -> 8, of which waited for: 7 -> 6; matrix products, arithmetic and copies ran while one was open for 7% -> 8% of each run, Pallas kernels for 0% -> 0%
where the time goes in v8:
time: 234 us; the launch traced here: 231 us
  waiting for transfers between devices  84.3 us (36%)
  Pallas kernels  48.4 us (21%)
  starting transfers between devices  34.5 us (15%)
  other arithmetic  23.8 us (10%)
  local copies, waits for them, and re-layouts  19 us (8%)
  between operations  14.5 us (6%)
  matrix products  6.22 us (3%)
    pallas_call x2, Pallas kernels, conv_flat(): pl.pallas_call(body, grid=(out_depth,), in_specs=in_specs, out_specs=pl.B...  39.5 us
    all_to_all x1, waiting for transfers between devices, per_device(): lax.all_to_all((-step_size * partial_value).astype(jnp.bfloat16), 'coil',...  26.8 us
    all_gather x1, waiting for transfers between devices, per_device(): lax.all_gather(pixels, 'coil', axis=2, tiled=True).astype(jnp.float32)  21.2 us
    all_to_all x1, waiting for transfers between devices, per_device(): lax.all_to_all(residual, 'slab', split_axis=2, concat_axis=3, tiled=True)  14.6 us
    all_to_all x1, waiting for transfers between devices, per_device(): lax.all_to_all(spectrum, 'slab', split_axis=3, concat_axis=2, tiled=True)  12.3 us
    ppermute x2, waiting for transfers between devices, padded_2(): lax.ppermute(lax.slice_in_dim(block, 0, width, axis=dim), axis, backward)  9.32 us
    pallas_call x1, Pallas kernels, conv_roll(): pl.pallas_call(body, grid=(out_depth,), in_specs=in_specs, out_specs=pl.B...  8.88 us
    all_to_all x1, starting transfers between devices, per_device(): lax.all_to_all(spectrum, 'slab', split_axis=3, concat_axis=2, tiled=True)  8.26 us
  transfers between devices with their start and end apart: 8, of which 6 were waited for; matrix products, arithmetic and copies ran while one was open for 8% of the time, Pallas kernels for 0%

profile of v8, /device:TPU:121, one launch (start us, length us, event | category | flops | bytes accessed | tf_op | source)
XLA Modules:
  0.0 230.7 jit_solution(9695930430494754891)
XLA Ops:
  6.5 1.6 copy.131
  8.2 1.4 convert_element_type.194
  9.6 0.8 fusion.84
  10.4 0.8 fusion.59
  11.2 2.3 %fusion.58 = bf16[384,1,384]{2,0,1:T(8,128)(2,1)S(1)} fusion(), kind=kLoop, calls=%fused_computation.114 | loop fusion | flops 2064384 | bytes 294912 | tf_op jit(solution)/shard_map/neg | solution.py:36
  13.6 2.6 %fusion.43 = (bf16[384,1,384]{2,0,1:T(8,128)(2,1)S(1)}, bf16[384,1,384]{2,0,1:T(8,128)(2,1)S(1)}) fusion(), kind=kLoop, calls=%fused_computation.86 | loop fusion | flops 1916928 | bytes 589824 | tf_op jit(solution)/shard_map/stack;squeeze | solution.py:37
  16.2 0.9 fusion.47
  17.1 1.2 fusion.33
  18.3 21.2 %all-gather.2.cloned.1.call-done = bf16[2,4,192,384]{3,2,0,1:T(8,128)(2,1)} async-done(((bf16[2,4,24,384]{3,2,0,1:T(8,128)(2,1)}), bf16[2,4,192,384]{3,2,0,1:T(8,128)(2,1)}) %all-gather.2.cloned.1.call-update) | async-done | bytes 1179664 | tf_op jit(solution)/shard_map/all_gather | solution.py:216
  39.5 1.4 convert_element_type.200
  40.9 0.4 fusion.17
  41.4 1.1 fusion.7
  42.5 0.8 fusion.3
  43.4 2.0 copy.72
  45.3 8.3 %all-to-all-start = ((bf16[2,1,4,192,384]{4,2,0,1,3:T(4,128)(2,1)}), bf16[2,1,4,192,384]{4,2,0,1,3:T(4,128)(2,1)S(1)}, u32[]{:S(2)}, u32[]{:S(2)}) async-start(bf16[2,1,4,192,384]{4,2,0,1,3:T(4,128)(2,1)} %copy.72), calls=%async_computation | async-start | bytes 2359296 | tf_op jit(solution)/shard_map/all_to_all | solution.py:225
  54.3 0.6 compare_and_fusion.3
  54.9 0.5 compare_and_fusion.2
  55.4 0.3 fusion.87
  55.6 0.3 fusion.85
  55.9 0.7 fusion.64
  56.7 0.6 compare_and_fusion.1
  57.3 12.3 %all-to-all-done = bf16[2,1,4,192,384]{4,2,0,1,3:T(4,128)(2,1)S(1)} async-done(((bf16[2,1,4,192,384]{4,2,0,1,3:T(4,128)(2,1)}), bf16[2,1,4,192,384]{4,2,0,1,3:T(4,128)(2,1)S(1)}, u32[]{:S(2)}, u32[]{:S(2)}) %all-to-all-start) | async-done | bytes 1179680 | tf_op jit(solution)/shard_map/all_to_all | solution.py:225
  69.6 0.4 copy.73
  70.0 1.6 copy.74
  71.5 2.4 %reshape.574 = bf16[2,128,6,384,1]{3,1,0,2,4:T(8,128)(2,1)S(1)} reshape(bf16[2,1,32,4,6,384]{5,3,2,0,4,1:T(4,128)(2,1)} %copy.74) | data formatting | bytes 2359296 | tf_op jit(solution)/shard_map/reshape.18
  74.0 1.9 fusion.9
  75.8 0.5 fusion.6
  76.3 2.3 copy.77
  78.6 6.8 %all-to-all-start.1 = ((bf16[2,1,128,6,384]{4,0,3,1,2:T(2,128)(2,1)}), bf16[2,1,128,6,384]{4,0,3,1,2:T(2,128)(2,1)S(1)}, u32[]{:S(2)}, u32[]{:S(2)}) async-start(bf16[2,1,128,6,384]{4,0,3,1,2:T(2,128)(2,1)} %copy.77), calls=%async_computation.1 | async-start | bytes 2359296 | tf_op jit(solution)/shard_map/all_to_all | solution.py:232
  85.4 1.0 and_convert_fusion.refs_0_
  86.4 14.6 %all-to-all-done.1 = bf16[2,1,128,6,384]{4,0,3,1,2:T(2,128)(2,1)S(1)} async-done(((bf16[2,1,128,6,384]{4,0,3,1,2:T(2,128)(2,1)}), bf16[2,1,128,6,384]{4,0,3,1,2:T(2,128)(2,1)S(1)}, u32[]{:S(2)}, u32[]{:S(2)}) %all-to-all-start.1) | async-done | bytes 1179680 | tf_op jit(solution)/shard_map/all_to_all | solution.py:232
  101.1 0.5 copy.78
  101.5 0.5 copy-done.6
  102.1 0.8 fusion.4
  102.9 0.2 copy-done.1
  103.2 0.2 copy-done.2
  103.3 1.1 convert_bitcast_fusion
  104.5 0.3 fusion.20
  104.8 0.2 fusion
  105.0 2.3 copy.85
  107.3 7.6 %all-to-all-start.2 = ((bf16[2,4,192,384]{3,0,1,2:T(2,128)(2,1)}), bf16[2,4,192,384]{3,0,1,2:T(2,128)(2,1)S(1)}, u32[]{:S(2)}, u32[]{:S(2)}) async-start(bf16[2,4,192,384]{3,0,1,2:T(2,128)(2,1)} %copy.85), calls=%async_computation.2 | async-start | bytes 2359296 | tf_op jit(solution)/shard_map/all_to_all | solution.py:246
  114.9 0.9 and_convert_fusion.1.refs_0_
  115.8 26.8 %all-to-all-done.2 = bf16[2,4,192,384]{3,0,1,2:T(2,128)(2,1)S(1)} async-done(((bf16[2,4,192,384]{3,0,1,2:T(2,128)(2,1)}), bf16[2,4,192,384]{3,0,1,2:T(2,128)(2,1)S(1)}, u32[]{:S(2)}, u32[]{:S(2)}) %all-to-all-start.2) | async-done | bytes 1179680 | tf_op jit(solution)/shard_map/all_to_all | solution.py:246
  142.7 1.0 convert_reduce_fusion
  143.8 4.6 %collective-permute-start = (bf16[2,4,3,384]{3,2,0,1:T(4,128)(2,1)S(1)}, bf16[2,4,3,384]{3,2,0,1:T(4,128)(2,1)S(1)}, u32[]{:S(2)}, u32[]{:S(2)}) collective-permute-start(bf16[2,4,3,384]{3,2,0,1:T(4,128)(2,1)S(1)} %get-tuple-element.23), channel_id=1, source_target_pairs={{0,32},{32,64},{64,96},{96,128},{128,160},{160,192},{192,224},{1,3... | collective-permute-start | bytes 55304 | tf_op jit(solution)/shard_map/ppermute | solution.py:16
  148.5 1.9 collective-permute-start.1
  150.4 5.3 %collective-permute-done.1 = bf16[2,4,3,384]{3,2,0,1:T(4,128)(2,1)S(1)} collective-permute-done((bf16[2,4,3,384]{3,2,0,1:T(4,128)(2,1)S(1)}, bf16[2,4,3,384]{3,2,0,1:T(4,128)(2,1)S(1)}, u32[]{:S(2)}, u32[]{:S(2)}) %collective-permute-start.1) | collective-permute-done | bytes 18464 | tf_op jit(solution)/shard_map/ppermute | solution.py:19
  155.8 2.2 collective-permute-start.2
  158.0 3.1 %collective-permute-start.3 = (bf16[2,3,30,384]{3,2,0,1:T(8,128)(2,1)S(1)}, bf16[2,3,30,384]{3,2,0,1:T(8,128)(2,1)S(1)}, u32[]{:S(2)}, u32[]{:S(2)}) collective-permute-start(bf16[2,3,30,384]{3,2,0,1:T(8,128)(2,1)S(1)} %get-tuple-element.18), channel_id=1, source_target_pairs={{1,0},{2,1},{3,2},{4,3},{5,4},{6,5},{7,6},{8,7},{9,8},{10,9},{11,1... | collective-permute-start | bytes 414728 | tf_op jit(solution)/shard_map/ppermute | solution.py:19
  161.2 0.1 copy.88
  161.4 0.2 copy.89
  161.5 0.8 reshape.560.w_ref
  162.3 0.7 pad.18.w_ref
  163.1 0.6 pad_bitcast_fusion.w_ref
  163.7 4.0 %collective-permute-done.3 = bf16[2,3,30,384]{3,2,0,1:T(8,128)(2,1)S(1)} collective-permute-done((bf16[2,3,30,384]{3,2,0,1:T(8,128)(2,1)S(1)}, bf16[2,3,30,384]{3,2,0,1:T(8,128)(2,1)S(1)}, u32[]{:S(2)}, u32[]{:S(2)}) %collective-permute-start.3) | collective-permute-done | bytes 138272 | tf_op jit(solution)/shard_map/ppermute | solution.py:19
  167.8 0.2 reshape.558
  168.0 1.4 compare_select_fusion.1
  169.4 3.6 %maximum_maximum_fusion.s0.s1.s2 = bf16[10,16,11520]{2,1,0:T(8,128)(2,1)} fusion(bf16[10,2,11520]{2,1,0:T(2,128)(2,1)S(1)} %get-tuple-element.14, bf16[10,2,11520]{2,1,0:T(2,128)(2,1)S(1)} %reshape.558, bf16[10,2,11520]{2,1,0:T(2,128)(2,1)S(1)} %get-tuple-element.13, bf16[16]{0:T(256)(128)(2,1)S(1)} %pad.23.clone), kind=kLoop, calls=%fused_computation | loop fusion | flops 14745600 | bytes 5068832 | tf_op jit(solution)/shard_map/concatenate | solution.py:114
  173.1 17.9 %shard_map.82.s0.s1.s2 = bf16[8,96,10752]{2,1,0:T(8,128)(2,1)} custom-call(bf16[10,16,11520]{2,1,0:T(8,128)(2,1)} %maximum_maximum_fusion.s0.s1.s2, bf16[10,16,11520]{2,1,0:T(8,128)(2,1)} %maximum_maximum_fusion.s0.s1.s2, bf16[10,16,11520]{2,1,0:T(8,128)(2,1)} %maximum_maximum_fusion.s0.s1.s2, bf16[3,3,32,16]{3,2,1,0:T(8,128)(2,1)} %pad.18.w_ref, ...), custom_call_target="tpu_custom_call" | custom-call | tf_op jit(solution)/shard_map/pallas_call | solution.py:93
  190.9 21.6 %shard_map.83.s0.s1.s2 = bf16[6,32,9984]{2,1,0:T(8,128)(2,1)} custom-call(bf16[8,96,10752]{2,1,0:T(8,128)(2,1)} %shard_map.82.s0.s1.s2, bf16[8,96,10752]{2,1,0:T(8,128)(2,1)} %shard_map.82.s0.s1.s2, bf16[8,96,10752]{2,1,0:T(8,128)(2,1)} %shard_map.82.s0.s1.s2, bf16[3,3,32,96]{3,2,1,0:T(8,128)(2,1)} %reshape.560.w_ref, f32[6,1,9984]{2,1,0:T(1,128)} %and_convert_fusion.1.refs_0_), custom_call_target="tpu_custom_call" | custom-call | tf_op jit(solution)/shard_map/pallas_call | solution.py:93
  212.6 8.9 %shard_map.84 = f32[4,8,9216]{2,1,0:T(8,128)} custom-call(bf16[6,32,9984]{2,1,0:T(8,128)(2,1)} %shard_map.83.s0.s1.s2, bf16[6,32,9984]{2,1,0:T(8,128)(2,1)} %shard_map.83.s0.s1.s2, bf16[6,32,9984]{2,1,0:T(8,128)(2,1)} %shard_map.83.s0.s1.s2, bf16[3,3,24,32]{3,2,1,0:T(8,128)(2,1)} %pad_bitcast_fusion.w_ref), custom_call_target="tpu_custom_call" | custom-call | tf_op jit(solution)/shard_map/pallas_call | solution.py:169
  221.4 1.3 slice.140
  222.8 0.2 reshape.562
  223.1 0.7 copy.90
  (46 shorter events, 0.7 us)
Async XLA Ops:
  6.5 33.0 %all-gather.2.cloned.1.call-start = ((), (), s32[]{:S(2)}) async-start(), calls=%async_computation.3 | async-start | bytes 1327104 | tf_op jit(solution)/shard_map/all_gather | solution.py:216
  41.4 1.2 copy-start.8
  41.4 1.2 copy-start.9
  45.3 8.3 %copy-start.13 = (s32[128,6]{0,1:T(8,128)S(1)}, s32[128,6]{0,1:T(8,128)}, u32[]{:S(2)}) copy-start(s32[128,6]{0,1:T(8,128)} %param.11) | copy-start | bytes 9220
  45.3 24.2 %all-to-all-start = ((bf16[2,1,4,192,384]{4,2,0,1,3:T(4,128)(2,1)}), bf16[2,1,4,192,384]{4,2,0,1,3:T(4,128)(2,1)S(1)}, u32[]{:S(2)}, u32[]{:S(2)}) async-start(bf16[2,1,4,192,384]{4,2,0,1,3:T(4,128)(2,1)} %copy.72), calls=%async_computation | async-start | bytes 2359296 | tf_op jit(solution)/shard_map/all_to_all | solution.py:225
  73.9 1.9 copy-start.3
  73.9 1.9 copy-start.4
  78.6 6.8 %copy-start.15 = (pred[8]{0:T(512)(128)(4,1)S(1)}, pred[8]{0:T(512)(128)(4,1)}, u32[]{:S(2)}) copy-start(pred[8]{0:T(512)(128)(4,1)} %compare_and_fusion.3) | copy-start | bytes 28
  78.6 22.5 %all-to-all-start.1 = ((bf16[2,1,128,6,384]{4,0,3,1,2:T(2,128)(2,1)}), bf16[2,1,128,6,384]{4,0,3,1,2:T(2,128)(2,1)S(1)}, u32[]{:S(2)}, u32[]{:S(2)}) async-start(bf16[2,1,128,6,384]{4,0,3,1,2:T(2,128)(2,1)} %copy.77), calls=%async_computation.1 | async-start | bytes 2359296 | tf_op jit(solution)/shard_map/all_to_all | solution.py:232
  101.1 0.9 copy-start.6
  101.1 1.0 copy-start.7
  102.1 1.1 copy-start.1
  102.1 1.2 copy-start.2
  107.3 7.6 %copy-start.10 = (pred[9984]{0:T(1024)(128)(4,1)S(1)}, pred[9984]{0:T(1024)(128)(4,1)}, u32[]{:S(2)}) copy-start(pred[9984]{0:T(1024)(128)(4,1)} %compare_and_fusion.1) | copy-start | bytes 29956
  107.3 7.6 %copy-start.14 = (pred[6]{0:T(512)(128)(4,1)S(1)}, pred[6]{0:T(512)(128)(4,1)}, u32[]{:S(2)}) copy-start(pred[6]{0:T(512)(128)(4,1)} %compare_and_fusion.2) | copy-start | bytes 22
  107.3 35.4 %all-to-all-start.2 = ((bf16[2,4,192,384]{3,0,1,2:T(2,128)(2,1)}), bf16[2,4,192,384]{3,0,1,2:T(2,128)(2,1)S(1)}, u32[]{:S(2)}, u32[]{:S(2)}) async-start(bf16[2,4,192,384]{3,0,1,2:T(2,128)(2,1)} %copy.85), calls=%async_computation.2 | async-start | bytes 2359296 | tf_op jit(solution)/shard_map/all_to_all | solution.py:246
  114.9 28.8 %copy-start = (f32[2,4,24,384]{3,2,1,0:T(8,128)S(1)}, f32[2,4,24,384]{3,2,1,0:T(8,128)}, u32[]{:S(2)}) copy-start(f32[2,4,24,384]{3,2,1,0:T(8,128)} %param.8) | copy-start | bytes 884740
  143.7 17.5 %copy-start.11 = (bf16[3,3,32,3,2]{2,4,3,1,0:T(2,128)(2,1)S(1)}, bf16[3,3,32,3,2]{2,4,3,1,0:T(2,128)(2,1)}, u32[]{:S(2)}) copy-start(bf16[3,3,32,3,2]{2,4,3,1,0:T(2,128)(2,1)} %param.13) | copy-start | bytes 10372
  143.7 17.7 %copy-start.5 = (bf16[3,3,32,3,32]{4,2,3,1,0:T(8,128)(2,1)S(1)}, bf16[3,3,32,3,32]{4,2,3,1,0:T(8,128)(2,1)}, u32[]{:S(2)}) copy-start(bf16[3,3,32,3,32]{4,2,3,1,0:T(8,128)(2,1)} %param.14) | copy-start | bytes 165892
  143.8 19.3 %copy-start.12 = (bf16[3,3,2,3,32]{4,2,3,1,0:T(2,128)(2,1)S(1)}, bf16[3,3,2,3,32]{4,2,3,1,0:T(2,128)(2,1)}, u32[]{:S(2)}) copy-start(bf16[3,3,2,3,32]{4,2,3,1,0:T(2,128)(2,1)} %param.15) | copy-start | bytes 10372
  143.8 6.6 %collective-permute-start = (bf16[2,4,3,384]{3,2,0,1:T(4,128)(2,1)S(1)}, bf16[2,4,3,384]{3,2,0,1:T(4,128)(2,1)S(1)}, u32[]{:S(2)}, u32[]{:S(2)}) collective-permute-start(bf16[2,4,3,384]{3,2,0,1:T(4,128)(2,1)S(1)} %get-tuple-element.23), channel_id=1, source_target_pairs={{0,32},{32,64},{64,96},{96,128},{128,160},{160,192},{192,224},{1,3... | collective-permute-start | bytes 55304 | tf_op jit(solution)/shard_map/ppermute | solution.py:16
  148.5 7.3 %collective-permute-start.1 = (bf16[2,4,3,384]{3,2,0,1:T(4,128)(2,1)S(1)}, bf16[2,4,3,384]{3,2,0,1:T(4,128)(2,1)S(1)}, u32[]{:S(2)}, u32[]{:S(2)}) collective-permute-start(bf16[2,4,3,384]{3,2,0,1:T(4,128)(2,1)S(1)} %get-tuple-element.24), channel_id=1, source_target_pairs={{32,0},{64,32},{96,64},{128,96},{160,128},{192,160},{224,192},{33,... | collective-permute-start | bytes 55304 | tf_op jit(solution)/shard_map/ppermute | solution.py:19
  155.8 7.9 %collective-permute-start.2 = (bf16[2,3,30,384]{3,2,0,1:T(8,128)(2,1)S(1)}, bf16[2,3,30,384]{3,2,0,1:T(8,128)(2,1)S(1)}, u32[]{:S(2)}, u32[]{:S(2)}) collective-permute-start(bf16[2,3,30,384]{3,2,0,1:T(8,128)(2,1)S(1)} %get-tuple-element.17), channel_id=1, source_target_pairs={{0,1},{1,2},{2,3},{3,4},{4,5},{5,6},{6,7},{7,8},{8,9},{9,10},{10,1... | collective-permute-start | bytes 414728 | tf_op jit(solution)/shard_map/ppermute | solution.py:16
  158.0 9.7 %collective-permute-start.3 = (bf16[2,3,30,384]{3,2,0,1:T(8,128)(2,1)S(1)}, bf16[2,3,30,384]{3,2,0,1:T(8,128)(2,1)S(1)}, u32[]{:S(2)}, u32[]{:S(2)}) collective-permute-start(bf16[2,3,30,384]{3,2,0,1:T(8,128)(2,1)S(1)} %get-tuple-element.18), channel_id=1, source_target_pairs={{1,0},{2,1},{3,2},{4,3},{5,4},{6,5},{7,6},{8,7},{9,8},{10,9},{11,1... | collective-permute-start | bytes 414728 | tf_op jit(solution)/shard_map/ppermute | solution.py:19
Sparse Core Ops, SparseCore 0:
  9.2 30.2 all-gather.1

commit v9 on v8

--- a/solution.py
+++ b/solution.py
@@ -195,6 +195,36 @@
 def convolve_roll(block, weight, out_rows, inside=None):
     out = conv_roll(padded_channels(block), tap_matrix(weight), out_rows, inside)
     return out[:, : weight.shape[2]]
+
+
+def halo_both(block, width):
+    coils = lax.axis_size("coil")
+    slabs = lax.axis_size("slab")
+
+    def moved(piece, coil_step, slab_step):
+        pairs = []
+        for coil in range(coils):
+            for slab in range(slabs):
+                target_coil, target_slab = coil + coil_step, slab + slab_step
+                if 0 <= target_coil < coils and 0 <= target_slab < slabs:
+                    pairs.append((coil * slabs + slab, target_coil * slabs + target_slab))
+        return lax.ppermute(piece, ("coil", "slab"), pairs)
+
+    depth, rows = block.shape[1], block.shape[2]
+    rows_of = {1: (rows - width, rows), 0: (0, rows), -1: (0, width)}
+    depth_of = {1: (depth - width, depth), 0: (0, depth), -1: (0, width)}
+    grid = []
+    for slab_step in (1, 0, -1):
+        line = []
+        for coil_step in (1, 0, -1):
+            low_z, high_z = depth_of[slab_step]
+            low_y, high_y = rows_of[coil_step]
+            piece = block[:, low_z:high_z, low_y:high_y]
+            if coil_step or slab_step:
+                piece = moved(piece, coil_step, slab_step)
+            line.append(piece)
+        grid.append(jnp.concatenate(line, axis=2))
+    return jnp.concatenate(grid, axis=1)
 
 
 def per_device(
@@ -251,8 +281,7 @@
         gathered.astype(jnp.float32).reshape(2, slab_rows, coils, coil_rows, READ), axis=2
     )
     updated = image_field + scattered
-    activations = padded_2(updated.astype(jnp.bfloat16), (("coil", 2),), 3)
-    activations = padded_2(activations, (("slab", 1),), 3)
+    activations = halo_both(updated.astype(jnp.bfloat16), 3)
     depth, rows = activations.shape[1], activations.shape[2]
     activations = activations.transpose(1, 0, 2, 3).reshape(depth, 2, rows * READ)
     for layer_index, weight in enumerate(weights):

time: 234 us -> 247 us (1.056)
  starting transfers between devices: 34.5 us -> 53.4 us
  waiting for transfers between devices: 84.3 us -> 75.4 us
    ppermute x4 -> x8, starting transfers between devices: 11.8 us -> 30.7 us  [moved(): return lax.ppermute(piece, ('coil', 'slab'), pairs)]
    ppermute x4 -> x8, waiting for transfers between devices: 9.33 us -> 2.56 us  [moved(): return lax.ppermute(piece, ('coil', 'slab'), pairs)]
  transfers between devices with their start and end apart: 8 -> 12, of which waited for: 6 -> 5; matrix products, arithmetic and copies ran while one was open for 8% -> 8% of each run, Pallas kernels for 0% -> 0%
where the time goes in v9:
time: 247 us; the launch traced here: 243 us
  waiting for transfers between devices  75.4 us (31%)
  starting transfers between devices  53.4 us (22%)
  Pallas kernels  48.4 us (20%)
  other arithmetic  25.9 us (10%)
  local copies, waits for them, and re-layouts  19 us (8%)
  between operations  14.5 us (6%)
  matrix products  6.22 us (3%)
    pallas_call x2, Pallas kernels, conv_flat(): pl.pallas_call(body, grid=(out_depth,), in_specs=in_specs, out_specs=pl.B...  39.5 us
    ppermute x8, starting transfers between devices, moved(): return lax.ppermute(piece, ('coil', 'slab'), pairs)  30.7 us
    all_to_all x1, waiting for transfers between devices, per_device(): lax.all_to_all((-step_size * partial_value).astype(jnp.bfloat16), 'coil',...  26.8 us
    all_gather x1, waiting for transfers between devices, per_device(): lax.all_gather(pixels, 'coil', axis=2, tiled=True).astype(jnp.float32)  21.2 us
    all_to_all x1, waiting for transfers between devices, per_device(): lax.all_to_all(residual, 'slab', split_axis=2, concat_axis=3, tiled=True)  13.9 us
    all_to_all x1, waiting for transfers between devices, per_device(): lax.all_to_all(spectrum, 'slab', split_axis=3, concat_axis=2, tiled=True)  10.9 us
    pallas_call x1, Pallas kernels, conv_roll(): pl.pallas_call(body, grid=(out_depth,), in_specs=in_specs, out_specs=pl.B...  8.86 us
    all_to_all x1, starting transfers between devices, per_device(): lax.all_to_all(spectrum, 'slab', split_axis=3, concat_axis=2, tiled=True)  8.27 us
  transfers between devices with their start and end apart: 12, of which 5 were waited for; matrix products, arithmetic and copies ran while one was open for 8% of the time, Pallas kernels for 0%

profile of v9, /device:TPU:121, one launch (start us, length us, event | category | flops | bytes accessed | tf_op | source)
XLA Modules:
  0.0 242.7 jit_solution(6304232838196100147)
XLA Ops:
  6.5 1.6 copy.131
  8.2 1.4 convert_element_type.194
  9.6 0.8 fusion.84
  10.4 0.8 fusion.59
  11.2 2.3 fusion.58
  13.6 2.6 %fusion.43 = (bf16[384,1,384]{2,0,1:T(8,128)(2,1)S(1)}, bf16[384,1,384]{2,0,1:T(8,128)(2,1)S(1)}) fusion(), kind=kLoop, calls=%fused_computation.86 | loop fusion | flops 1916928 | bytes 589824 | tf_op jit(solution)/shard_map/stack;squeeze | solution.py:37
  16.2 0.9 fusion.47
  17.1 1.3 fusion.33
  18.3 21.2 %all-gather.2.cloned.1.call-done = bf16[2,4,192,384]{3,2,0,1:T(8,128)(2,1)} async-done(((bf16[2,4,24,384]{3,2,0,1:T(8,128)(2,1)}), bf16[2,4,192,384]{3,2,0,1:T(8,128)(2,1)}) %all-gather.2.cloned.1.call-update) | async-done | bytes 1179664 | tf_op jit(solution)/shard_map/all_gather | solution.py:246
  39.5 1.4 convert_element_type.200
  40.9 0.4 fusion.17
  41.4 1.1 fusion.7
  42.5 0.8 fusion.3
  43.4 1.9 copy.72
  45.3 8.3 %all-to-all-start = ((bf16[2,1,4,192,384]{4,2,0,1,3:T(4,128)(2,1)}), bf16[2,1,4,192,384]{4,2,0,1,3:T(4,128)(2,1)S(1)}, u32[]{:S(2)}, u32[]{:S(2)}) async-start(bf16[2,1,4,192,384]{4,2,0,1,3:T(4,128)(2,1)} %copy.72), calls=%async_computation | async-start | bytes 2359296 | tf_op jit(solution)/shard_map/all_to_all | solution.py:255
  54.3 0.6 compare_and_fusion.3
  54.8 0.6 compare_and_fusion.2
  55.4 0.3 fusion.87
  55.7 0.3 fusion.85
  56.0 0.7 fusion.64
  56.7 0.6 compare_and_fusion
  57.4 0.6 compare_and_fusion.1
  58.0 0.6 iota_remainder_fusion.2
  58.6 10.9 %all-to-all-done = bf16[2,1,4,192,384]{4,2,0,1,3:T(4,128)(2,1)S(1)} async-done(((bf16[2,1,4,192,384]{4,2,0,1,3:T(4,128)(2,1)}), bf16[2,1,4,192,384]{4,2,0,1,3:T(4,128)(2,1)S(1)}, u32[]{:S(2)}, u32[]{:S(2)}) %all-to-all-start) | async-done | bytes 1179680 | tf_op jit(solution)/shard_map/all_to_all | solution.py:255
  69.5 0.4 copy.73
  69.9 1.6 copy.74
  71.5 2.4 reshape.574
  73.9 1.9 fusion.9
  75.8 0.5 fusion.6
  76.3 2.2 copy.77
  78.6 6.8 %all-to-all-start.1 = ((bf16[2,1,128,6,384]{4,0,3,1,2:T(2,128)(2,1)}), bf16[2,1,128,6,384]{4,0,3,1,2:T(2,128)(2,1)S(1)}, u32[]{:S(2)}, u32[]{:S(2)}) async-start(bf16[2,1,128,6,384]{4,0,3,1,2:T(2,128)(2,1)} %copy.77), calls=%async_computation.1 | async-start | bytes 2359296 | tf_op jit(solution)/shard_map/all_to_all | solution.py:262
  85.3 1.7 and_convert_fusion.refs_0_
  87.0 13.9 %all-to-all-done.1 = bf16[2,1,128,6,384]{4,0,3,1,2:T(2,128)(2,1)S(1)} async-done(((bf16[2,1,128,6,384]{4,0,3,1,2:T(2,128)(2,1)}), bf16[2,1,128,6,384]{4,0,3,1,2:T(2,128)(2,1)S(1)}, u32[]{:S(2)}, u32[]{:S(2)}) %all-to-all-start.1) | async-done | bytes 1179680 | tf_op jit(solution)/shard_map/all_to_all | solution.py:262
  101.0 0.5 copy.78
  101.4 0.5 copy-done.8
  102.0 0.8 fusion.4
  103.2 1.1 convert_bitcast_fusion
  104.3 0.3 fusion.20
  104.9 2.2 copy.85
  107.2 7.6 %all-to-all-start.2 = ((bf16[2,4,192,384]{3,0,1,2:T(2,128)(2,1)}), bf16[2,4,192,384]{3,0,1,2:T(2,128)(2,1)S(1)}, u32[]{:S(2)}, u32[]{:S(2)}) async-start(bf16[2,4,192,384]{3,0,1,2:T(2,128)(2,1)} %copy.85), calls=%async_computation.2 | async-start | bytes 2359296 | tf_op jit(solution)/shard_map/all_to_all | solution.py:276
  114.8 0.9 and_convert_fusion.1.refs_0_
  115.7 26.8 %all-to-all-done.2 = bf16[2,4,192,384]{3,0,1,2:T(2,128)(2,1)S(1)} async-done(((bf16[2,4,192,384]{3,0,1,2:T(2,128)(2,1)}), bf16[2,4,192,384]{3,0,1,2:T(2,128)(2,1)S(1)}, u32[]{:S(2)}, u32[]{:S(2)}) %all-to-all-start.2) | async-done | bytes 1179680 | tf_op jit(solution)/shard_map/all_to_all | solution.py:276
  142.5 1.0 convert_reduce_fusion
  143.7 3.8 %collective-permute-start = (bf16[2,3,3,384]{3,2,0,1:T(4,128)(2,1)S(1)}, bf16[2,3,3,384]{3,2,0,1:T(4,128)(2,1)S(1)}, u32[]{:S(2)}, u32[]{:S(2)}) collective-permute-start(bf16[2,3,3,384]{3,2,0,1:T(4,128)(2,1)S(1)} %get-tuple-element.21), channel_id=1, source_target_pairs={{0,33},{1,34},{2,35},{3,36},{4,37},{5,38},{6,39},{7,40},{8,41},{9,... | collective-permute-start | bytes 41480 | tf_op jit(solution)/shard_map/ppermute | solution.py:211
  147.4 2.7 %collective-permute-start.2 = (bf16[2,3,3,384]{3,2,0,1:T(4,128)(2,1)S(1)}, bf16[2,3,3,384]{3,2,0,1:T(4,128)(2,1)S(1)}, u32[]{:S(2)}, u32[]{:S(2)}) collective-permute-start(bf16[2,3,3,384]{3,2,0,1:T(4,128)(2,1)S(1)} %get-tuple-element.24), channel_id=1, source_target_pairs={{32,1},{33,2},{34,3},{35,4},{36,5},{37,6},{38,7},{39,8},{40,9},{41... | collective-permute-start | bytes 41480 | tf_op jit(solution)/shard_map/ppermute | solution.py:211
  150.1 4.1 %collective-permute-start.5 = (bf16[2,3,3,384]{3,2,0,1:T(4,128)(2,1)S(1)}, bf16[2,3,3,384]{3,2,0,1:T(4,128)(2,1)S(1)}, u32[]{:S(2)}, u32[]{:S(2)}) collective-permute-start(bf16[2,3,3,384]{3,2,0,1:T(4,128)(2,1)S(1)} %get-tuple-element.23), channel_id=1, source_target_pairs={{1,32},{2,33},{3,34},{4,35},{5,36},{6,37},{7,38},{8,39},{9,40},{10... | collective-permute-start | bytes 41480 | tf_op jit(solution)/shard_map/ppermute | solution.py:211
  154.3 1.9 collective-permute-start.7
  156.2 10.2 %collective-permute-start.1 = (bf16[2,3,24,384]{3,2,0,1:T(8,128)(2,1)S(1)}, bf16[2,3,24,384]{3,2,0,1:T(8,128)(2,1)S(1)}, u32[]{:S(2)}, u32[]{:S(2)}) collective-permute-start(bf16[2,3,24,384]{3,2,0,1:T(8,128)(2,1)S(1)} %get-tuple-element.25), channel_id=1, source_target_pairs={{0,1},{1,2},{2,3},{3,4},{4,5},{5,6},{6,7},{7,8},{8,9},{9,10},{10,1... | collective-permute-start | bytes 331784 | tf_op jit(solution)/shard_map/ppermute | solution.py:211
  166.4 1.9 collective-permute-start.6
  168.3 4.0 %collective-permute-start.3 = (bf16[2,4,3,384]{3,2,0,1:T(4,128)(2,1)S(1)}, bf16[2,4,3,384]{3,2,0,1:T(4,128)(2,1)S(1)}, u32[]{:S(2)}, u32[]{:S(2)}) collective-permute-start(bf16[2,4,3,384]{3,2,0,1:T(4,128)(2,1)S(1)} %get-tuple-element.27), channel_id=1, source_target_pairs={{0,32},{1,33},{2,34},{3,35},{4,36},{5,37},{6,38},{7,39},{8,40},{9,... | collective-permute-start | bytes 55304 | tf_op jit(solution)/shard_map/ppermute | solution.py:211
  172.3 2.1 collective-permute-start.4
  174.5 0.6 pad_bitcast_fusion.w_ref
  175.5 0.8 reshape.560.w_ref
  176.3 0.6 pad.18.w_ref
  177.0 2.5 %collective-permute-done.4 = bf16[2,4,3,384]{3,2,0,1:T(4,128)(2,1)S(1)} collective-permute-done((bf16[2,4,3,384]{3,2,0,1:T(4,128)(2,1)S(1)}, bf16[2,4,3,384]{3,2,0,1:T(4,128)(2,1)S(1)}, u32[]{:S(2)}, u32[]{:S(2)}) %collective-permute-start.4) | collective-permute-done | bytes 18464 | tf_op jit(solution)/shard_map/ppermute | solution.py:211
  179.6 0.2 maximum_bitcast_fusion.6
  180.0 1.4 compare_select_fusion.1
  181.4 3.6 %maximum_maximum_fusion.s0.s1.s2 = bf16[10,16,11520]{2,1,0:T(8,128)(2,1)} fusion(bf16[10,2,11520]{2,1,0:T(2,128)(2,1)S(1)} %get-tuple-element.14, bf16[10,2,11520]{2,1,0:T(2,128)(2,1)S(1)} %reshape.558, bf16[10,2,11520]{2,1,0:T(2,128)(2,1)S(1)} %get-tuple-element.13, bf16[16]{0:T(256)(128)(2,1)S(1)} %pad.23.clone), kind=kLoop, calls=%fused_computation | loop fusion | flops 14745600 | bytes 5068832 | tf_op jit(solution)/shard_map/concatenate | solution.py:114
  185.1 17.9 %shard_map.82.s0.s1.s2 = bf16[8,96,10752]{2,1,0:T(8,128)(2,1)} custom-call(bf16[10,16,11520]{2,1,0:T(8,128)(2,1)} %maximum_maximum_fusion.s0.s1.s2, bf16[10,16,11520]{2,1,0:T(8,128)(2,1)} %maximum_maximum_fusion.s0.s1.s2, bf16[10,16,11520]{2,1,0:T(8,128)(2,1)} %maximum_maximum_fusion.s0.s1.s2, bf16[3,3,32,16]{3,2,1,0:T(8,128)(2,1)} %pad.18.w_ref, ...), custom_call_target="tpu_custom_call" | custom-call | tf_op jit(solution)/shard_map/pallas_call | solution.py:93
  202.9 21.7 %shard_map.83.s0.s1.s2 = bf16[6,32,9984]{2,1,0:T(8,128)(2,1)} custom-call(bf16[8,96,10752]{2,1,0:T(8,128)(2,1)} %shard_map.82.s0.s1.s2, bf16[8,96,10752]{2,1,0:T(8,128)(2,1)} %shard_map.82.s0.s1.s2, bf16[8,96,10752]{2,1,0:T(8,128)(2,1)} %shard_map.82.s0.s1.s2, bf16[3,3,32,96]{3,2,1,0:T(8,128)(2,1)} %reshape.560.w_ref, f32[6,1,9984]{2,1,0:T(1,128)} %and_convert_fusion.1.refs_0_), custom_call_target="tpu_custom_call" | custom-call | tf_op jit(solution)/shard_map/pallas_call | solution.py:93
  224.6 8.9 %shard_map.84 = f32[4,8,9216]{2,1,0:T(8,128)} custom-call(bf16[6,32,9984]{2,1,0:T(8,128)(2,1)} %shard_map.83.s0.s1.s2, bf16[6,32,9984]{2,1,0:T(8,128)(2,1)} %shard_map.83.s0.s1.s2, bf16[6,32,9984]{2,1,0:T(8,128)(2,1)} %shard_map.83.s0.s1.s2, bf16[3,3,24,32]{3,2,1,0:T(8,128)(2,1)} %pad_bitcast_fusion.w_ref), custom_call_target="tpu_custom_call" | custom-call | tf_op jit(solution)/shard_map/pallas_call | solution.py:169
  233.5 1.3 slice.160
  234.8 0.2 reshape.562
  235.1 0.7 copy.90
  (58 shorter events, 1.7 us)
Async XLA Ops:
  6.5 33.0 %all-gather.2.cloned.1.call-start = ((), (), s32[]{:S(2)}) async-start(), calls=%async_computation.3 | async-start | bytes 1327104 | tf_op jit(solution)/shard_map/all_gather | solution.py:246
  41.4 1.2 copy-start.10
  41.4 1.2 copy-start.11
  45.3 8.3 %copy-start.15 = (s32[128,6]{0,1:T(8,128)S(1)}, s32[128,6]{0,1:T(8,128)}, u32[]{:S(2)}) copy-start(s32[128,6]{0,1:T(8,128)} %param.11) | copy-start | bytes 9220
  45.3 24.2 %all-to-all-start = ((bf16[2,1,4,192,384]{4,2,0,1,3:T(4,128)(2,1)}), bf16[2,1,4,192,384]{4,2,0,1,3:T(4,128)(2,1)S(1)}, u32[]{:S(2)}, u32[]{:S(2)}) async-start(bf16[2,1,4,192,384]{4,2,0,1,3:T(4,128)(2,1)} %copy.72), calls=%async_computation | async-start | bytes 2359296 | tf_op jit(solution)/shard_map/all_to_all | solution.py:255
  73.9 1.9 copy-start.3
  73.9 1.9 copy-start.4
  78.6 6.8 %copy-start.17 = (pred[8]{0:T(512)(128)(4,1)S(1)}, pred[8]{0:T(512)(128)(4,1)}, u32[]{:S(2)}) copy-start(pred[8]{0:T(512)(128)(4,1)} %compare_and_fusion.3) | copy-start | bytes 28
  78.6 22.4 %all-to-all-start.1 = ((bf16[2,1,128,6,384]{4,0,3,1,2:T(2,128)(2,1)}), bf16[2,1,128,6,384]{4,0,3,1,2:T(2,128)(2,1)S(1)}, u32[]{:S(2)}, u32[]{:S(2)}) async-start(bf16[2,1,128,6,384]{4,0,3,1,2:T(2,128)(2,1)} %copy.77), calls=%async_computation.1 | async-start | bytes 2359296 | tf_op jit(solution)/shard_map/all_to_all | solution.py:262
  101.0 0.9 copy-start.8
  101.0 1.0 copy-start.9
  102.0 1.1 copy-start.1
  102.0 1.2 copy-start.2
  107.2 7.6 %copy-start.12 = (pred[9984]{0:T(1024)(128)(4,1)S(1)}, pred[9984]{0:T(1024)(128)(4,1)}, u32[]{:S(2)}) copy-start(pred[9984]{0:T(1024)(128)(4,1)} %compare_and_fusion.1) | copy-start | bytes 29956
  107.2 7.6 %copy-start.16 = (pred[6]{0:T(512)(128)(4,1)S(1)}, pred[6]{0:T(512)(128)(4,1)}, u32[]{:S(2)}) copy-start(pred[6]{0:T(512)(128)(4,1)} %compare_and_fusion.2) | copy-start | bytes 22
  107.2 35.3 %all-to-all-start.2 = ((bf16[2,4,192,384]{3,0,1,2:T(2,128)(2,1)}), bf16[2,4,192,384]{3,0,1,2:T(2,128)(2,1)S(1)}, u32[]{:S(2)}, u32[]{:S(2)}) async-start(bf16[2,4,192,384]{3,0,1,2:T(2,128)(2,1)} %copy.85), calls=%async_computation.2 | async-start | bytes 2359296 | tf_op jit(solution)/shard_map/all_to_all | solution.py:276
  114.8 28.7 %copy-start = (f32[2,4,24,384]{3,2,1,0:T(8,128)S(1)}, f32[2,4,24,384]{3,2,1,0:T(8,128)}, u32[]{:S(2)}) copy-start(f32[2,4,24,384]{3,2,1,0:T(8,128)} %param.8) | copy-start | bytes 884740
  142.5 32.0 %copy-start.14 = (bf16[3,3,2,3,32]{4,2,3,1,0:T(2,128)(2,1)S(1)}, bf16[3,3,2,3,32]{4,2,3,1,0:T(2,128)(2,1)}, u32[]{:S(2)}) copy-start(bf16[3,3,2,3,32]{4,2,3,1,0:T(2,128)(2,1)} %param.15) | copy-start | bytes 10372
  142.5 32.7 %copy-start.13 = (bf16[3,3,32,3,2]{2,4,3,1,0:T(2,128)(2,1)S(1)}, bf16[3,3,32,3,2]{2,4,3,1,0:T(2,128)(2,1)}, u32[]{:S(2)}) copy-start(bf16[3,3,32,3,2]{2,4,3,1,0:T(2,128)(2,1)} %param.13) | copy-start | bytes 10372
  143.5 31.8 %copy-start.5 = (bf16[3,3,32,3,32]{4,2,3,1,0:T(8,128)(2,1)S(1)}, bf16[3,3,32,3,32]{4,2,3,1,0:T(8,128)(2,1)}, u32[]{:S(2)}) copy-start(bf16[3,3,32,3,32]{4,2,3,1,0:T(8,128)(2,1)} %param.14) | copy-start | bytes 165892
  143.7 22.7 %collective-permute-start = (bf16[2,3,3,384]{3,2,0,1:T(4,128)(2,1)S(1)}, bf16[2,3,3,384]{3,2,0,1:T(4,128)(2,1)S(1)}, u32[]{:S(2)}, u32[]{:S(2)}) collective-permute-start(bf16[2,3,3,384]{3,2,0,1:T(4,128)(2,1)S(1)} %get-tuple-element.21), channel_id=1, source_target_pairs={{0,33},{1,34},{2,35},{3,36},{4,37},{5,38},{6,39},{7,40},{8,41},{9,... | collective-permute-start | bytes 41480 | tf_op jit(solution)/shard_map/ppermute | solution.py:211
  147.4 20.9 %collective-permute-start.2 = (bf16[2,3,3,384]{3,2,0,1:T(4,128)(2,1)S(1)}, bf16[2,3,3,384]{3,2,0,1:T(4,128)(2,1)S(1)}, u32[]{:S(2)}, u32[]{:S(2)}) collective-permute-start(bf16[2,3,3,384]{3,2,0,1:T(4,128)(2,1)S(1)} %get-tuple-element.24), channel_id=1, source_target_pairs={{32,1},{33,2},{34,3},{35,4},{36,5},{37,6},{38,7},{39,8},{40,9},{41... | collective-permute-start | bytes 41480 | tf_op jit(solution)/shard_map/ppermute | solution.py:211
  150.1 22.2 %collective-permute-start.5 = (bf16[2,3,3,384]{3,2,0,1:T(4,128)(2,1)S(1)}, bf16[2,3,3,384]{3,2,0,1:T(4,128)(2,1)S(1)}, u32[]{:S(2)}, u32[]{:S(2)}) collective-permute-start(bf16[2,3,3,384]{3,2,0,1:T(4,128)(2,1)S(1)} %get-tuple-element.23), channel_id=1, source_target_pairs={{1,32},{2,33},{3,34},{4,35},{5,36},{6,37},{7,38},{8,39},{9,40},{10... | collective-permute-start | bytes 41480 | tf_op jit(solution)/shard_map/ppermute | solution.py:211
  154.3 22.8 %collective-permute-start.7 = (bf16[2,3,3,384]{3,2,0,1:T(4,128)(2,1)S(1)}, bf16[2,3,3,384]{3,2,0,1:T(4,128)(2,1)S(1)}, u32[]{:S(2)}, u32[]{:S(2)}) collective-permute-start(bf16[2,3,3,384]{3,2,0,1:T(4,128)(2,1)S(1)} %get-tuple-element.22), channel_id=1, source_target_pairs={{33,0},{34,1},{35,2},{36,3},{37,4},{38,5},{39,6},{40,7},{41,8},{42... | collective-permute-start | bytes 41480 | tf_op jit(solution)/shard_map/ppermute | solution.py:211
  156.2 23.4 %collective-permute-start.1 = (bf16[2,3,24,384]{3,2,0,1:T(8,128)(2,1)S(1)}, bf16[2,3,24,384]{3,2,0,1:T(8,128)(2,1)S(1)}, u32[]{:S(2)}, u32[]{:S(2)}) collective-permute-start(bf16[2,3,24,384]{3,2,0,1:T(8,128)(2,1)S(1)} %get-tuple-element.25), channel_id=1, source_target_pairs={{0,1},{1,2},{2,3},{3,4},{4,5},{5,6},{6,7},{7,8},{8,9},{9,10},{10,1... | collective-permute-start | bytes 331784 | tf_op jit(solution)/shard_map/ppermute | solution.py:211
  166.4 13.2 %collective-permute-start.6 = (bf16[2,3,24,384]{3,2,0,1:T(8,128)(2,1)S(1)}, bf16[2,3,24,384]{3,2,0,1:T(8,128)(2,1)S(1)}, u32[]{:S(2)}, u32[]{:S(2)}) collective-permute-start(bf16[2,3,24,384]{3,2,0,1:T(8,128)(2,1)S(1)} %get-tuple-element.26), channel_id=1, source_target_pairs={{1,0},{2,1},{3,2},{4,3},{5,4},{6,5},{7,6},{8,7},{9,8},{10,9},{11,1... | collective-permute-start | bytes 331784 | tf_op jit(solution)/shard_map/ppermute | solution.py:211
  168.3 8.7 %collective-permute-start.3 = (bf16[2,4,3,384]{3,2,0,1:T(4,128)(2,1)S(1)}, bf16[2,4,3,384]{3,2,0,1:T(4,128)(2,1)S(1)}, u32[]{:S(2)}, u32[]{:S(2)}) collective-permute-start(bf16[2,4,3,384]{3,2,0,1:T(4,128)(2,1)S(1)} %get-tuple-element.27), channel_id=1, source_target_pairs={{0,32},{1,33},{2,34},{3,35},{4,36},{5,37},{6,38},{7,39},{8,40},{9,... | collective-permute-start | bytes 55304 | tf_op jit(solution)/shard_map/ppermute | solution.py:211
  172.3 7.3 %collective-permute-start.4 = (bf16[2,4,3,384]{3,2,0,1:T(4,128)(2,1)S(1)}, bf16[2,4,3,384]{3,2,0,1:T(4,128)(2,1)S(1)}, u32[]{:S(2)}, u32[]{:S(2)}) collective-permute-start(bf16[2,4,3,384]{3,2,0,1:T(4,128)(2,1)S(1)} %get-tuple-element.28), channel_id=1, source_target_pairs={{32,0},{33,1},{34,2},{35,3},{36,4},{37,5},{38,6},{39,7},{40,8},{41... | collective-permute-start | bytes 55304 | tf_op jit(solution)/shard_map/ppermute | solution.py:211
  175.5 4.5 %copy-start.6 = (s32[11520]{0:T(1024)S(1)}, s32[11520]{0:T(1024)}, u32[]{:S(2)}) copy-start(s32[11520]{0:T(1024)} %get-tuple-element.43) | copy-start | bytes 138244
  175.5 4.5 %copy-start.7 = (s32[11520]{0:T(1024)S(1)}, s32[11520]{0:T(1024)}, u32[]{:S(2)}) copy-start(s32[11520]{0:T(1024)} %get-tuple-element.44) | copy-start | bytes 138244
Sparse Core Ops, SparseCore 0:
  9.2 30.2 all-gather.1

commit v10 on v8

--- a/solution.py
+++ b/solution.py
@@ -127,10 +127,11 @@
     return out[:, : weight.shape[2]]
 
 
-def conv_roll(block, kernel, out_rows, inside=None):
+def conv_roll(block, kernel, out_rows, inside=None, kept=None):
     depth_in, width, lanes_in = block.shape
     out_depth = depth_in - 2
     out_channels = kernel.shape[2] // 3
+    kept = kept or out_channels
     lanes = out_rows * READ
     starts = range(0, lanes, CHUNK)
 
@@ -155,7 +156,7 @@
                 + jnp.where(place == 0, 0.0, left)
                 + jnp.where(place == READ - 1, 0.0, right)
             )
-            o_ref[0, :, pl.ds(start, size)] = finish(total, refs, start, size, False)
+            o_ref[0, :, pl.ds(start, size)] = finish(total[:kept], refs, start, size, False)
 
     in_specs = [
         pl.BlockSpec((1, width, lanes_in), lambda z, dz=dz: (z + dz, 0, 0)) for dz in range(3)
@@ -170,8 +171,8 @@
         body,
         grid=(out_depth,),
         in_specs=in_specs,
-        out_specs=pl.BlockSpec((1, out_channels, lanes), lambda z: (z, 0, 0)),
-        out_shape=jax.ShapeDtypeStruct((out_depth, out_channels, lanes), kind),
+        out_specs=pl.BlockSpec((1, kept, lanes), lambda z: (z, 0, 0)),
+        out_shape=jax.ShapeDtypeStruct((out_depth, kept, lanes), kind),
     )(block, block, block, kernel, *extra)
 
 
@@ -193,7 +194,7 @@
 
 
 def convolve_roll(block, weight, out_rows, inside=None):
-    out = conv_roll(padded_channels(block), tap_matrix(weight), out_rows, inside)
+    out = conv_roll(padded_channels(block), tap_matrix(weight), out_rows, inside, weight.shape[2])
     return out[:, : weight.shape[2]]
 
 

time: 234 us -> 233 us (level)
  no operation moved by 1% of the time
where the time goes in v10:
time: 233 us; the launch traced here: 230 us
  waiting for transfers between devices  84.3 us (36%)
  Pallas kernels  48.3 us (21%)
  starting transfers between devices  34.5 us (15%)
  other arithmetic  23.8 us (10%)
  local copies, waits for them, and re-layouts  18.6 us (8%)
  between operations  14.5 us (6%)
  matrix products  6.22 us (3%)
    pallas_call x2, Pallas kernels, conv_flat(): pl.pallas_call(body, grid=(out_depth,), in_specs=in_specs, out_specs=pl.B...  39.5 us
    all_to_all x1, waiting for transfers between devices, per_device(): lax.all_to_all((-step_size * partial_value).astype(jnp.bfloat16), 'coil',...  26.8 us
    all_gather x1, waiting for transfers between devices, per_device(): lax.all_gather(pixels, 'coil', axis=2, tiled=True).astype(jnp.float32)  21.2 us
    all_to_all x1, waiting for transfers between devices, per_device(): lax.all_to_all(residual, 'slab', split_axis=2, concat_axis=3, tiled=True)  14.6 us
    all_to_all x1, waiting for transfers between devices, per_device(): lax.all_to_all(spectrum, 'slab', split_axis=3, concat_axis=2, tiled=True)  12.3 us
    ppermute x2, waiting for transfers between devices, padded_2(): lax.ppermute(lax.slice_in_dim(block, 0, width, axis=dim), axis, backward)  9.32 us
    pallas_call x1, Pallas kernels, conv_roll(): pl.pallas_call(body, grid=(out_depth,), in_specs=in_specs, out_specs=pl.B...  8.81 us
    all_to_all x1, starting transfers between devices, per_device(): lax.all_to_all(spectrum, 'slab', split_axis=3, concat_axis=2, tiled=True)  8.26 us
  transfers between devices with their start and end apart: 8, of which 6 were waited for; matrix products, arithmetic and copies ran while one was open for 8% of the time, Pallas kernels for 0%

profile of v10, /device:TPU:121, one launch (start us, length us, event | category | flops | bytes accessed | tf_op | source)
XLA Modules:
  0.0 230.2 jit_solution(3549068544785542441)
XLA Ops:
  6.5 1.6 copy.131
  8.2 1.4 convert_element_type.194
  9.6 0.8 fusion.84
  10.4 0.8 fusion.59
  11.2 2.3 %fusion.58 = bf16[384,1,384]{2,0,1:T(8,128)(2,1)S(1)} fusion(), kind=kLoop, calls=%fused_computation.114 | loop fusion | flops 2064384 | bytes 294912 | tf_op jit(solution)/shard_map/neg | solution.py:36
  13.6 2.6 %fusion.43 = (bf16[384,1,384]{2,0,1:T(8,128)(2,1)S(1)}, bf16[384,1,384]{2,0,1:T(8,128)(2,1)S(1)}) fusion(), kind=kLoop, calls=%fused_computation.86 | loop fusion | flops 1916928 | bytes 589824 | tf_op jit(solution)/shard_map/stack;squeeze | solution.py:37
  16.2 0.9 fusion.47
  17.1 1.2 fusion.33
  18.3 21.2 %all-gather.2.cloned.1.call-done = bf16[2,4,192,384]{3,2,0,1:T(8,128)(2,1)} async-done(((bf16[2,4,24,384]{3,2,0,1:T(8,128)(2,1)}), bf16[2,4,192,384]{3,2,0,1:T(8,128)(2,1)}) %all-gather.2.cloned.1.call-update) | async-done | bytes 1179664 | tf_op jit(solution)/shard_map/all_gather | solution.py:217
  39.5 1.4 convert_element_type.200
  40.9 0.4 fusion.17
  41.4 1.1 fusion.7
  42.5 0.8 fusion.3
  43.4 2.0 copy.72
  45.3 8.3 %all-to-all-start = ((bf16[2,1,4,192,384]{4,2,0,1,3:T(4,128)(2,1)}), bf16[2,1,4,192,384]{4,2,0,1,3:T(4,128)(2,1)S(1)}, u32[]{:S(2)}, u32[]{:S(2)}) async-start(bf16[2,1,4,192,384]{4,2,0,1,3:T(4,128)(2,1)} %copy.72), calls=%async_computation | async-start | bytes 2359296 | tf_op jit(solution)/shard_map/all_to_all | solution.py:226
  54.3 0.6 compare_and_fusion.3
  54.9 0.5 compare_and_fusion.2
  55.4 0.3 fusion.87
  55.6 0.3 fusion.85
  55.9 0.7 fusion.64
  56.7 0.6 compare_and_fusion.1
  57.3 12.3 %all-to-all-done = bf16[2,1,4,192,384]{4,2,0,1,3:T(4,128)(2,1)S(1)} async-done(((bf16[2,1,4,192,384]{4,2,0,1,3:T(4,128)(2,1)}), bf16[2,1,4,192,384]{4,2,0,1,3:T(4,128)(2,1)S(1)}, u32[]{:S(2)}, u32[]{:S(2)}) %all-to-all-start) | async-done | bytes 1179680 | tf_op jit(solution)/shard_map/all_to_all | solution.py:226
  69.6 0.4 copy.73
  70.0 1.6 copy.74
  71.5 2.4 %reshape.574 = bf16[2,128,6,384,1]{3,1,0,2,4:T(8,128)(2,1)S(1)} reshape(bf16[2,1,32,4,6,384]{5,3,2,0,4,1:T(4,128)(2,1)} %copy.74) | data formatting | bytes 2359296 | tf_op jit(solution)/shard_map/reshape.18
  74.0 1.9 fusion.9
  75.8 0.5 fusion.6
  76.3 2.3 copy.77
  78.6 6.8 %all-to-all-start.1 = ((bf16[2,1,128,6,384]{4,0,3,1,2:T(2,128)(2,1)}), bf16[2,1,128,6,384]{4,0,3,1,2:T(2,128)(2,1)S(1)}, u32[]{:S(2)}, u32[]{:S(2)}) async-start(bf16[2,1,128,6,384]{4,0,3,1,2:T(2,128)(2,1)} %copy.77), calls=%async_computation.1 | async-start | bytes 2359296 | tf_op jit(solution)/shard_map/all_to_all | solution.py:233
  85.4 1.0 and_convert_fusion.refs_0_
  86.4 14.6 %all-to-all-done.1 = bf16[2,1,128,6,384]{4,0,3,1,2:T(2,128)(2,1)S(1)} async-done(((bf16[2,1,128,6,384]{4,0,3,1,2:T(2,128)(2,1)}), bf16[2,1,128,6,384]{4,0,3,1,2:T(2,128)(2,1)S(1)}, u32[]{:S(2)}, u32[]{:S(2)}) %all-to-all-start.1) | async-done | bytes 1179680 | tf_op jit(solution)/shard_map/all_to_all | solution.py:233
  101.1 0.5 copy.78
  101.5 0.5 copy-done.6
  102.1 0.8 fusion.4
  102.9 0.2 copy-done.1
  103.2 0.2 copy-done.2
  103.3 1.1 convert_bitcast_fusion
  104.5 0.3 fusion.20
  104.8 0.2 fusion
  105.0 2.3 copy.85
  107.3 7.6 %all-to-all-start.2 = ((bf16[2,4,192,384]{3,0,1,2:T(2,128)(2,1)}), bf16[2,4,192,384]{3,0,1,2:T(2,128)(2,1)S(1)}, u32[]{:S(2)}, u32[]{:S(2)}) async-start(bf16[2,4,192,384]{3,0,1,2:T(2,128)(2,1)} %copy.85), calls=%async_computation.2 | async-start | bytes 2359296 | tf_op jit(solution)/shard_map/all_to_all | solution.py:247
  114.9 0.9 and_convert_fusion.1.refs_0_
  115.8 26.8 %all-to-all-done.2 = bf16[2,4,192,384]{3,0,1,2:T(2,128)(2,1)S(1)} async-done(((bf16[2,4,192,384]{3,0,1,2:T(2,128)(2,1)}), bf16[2,4,192,384]{3,0,1,2:T(2,128)(2,1)S(1)}, u32[]{:S(2)}, u32[]{:S(2)}) %all-to-all-start.2) | async-done | bytes 1179680 | tf_op jit(solution)/shard_map/all_to_all | solution.py:247
  142.7 1.0 convert_reduce_fusion
  143.8 4.6 %collective-permute-start = (bf16[2,4,3,384]{3,2,0,1:T(4,128)(2,1)S(1)}, bf16[2,4,3,384]{3,2,0,1:T(4,128)(2,1)S(1)}, u32[]{:S(2)}, u32[]{:S(2)}) collective-permute-start(bf16[2,4,3,384]{3,2,0,1:T(4,128)(2,1)S(1)} %get-tuple-element.23), channel_id=1, source_target_pairs={{0,32},{32,64},{64,96},{96,128},{128,160},{160,192},{192,224},{1,3... | collective-permute-start | bytes 55304 | tf_op jit(solution)/shard_map/ppermute | solution.py:16
  148.5 1.9 collective-permute-start.1
  150.4 5.3 %collective-permute-done.1 = bf16[2,4,3,384]{3,2,0,1:T(4,128)(2,1)S(1)} collective-permute-done((bf16[2,4,3,384]{3,2,0,1:T(4,128)(2,1)S(1)}, bf16[2,4,3,384]{3,2,0,1:T(4,128)(2,1)S(1)}, u32[]{:S(2)}, u32[]{:S(2)}) %collective-permute-start.1) | collective-permute-done | bytes 18464 | tf_op jit(solution)/shard_map/ppermute | solution.py:19
  155.8 2.2 collective-permute-start.2
  158.0 3.1 %collective-permute-start.3 = (bf16[2,3,30,384]{3,2,0,1:T(8,128)(2,1)S(1)}, bf16[2,3,30,384]{3,2,0,1:T(8,128)(2,1)S(1)}, u32[]{:S(2)}, u32[]{:S(2)}) collective-permute-start(bf16[2,3,30,384]{3,2,0,1:T(8,128)(2,1)S(1)} %get-tuple-element.18), channel_id=1, source_target_pairs={{1,0},{2,1},{3,2},{4,3},{5,4},{6,5},{7,6},{8,7},{9,8},{10,9},{11,1... | collective-permute-start | bytes 414728 | tf_op jit(solution)/shard_map/ppermute | solution.py:19
  161.2 0.1 copy.88
  161.4 0.2 copy.89
  161.5 0.8 reshape.560.w_ref
  162.3 0.7 pad.18.w_ref
  163.1 0.6 pad_bitcast_fusion.w_ref
  163.7 4.0 %collective-permute-done.3 = bf16[2,3,30,384]{3,2,0,1:T(8,128)(2,1)S(1)} collective-permute-done((bf16[2,3,30,384]{3,2,0,1:T(8,128)(2,1)S(1)}, bf16[2,3,30,384]{3,2,0,1:T(8,128)(2,1)S(1)}, u32[]{:S(2)}, u32[]{:S(2)}) %collective-permute-start.3) | collective-permute-done | bytes 138272 | tf_op jit(solution)/shard_map/ppermute | solution.py:19
  167.7 0.1 maximum_bitcast_fusion.6
  167.8 0.2 reshape.558
  168.0 1.4 compare_select_fusion.1
  169.4 3.6 %maximum_maximum_fusion.s0.s1.s2 = bf16[10,16,11520]{2,1,0:T(8,128)(2,1)} fusion(bf16[10,2,11520]{2,1,0:T(2,128)(2,1)S(1)} %get-tuple-element.14, bf16[10,2,11520]{2,1,0:T(2,128)(2,1)S(1)} %reshape.558, bf16[10,2,11520]{2,1,0:T(2,128)(2,1)S(1)} %get-tuple-element.13, bf16[16]{0:T(256)(128)(2,1)S(1)} %pad.23.clone), kind=kLoop, calls=%fused_computation | loop fusion | flops 14745600 | bytes 5068832 | tf_op jit(solution)/shard_map/concatenate | solution.py:114
  173.1 17.9 %shard_map.82.s0.s1.s2 = bf16[8,96,10752]{2,1,0:T(8,128)(2,1)} custom-call(bf16[10,16,11520]{2,1,0:T(8,128)(2,1)} %maximum_maximum_fusion.s0.s1.s2, bf16[10,16,11520]{2,1,0:T(8,128)(2,1)} %maximum_maximum_fusion.s0.s1.s2, bf16[10,16,11520]{2,1,0:T(8,128)(2,1)} %maximum_maximum_fusion.s0.s1.s2, bf16[3,3,32,16]{3,2,1,0:T(8,128)(2,1)} %pad.18.w_ref, ...), custom_call_target="tpu_custom_call" | custom-call | tf_op jit(solution)/shard_map/pallas_call | solution.py:93
  190.9 21.6 %shard_map.83.s0.s1.s2 = bf16[6,32,9984]{2,1,0:T(8,128)(2,1)} custom-call(bf16[8,96,10752]{2,1,0:T(8,128)(2,1)} %shard_map.82.s0.s1.s2, bf16[8,96,10752]{2,1,0:T(8,128)(2,1)} %shard_map.82.s0.s1.s2, bf16[8,96,10752]{2,1,0:T(8,128)(2,1)} %shard_map.82.s0.s1.s2, bf16[3,3,32,96]{3,2,1,0:T(8,128)(2,1)} %reshape.560.w_ref, f32[6,1,9984]{2,1,0:T(1,128)} %and_convert_fusion.1.refs_0_), custom_call_target="tpu_custom_call" | custom-call | tf_op jit(solution)/shard_map/pallas_call | solution.py:93
  212.6 8.8 %shard_map.84 = f32[4,2,9216]{2,1,0:T(2,128)} custom-call(bf16[6,32,9984]{2,1,0:T(8,128)(2,1)} %shard_map.83.s0.s1.s2, bf16[6,32,9984]{2,1,0:T(8,128)(2,1)} %shard_map.83.s0.s1.s2, bf16[6,32,9984]{2,1,0:T(8,128)(2,1)} %shard_map.83.s0.s1.s2, bf16[3,3,24,32]{3,2,1,0:T(8,128)(2,1)} %pad_bitcast_fusion.w_ref), custom_call_target="tpu_custom_call" | custom-call | tf_op jit(solution)/shard_map/pallas_call | solution.py:170
  221.4 1.2 reshape.562
  222.6 0.7 copy.90
  (45 shorter events, 0.6 us)
Async XLA Ops:
  6.5 33.0 %all-gather.2.cloned.1.call-start = ((), (), s32[]{:S(2)}) async-start(), calls=%async_computation.3 | async-start | bytes 1327104 | tf_op jit(solution)/shard_map/all_gather | solution.py:217
  41.4 1.2 copy-start.8
  41.4 1.2 copy-start.9
  45.3 8.3 %copy-start.13 = (s32[128,6]{0,1:T(8,128)S(1)}, s32[128,6]{0,1:T(8,128)}, u32[]{:S(2)}) copy-start(s32[128,6]{0,1:T(8,128)} %param.11) | copy-start | bytes 9220
  45.3 24.2 %all-to-all-start = ((bf16[2,1,4,192,384]{4,2,0,1,3:T(4,128)(2,1)}), bf16[2,1,4,192,384]{4,2,0,1,3:T(4,128)(2,1)S(1)}, u32[]{:S(2)}, u32[]{:S(2)}) async-start(bf16[2,1,4,192,384]{4,2,0,1,3:T(4,128)(2,1)} %copy.72), calls=%async_computation | async-start | bytes 2359296 | tf_op jit(solution)/shard_map/all_to_all | solution.py:226
  73.9 1.9 copy-start.3
  73.9 1.9 copy-start.4
  78.6 6.8 %copy-start.15 = (pred[8]{0:T(512)(128)(4,1)S(1)}, pred[8]{0:T(512)(128)(4,1)}, u32[]{:S(2)}) copy-start(pred[8]{0:T(512)(128)(4,1)} %compare_and_fusion.3) | copy-start | bytes 28
  78.6 22.5 %all-to-all-start.1 = ((bf16[2,1,128,6,384]{4,0,3,1,2:T(2,128)(2,1)}), bf16[2,1,128,6,384]{4,0,3,1,2:T(2,128)(2,1)S(1)}, u32[]{:S(2)}, u32[]{:S(2)}) async-start(bf16[2,1,128,6,384]{4,0,3,1,2:T(2,128)(2,1)} %copy.77), calls=%async_computation.1 | async-start | bytes 2359296 | tf_op jit(solution)/shard_map/all_to_all | solution.py:233
  101.1 0.9 copy-start.6
  101.1 1.0 copy-start.7
  102.1 1.1 copy-start.1
  102.1 1.2 copy-start.2
  107.3 7.6 %copy-start.10 = (pred[9984]{0:T(1024)(128)(4,1)S(1)}, pred[9984]{0:T(1024)(128)(4,1)}, u32[]{:S(2)}) copy-start(pred[9984]{0:T(1024)(128)(4,1)} %compare_and_fusion.1) | copy-start | bytes 29956
  107.3 7.6 %copy-start.14 = (pred[6]{0:T(512)(128)(4,1)S(1)}, pred[6]{0:T(512)(128)(4,1)}, u32[]{:S(2)}) copy-start(pred[6]{0:T(512)(128)(4,1)} %compare_and_fusion.2) | copy-start | bytes 22
  107.3 35.4 %all-to-all-start.2 = ((bf16[2,4,192,384]{3,0,1,2:T(2,128)(2,1)}), bf16[2,4,192,384]{3,0,1,2:T(2,128)(2,1)S(1)}, u32[]{:S(2)}, u32[]{:S(2)}) async-start(bf16[2,4,192,384]{3,0,1,2:T(2,128)(2,1)} %copy.85), calls=%async_computation.2 | async-start | bytes 2359296 | tf_op jit(solution)/shard_map/all_to_all | solution.py:247
  114.9 28.8 %copy-start = (f32[2,4,24,384]{3,2,1,0:T(8,128)S(1)}, f32[2,4,24,384]{3,2,1,0:T(8,128)}, u32[]{:S(2)}) copy-start(f32[2,4,24,384]{3,2,1,0:T(8,128)} %param.8) | copy-start | bytes 884740
  143.7 17.5 %copy-start.11 = (bf16[3,3,32,3,2]{2,4,3,1,0:T(2,128)(2,1)S(1)}, bf16[3,3,32,3,2]{2,4,3,1,0:T(2,128)(2,1)}, u32[]{:S(2)}) copy-start(bf16[3,3,32,3,2]{2,4,3,1,0:T(2,128)(2,1)} %param.13) | copy-start | bytes 10372
  143.7 17.7 %copy-start.5 = (bf16[3,3,32,3,32]{4,2,3,1,0:T(8,128)(2,1)S(1)}, bf16[3,3,32,3,32]{4,2,3,1,0:T(8,128)(2,1)}, u32[]{:S(2)}) copy-start(bf16[3,3,32,3,32]{4,2,3,1,0:T(8,128)(2,1)} %param.14) | copy-start | bytes 165892
  143.8 19.3 %copy-start.12 = (bf16[3,3,2,3,32]{4,2,3,1,0:T(2,128)(2,1)S(1)}, bf16[3,3,2,3,32]{4,2,3,1,0:T(2,128)(2,1)}, u32[]{:S(2)}) copy-start(bf16[3,3,2,3,32]{4,2,3,1,0:T(2,128)(2,1)} %param.15) | copy-start | bytes 10372
  143.8 6.6 %collective-permute-start = (bf16[2,4,3,384]{3,2,0,1:T(4,128)(2,1)S(1)}, bf16[2,4,3,384]{3,2,0,1:T(4,128)(2,1)S(1)}, u32[]{:S(2)}, u32[]{:S(2)}) collective-permute-start(bf16[2,4,3,384]{3,2,0,1:T(4,128)(2,1)S(1)} %get-tuple-element.23), channel_id=1, source_target_pairs={{0,32},{32,64},{64,96},{96,128},{128,160},{160,192},{192,224},{1,3... | collective-permute-start | bytes 55304 | tf_op jit(solution)/shard_map/ppermute | solution.py:16
  148.5 7.3 %collective-permute-start.1 = (bf16[2,4,3,384]{3,2,0,1:T(4,128)(2,1)S(1)}, bf16[2,4,3,384]{3,2,0,1:T(4,128)(2,1)S(1)}, u32[]{:S(2)}, u32[]{:S(2)}) collective-permute-start(bf16[2,4,3,384]{3,2,0,1:T(4,128)(2,1)S(1)} %get-tuple-element.24), channel_id=1, source_target_pairs={{32,0},{64,32},{96,64},{128,96},{160,128},{192,160},{224,192},{33,... | collective-permute-start | bytes 55304 | tf_op jit(solution)/shard_map/ppermute | solution.py:19
  155.8 7.9 %collective-permute-start.2 = (bf16[2,3,30,384]{3,2,0,1:T(8,128)(2,1)S(1)}, bf16[2,3,30,384]{3,2,0,1:T(8,128)(2,1)S(1)}, u32[]{:S(2)}, u32[]{:S(2)}) collective-permute-start(bf16[2,3,30,384]{3,2,0,1:T(8,128)(2,1)S(1)} %get-tuple-element.17), channel_id=1, source_target_pairs={{0,1},{1,2},{2,3},{3,4},{4,5},{5,6},{6,7},{7,8},{8,9},{9,10},{10,1... | collective-permute-start | bytes 414728 | tf_op jit(solution)/shard_map/ppermute | solution.py:16
  158.0 9.7 %collective-permute-start.3 = (bf16[2,3,30,384]{3,2,0,1:T(8,128)(2,1)S(1)}, bf16[2,3,30,384]{3,2,0,1:T(8,128)(2,1)S(1)}, u32[]{:S(2)}, u32[]{:S(2)}) collective-permute-start(bf16[2,3,30,384]{3,2,0,1:T(8,128)(2,1)S(1)} %get-tuple-element.18), channel_id=1, source_target_pairs={{1,0},{2,1},{3,2},{4,3},{5,4},{6,5},{7,6},{8,7},{9,8},{10,9},{11,1... | collective-permute-start | bytes 414728 | tf_op jit(solution)/shard_map/ppermute | solution.py:19
Sparse Core Ops, SparseCore 0:
  9.2 30.2 all-gather.1
